TPU v7x, 32 devices: a whole 2x2x4 slice. The times are simulated.
32 devices in a mesh: dp: 4 (over y, x), fsdp: 8 (over z, core).
Axes of the slice: x: 2, y: 2, z: 4, core: 2. Of those that a mesh axis runs over, the one named last changes fastest.
Arguments:
- frames: bfloat16 [256, 1024, 512], P(('dp', 'fsdp')), may hold values from -6 to 6
- counts: int32 [256], P(('dp', 'fsdp')), may hold values from 64 to 1024, as said below
- cotangent: bfloat16 [256, 1024, 512], P(('dp', 'fsdp')), may hold values from -6 to 6
- master: float32 [1581056], P(('dp', 'fsdp'))
- momentum: float32 [1581056], P(('dp', 'fsdp')), may hold values from -48 to 48
- average: float32 [1581056], P(('dp', 'fsdp')), may hold values from -0.75 to 0.75
- disc_grads: float32 [1048576], P(('dp', 'fsdp'))
Outputs:
- block_out: bfloat16 [256, 1024, 512], P(('dp', 'fsdp'))
- input_grad: float32 [256, 1024, 512], P(('dp', 'fsdp'))
- grad_norm: float32 [], replicated
- new_master: float32 [1581056], P(('dp', 'fsdp'))
- new_momentum: float32 [1581056], P(('dp', 'fsdp'))
- new_average: float32 [1581056], P(('dp', 'fsdp'))
- master_copy: bfloat16 [1581056], P(('dp', 'fsdp'))
- average_copy: bfloat16 [1581056], P(('dp', 'fsdp'))
Inputs may be any that keep to these rules, and one draw needn't show every extreme that they name: `counts`: clip 0 has 1024 true frames and clip 1 has 64.
All inputs are finite; a program needn't handle non-finite values.
Results may differ from a plain program's by a relative error of at most 0.0014.
The roundings to bfloat16 on the way count: a program that leaves them out, or rounds other values in their place, can miss the bound.
Values may be sent and summed in bfloat16 or wider, within the bound.
No kernel may reach another device: no remote copies, remote signals or barrier semaphores. Data moves between devices by JAX's collectives and lax.ppermute only.
A program may use at most 320 MiB of HBM per device.

v0:
```python
import jax
import jax.numpy as jnp
from jax import lax
from jax.sharding import PartitionSpec as P

D = 512
FF = 1536
KERNEL = 7


def unpack(packed):
    shapes = [(D, FF), (FF, D), (KERNEL, D), (D,), (D,), (D,), (D,), (D,), (FF,)]
    pieces = []
    start_at = 0
    for shape in shapes:
        entries = 1
        for extent in shape:
            entries = entries * extent
        pieces.append(packed[start_at : start_at + entries].reshape(shape))
        start_at = start_at + entries
    return (tuple(pieces), start_at)


def conv_norm(masked, conv_w, conv_b, ln_g, ln_b):
    length = masked.shape[1]
    padded = jnp.pad(masked, ((0, 0), (KERNEL // 2, KERNEL // 2), (0, 0)))
    summed = conv_b + conv_w[0] * padded[:, 0:length, :]
    for offset in range(1, KERNEL):
        summed = summed + conv_w[offset] * padded[:, offset : offset + length, :]
    centre = jnp.mean(summed, axis=-1, keepdims=True)
    shifted = summed - centre
    spread = jnp.mean(shifted * shifted, axis=-1, keepdims=True)
    return shifted * lax.rsqrt(spread + 1e-06) * ln_g + ln_b


def exact_gelu(values):
    return jax.nn.gelu(values, approximate=False)


def contract_rows(left, right):
    return lax.dot_general(
        left, right, (((0,), (0,)), ((), ())), preferred_element_type=jnp.float32
    )


def contract_cols(left, right):
    return lax.dot_general(
        left, right, (((1,), (1,)), ((), ())), preferred_element_type=jnp.float32
    )


def body(frames, counts, cotangent, master, momentum, average, disc_grads):
    devices = lax.axis_size(("dp", "fsdp"))
    clips, length, width = frames.shape
    rows = clips * length
    flat_size = master.shape[0] * devices
    total_frames = jnp.float32(rows * devices)
    rounded = master.astype(jnp.bfloat16)
    packed = lax.all_gather(rounded, ("dp", "fsdp"), axis=0, tiled=True)
    (w_one, w_two, conv_w, conv_b, ln_g, ln_b, b_two, gamma, b_one), used = unpack(packed)
    slots = lax.broadcasted_iota(jnp.int32, (clips, length), 1)
    mask = (slots < counts[:, None]).astype(jnp.float32)[:, :, None]
    floats = frames.astype(jnp.float32)
    masked = floats * mask
    normed = conv_norm(
        masked,
        conv_w.astype(jnp.float32),
        conv_b.astype(jnp.float32),
        ln_g.astype(jnp.float32),
        ln_b.astype(jnp.float32),
    )
    act = normed.reshape(rows, width).astype(jnp.bfloat16)
    hidden = jnp.dot(act, w_one, preferred_element_type=jnp.float32) + b_one.astype(jnp.float32)
    gelled, gelu_pull = jax.vjp(exact_gelu, hidden)
    gelled_low = gelled.astype(jnp.bfloat16)
    branch = jnp.dot(gelled_low, w_two, preferred_element_type=jnp.float32) + b_two.astype(
        jnp.float32
    )
    mask_rows = mask.reshape(rows, 1)
    block_out = (
        mask_rows * (floats.reshape(rows, width) + gamma.astype(jnp.float32) * branch)
    ).astype(jnp.bfloat16)
    packed_back = lax.all_gather(rounded, ("dp", "fsdp"), axis=0, tiled=True)
    (w_one_b, w_two_b, conv_w_b, conv_b_b, ln_g_b, ln_b_b, b_two_b, gamma_b, b_one_b), used = (
        unpack(packed_back)
    )
    d_out = cotangent.astype(jnp.float32).reshape(rows, width) * mask_rows
    g_gamma = jnp.sum(d_out * branch, axis=0)
    d_branch = (d_out * gamma_b.astype(jnp.float32)).astype(jnp.bfloat16)
    g_b_two = jnp.sum(d_branch.astype(jnp.float32), axis=0)
    g_w_two = contract_rows(gelled_low, d_branch)
    d_gelled = contract_cols(d_branch, w_two_b)
    d_hidden = gelu_pull(d_gelled)[0].astype(jnp.bfloat16)
    g_b_one = jnp.sum(d_hidden.astype(jnp.float32), axis=0)
    g_w_one = contract_rows(act, d_hidden)
    d_act = contract_cols(d_hidden, w_one_b)
    _, norm_pull = jax.vjp(
        conv_norm,
        masked,
        conv_w_b.astype(jnp.float32),
        conv_b_b.astype(jnp.float32),
        ln_g_b.astype(jnp.float32),
        ln_b_b.astype(jnp.float32),
    )
    d_masked, g_conv_w, g_conv_b, g_ln_g, g_ln_b = norm_pull(d_act.reshape(clips, length, width))
    input_grad = d_out.reshape(clips, length, width) + mask * d_masked
    grad_full = jnp.concatenate(
        [
            g_w_one.reshape(-1),
            g_w_two.reshape(-1),
            g_conv_w.reshape(-1),
            g_conv_b,
            g_ln_g,
            g_ln_b,
            g_b_two,
            g_gamma,
            g_b_one,
            jnp.zeros((flat_size - used,), jnp.float32),
        ]
    )
    grad_shard = lax.psum_scatter(grad_full, ("dp", "fsdp"), scatter_dimension=0, tiled=True)
    own_sum, disc_sum = lax.psum(
        (jnp.sum(grad_shard * grad_shard), jnp.sum(disc_grads * disc_grads)), ("dp", "fsdp")
    )
    grad_norm = jnp.sqrt(own_sum + disc_sum)
    clipped = grad_shard * jnp.minimum(1.0, 20.0 * jnp.sqrt(total_frames) / (grad_norm + 1e-06))
    new_momentum = 0.9 * momentum + clipped
    new_master = master - (clipped + 0.9 * new_momentum) / jnp.sqrt(total_frames)
    new_average = 0.99 * average + 0.01 * new_master
    return (
        block_out.reshape(clips, length, width),
        input_grad,
        grad_norm,
        new_master,
        new_momentum,
        new_average,
        new_master.astype(jnp.bfloat16),
        new_average.astype(jnp.bfloat16),
    )


def solution(mesh):
    placed = (
        P(("dp", "fsdp"), None, None),
        P(("dp", "fsdp")),
        P(("dp", "fsdp"), None, None),
        P(("dp", "fsdp")),
        P(("dp", "fsdp")),
        P(("dp", "fsdp")),
        P(("dp", "fsdp")),
    )
    return jax.shard_map(
        body,
        mesh=mesh,
        in_specs=placed,
        out_specs=(
            P(("dp", "fsdp"), None, None),
            P(("dp", "fsdp"), None, None),
            P(),
            P(("dp", "fsdp")),
            P(("dp", "fsdp")),
            P(("dp", "fsdp")),
            P(("dp", "fsdp")),
            P(("dp", "fsdp")),
        ),
        check_vma=False,
    )
```

profile of v0, /device:TPU:0, one launch (start us, length us, event | category | flops | bytes accessed | tf_op | source)
XLA Modules:
  0.0 839.2 jit_solution(11517457408929615365)
XLA Ops:
  10.4 9.7 %broadcast_multiply_fusion.6 = f32[8,1024,512]{2,1,0:T(8,128)} fusion(f32[8,1024]{1,0:T(8,128)S(1)} %get-tuple-element.55, bf16[8,1024,512]{2,1,0:T(8,128)(2,1)} %param.7), kind=kLoop, calls=%fused_computation.60 | loop fusion | flops 8388608 | bytes 25198592 | tf_op jit(solution)/shard_map/mul | solution.py:64
  20.1 63.4 %all-gather.3.cloned.1.call-done = bf16[32,1,49408]{2,1,0:T(2,128)(2,1)} async-done(((bf16[1,1,49408]{2,1,0:T(2,128)(2,1)}), bf16[32,1,49408]{2,1,0:T(2,128)(2,1)}) %all-gather.3.cloned.1.call-update) | async-done | bytes 3162128 | tf_op jit(solution)/shard_map/all_gather | solution.py:59
  83.5 58.8 %reduce.1 = bf16[32,49408]{1,0:T(8,128)(2,1)} reduce(bf16[32,1,49408]{2,1,0:T(2,128)(2,1)} %all-gather.3.cloned.1.call-done, bf16[]{:T(256)} %constant.126), dimensions={1}, to_apply=%all-gather.reduce_sub_computation | reduce | bytes 6324226 | tf_op jit(solution)/shard_map/all_gather | solution.py:59
  142.3 6.0 reshape.212
  150.0 2.1 fusion.18
  152.1 2.7 reshape.213
  154.8 2.6 reshape.204
  157.5 2.3 slice.134
  159.8 40.9 %fusion.17 = (f32[8,1024]{1,0:T(8,128)S(1)}, f32[8,1024,512]{2,1,0:T(8,128)S(1)}) fusion(f32[512]{0:T(512)S(1)} %get-tuple-element.48, f32[512]{0:T(512)S(1)} %get-tuple-element.49, f32[512]{0:T(512)S(1)} %get-tuple-element.50, f32[8,1024,512]{2,1,0:T(8,128)} %broadcast_multiply_fusion.6, f32[512]{0:T(512)S(1)} %get-tuple-element.51, ...), kind=kLoop, calls=%fused_computation.98 | loop fusion | flops 62906368 | bytes 33603584 | tf_op jit(solution)/shard_map/reduce_sum | solution.py:30
  200.7 3.2 multiply_reduce_fusion.10
  204.0 3.1 add_convert_fusion.1
  207.2 121.0 %multiply_convert_fusion = (bf16[8192,1536]{1,0:T(8,128)(2,1)}, f32[8192,1536]{1,0:T(8,128)}, f32[8192,1536]{1,0:T(8,128)}) fusion(f32[1536]{0:T(1024)S(1)} %slice_convert_fusion.1, bf16[8192,512]{1,0:T(8,128)(2,1)S(1)} %bitcast.43, bf16[512,1536]{1,0:T(8,128)(2,1)S(1)} %copy-done.8), kind=kOutput, calls=%fused_computation.4 | convolution fusion | flops 13715374080 | bytes 135796736 | tf_op jit(solution)/shard_map/dot_general | solution.py:73
  328.3 24.6 %multiply_reduce_fusion = (f32[512]{0:T(512)}, bf16[8192,512]{1,0:T(8,128)(2,1)}, bf16[8192,512]{1,0:T(8,128)(2,1)}) fusion(bf16[8,1024,512]{2,1,0:T(8,128)(2,1)S(1)} %copy-done.1, f32[512]{0:T(512)S(1)} %copy-done.41, f32[8192]{0:T(1024)S(1)} %bitcast.45, f32[512]{0:T(512)S(1)} %copy-done.39, bf16[8,1024,512]{2,1,0:T(8,128)(2,1)S(1)} %copy-done.2, ...), kind=kOutput, calls=%fused_computation.31 | convolution fusion | flops 12935233536 | bytes 60332032 | tf_op jit(solution)/shard_map/dot_general | solution.py:76
  352.9 20.4 %convolution_bitcast_fusion = f32[192,4,8,128]{3,2,1,0:T(8,128)} fusion(bf16[8192,1536]{1,0:T(8,128)(2,1)} %get-tuple-element.26, bf16[8192,512]{1,0:T(8,128)(2,1)} %get-tuple-element.39), kind=kOutput, calls=%fused_computation.63 | convolution fusion | flops 12884901888 | bytes 36700160 | tf_op jit(solution)/shard_map/dot_general | solution.py:41
  373.3 46.6 %convert_reduce_fusion = (f32[1536]{0:T(1024)S(1)}, bf16[8192,1536]{1,0:T(8,128)(2,1)}) fusion(f32[8192,1536]{1,0:T(8,128)} %get-tuple-element.27, bf16[8192,512]{1,0:T(8,128)(2,1)} %get-tuple-element.39, bf16[1536,512]{1,0:T(8,128)(2,1)S(1)} %copy-done.7, f32[8192,1536]{1,0:T(8,128)} %get-tuple-element.56, f32[1536]{0:T(1024)S(1)} %slice_convert_fusion.1), kind=kOutput, calls=%fused_computation.2 | convolution fusion | flops 13098809344 | bytes 135802880 | tf_op jit(solution)/shard_map/dot_general | solution.py:47
  420.0 19.4 %fusion.20 = f32[512,1536]{1,0:T(8,128)S(1)} fusion(bf16[8192,512]{1,0:T(8,128)(2,1)} %bitcast.44, bf16[8192,1536]{1,0:T(8,128)(2,1)} %get-tuple-element.59), kind=kOutput, calls=%fused_computation.101 | convolution fusion | flops 12884901888 | bytes 36700160 | tf_op jit(solution)/shard_map/dot_general | solution.py:41
  439.4 1.9 reshape.207
  441.3 23.5 %multiply_reduce_fusion.1 = (f32[512]{0:T(512)S(1)}, f32[8,1024]{1,0:T(8,128)S(1)}, f32[512]{0:T(512)S(1)}, f32[8,1024,512]{2,1,0:T(8,128)S(1)}) fusion(f32[8,1024,512]{2,1,0:T(8,128)} %copy-done, f32[8,1024]{1,0:T(8,128)S(1)} %copy-done.16, f32[8,1024]{1,0:T(8,128)S(1)} %copy-done.12, f32[512]{0:T(512)S(1)} %copy-done.38, ...), kind=kOutput, calls=%fused_computation.34 | convolution fusion | flops 12918448128 | bytes 60397568 | tf_op jit(solution)/shard_map/dot_general | solution.py:47
  464.9 17.0 %fusion.15 = (f32[8,1024]{1,0:T(8,128)S(1)}, f32[8,1024,512]{2,1,0:T(8,128)}) fusion(f32[8,1024]{1,0:T(8,128)S(1)} %multiply_multiply_fusion.5, f32[8,1024,512]{2,1,0:T(8,128)} %copy-done, f32[8,1024]{1,0:T(8,128)S(1)} %copy-done.12, f32[8,1024]{1,0:T(8,128)S(1)} %copy-done.16, f32[8,1024,512]{2,1,0:T(8,128)S(1)} %get-tuple-element.57, f32[512]{0:T(512)S(1)} %copy-done.38), kind=kLoop, calls=%fused_computation.97 | loop fusion | flops 29351936 | bytes 50464768 | tf_op jit(solution)/shard_map/transpose(jvp())/reduce_sum | solution.py:31
  484.7 84.4 %multiply_reduce_fusion.8 = (f32[512]{0:T(512)S(1)}, f32[512]{0:T(512)S(1)}, f32[512]{0:T(512)S(1)}, f32[512]{0:T(512)S(1)}, f32[512]{0:T(512)S(1)}, /*index=5*/...) fusion(f32[8,1024,512]{2,1,0:T(8,128)} %broadcast_multiply_fusi, ...), kind=kLoop, calls=%fused_computation.41 | loop fusion | flops 130018816 | bytes 167872512 | tf_op jit(solution)/shard_map/transpose(jvp())/reduce_sum | solution.py:29
  582.0 155.3 %all-reduce.18.cloned.1.call-done = f32[1581056]{0:T(1024)} async-done(((f32[1581056]{0:T(1024)}), f32[1581056]{0:T(1024)}) %all-reduce.18.cloned.1.call-update) | async-done | bytes 6324240
  740.4 47.2 %fusion.7 = f32[8,1024,512]{2,1,0:T(8,128)} fusion(f32[8,1024,512]{2,1,0:T(8,128)} %get-tuple-element.36, f32[8,1024,512]{2,1,0:T(8,128)} %get-tuple-element.35, f32[8,1024,512]{2,1,0:T(8,128)} %get-tuple-element.34, f32[8,1024,512]{2,1,0:T(8,128)} %get-tuple-element.38, f32[8,1024,512]{2,1,0:T(8,128)} %get-tuple-element.32, ...), kind=kLoop, calls=%fused_computation.21 | loop fusion | flops 41943040 | bytes 142639104 | tf_op jit(solution)/shard_map/add | solution.py:106
  787.5 39.9 %psum.16 = f32[]{:T(128)} all-reduce(f32[]{:T(128)S(6)} %add.145), channel_id=1, replica_groups=mesh['dp'=4,'fsdp'=8] {'dp','fsdp'}, use_global_device_ids=true, to_apply=%region_19.20 | all-reduce | flops 1 | bytes 8 | tf_op jit(solution)/shard_map/psum | solution.py:122
  828.2 1.9 fusion.14
  (118 shorter events, 23.0 us)
Async XLA Ops:
  7.2 76.4 %all-gather.3.cloned.1.call-start = ((), (), s32[]{:S(2)}) async-start(), calls=%async_computation | async-start | bytes 6521856 | tf_op jit(solution)/shard_map/all_gather | solution.py:59
  9.0 728.4 %all-reduce.18.cloned.1.call-start = ((), (), s32[]{:S(2)}) async-start(), calls=%async_computation.1 | async-start | bytes 12648448
  150.0 54.0 %copy-start.37 = (f32[512]{0:T(512)}, f32[512]{0:T(512)S(1)}, u32[]{:S(2)}) copy-start(f32[512]{0:T(512)S(1)} %get-tuple-element.43) | copy-start | bytes 6148
  157.4 43.2 %copy-start.23 = (f32[512]{0:T(512)}, f32[512]{0:T(512)S(1)}, u32[]{:S(2)}) copy-start(f32[512]{0:T(512)S(1)} %get-tuple-element.47) | copy-start | bytes 6148
  157.4 43.2 %copy-start.25 = (f32[512]{0:T(512)}, f32[512]{0:T(512)S(1)}, u32[]{:S(2)}) copy-start(f32[512]{0:T(512)S(1)} %get-tuple-element.48) | copy-start | bytes 6148
  157.4 43.2 %copy-start.27 = (f32[512]{0:T(512)}, f32[512]{0:T(512)S(1)}, u32[]{:S(2)}) copy-start(f32[512]{0:T(512)S(1)} %get-tuple-element.49) | copy-start | bytes 6148
  157.4 43.2 %copy-start.29 = (f32[512]{0:T(512)}, f32[512]{0:T(512)S(1)}, u32[]{:S(2)}) copy-start(f32[512]{0:T(512)S(1)} %get-tuple-element.50) | copy-start | bytes 6148
  157.4 43.2 %copy-start.31 = (f32[512]{0:T(512)}, f32[512]{0:T(512)S(1)}, u32[]{:S(2)}) copy-start(f32[512]{0:T(512)S(1)} %get-tuple-element.51) | copy-start | bytes 6148
  157.4 43.2 %copy-start.33 = (f32[512]{0:T(512)}, f32[512]{0:T(512)S(1)}, u32[]{:S(2)}) copy-start(f32[512]{0:T(512)S(1)} %get-tuple-element.52) | copy-start | bytes 6148
  157.5 43.2 %copy-start.35 = (f32[512]{0:T(512)}, f32[512]{0:T(512)S(1)}, u32[]{:S(2)}) copy-start(f32[512]{0:T(512)S(1)} %get-tuple-element.53) | copy-start | bytes 6148
  203.9 124.3 %copy-start.17 = (f32[8,1024]{1,0:T(8,128)}, f32[8,1024]{1,0:T(8,128)S(1)}, u32[]{:S(2)}) copy-start(f32[8,1024]{1,0:T(8,128)S(1)} %multiply_reduce_fusion.10) | copy-start | bytes 98308
  204.0 124.3 %copy-start.15 = (f32[8,1024]{1,0:T(8,128)}, f32[8,1024]{1,0:T(8,128)S(1)}, u32[]{:S(2)}) copy-start(f32[8,1024]{1,0:T(8,128)S(1)} %fusion.12) | copy-start | bytes 98308
  207.1 121.1 %copy-start.5 = (bf16[8,1024,512]{2,1,0:T(8,128)(2,1)}, bf16[8,1024,512]{2,1,0:T(8,128)(2,1)S(1)}, u32[]{:S(2)}) copy-start(bf16[8,1024,512]{2,1,0:T(8,128)(2,1)S(1)} %add_convert_fusion.1) | copy-start | bytes 25165828
  207.2 121.1 %copy-start.1 = (bf16[8,1024,512]{2,1,0:T(8,128)(2,1)S(1)}, bf16[8,1024,512]{2,1,0:T(8,128)(2,1)}, u32[]{:S(2)}) copy-start(bf16[8,1024,512]{2,1,0:T(8,128)(2,1)} %param.9) | copy-start | bytes 25165828
  207.2 121.1 %copy-start.2 = (bf16[8,1024,512]{2,1,0:T(8,128)(2,1)S(1)}, bf16[8,1024,512]{2,1,0:T(8,128)(2,1)}, u32[]{:S(2)}) copy-start(bf16[8,1024,512]{2,1,0:T(8,128)(2,1)} %param.7) | copy-start | bytes 25165828
  207.2 121.1 %copy-start.22 = (f32[1,8,8,128]{3,1,2,0:T(8,128)S(1)}, f32[1,8,8,128]{3,1,2,0:T(8,128)}, u32[]{:S(2)}) copy-start(f32[1,8,8,128]{3,1,2,0:T(8,128)} %copy.18) | copy-start | bytes 98308
  207.2 121.1 %copy-start.39 = (f32[512]{0:T(512)S(1)}, f32[512]{0:T(512)}, u32[]{:S(2)}) copy-start(f32[512]{0:T(512)} %get-tuple-element.40) | copy-start | bytes 6148
  207.2 121.1 %copy-start.41 = (f32[512]{0:T(512)S(1)}, f32[512]{0:T(512)}, u32[]{:S(2)}) copy-start(f32[512]{0:T(512)} %get-tuple-element.41) | copy-start | bytes 6148
  441.2 23.5 %copy-start.18 = (f32[8,1024]{1,0:T(8,128)S(1)}, f32[8,1024]{1,0:T(8,128)}, u32[]{:S(2)}) copy-start(f32[8,1024]{1,0:T(8,128)} %copy-done.17) | copy-start | bytes 98308
  484.7 92.8 %copy-start.42 = (f32[512]{0:T(512)S(1)}, f32[512]{0:T(512)}, u32[]{:S(2)}) copy-start(f32[512]{0:T(512)} %get-tuple-element.30) | copy-start | bytes 6148
  484.7 96.7 %copy-start.21 = (f32[32768]{0:T(1024)S(1)}, f32[32768]{0:T(1024)}, u32[]{:S(2)}) copy-start(f32[32768]{0:T(1024)} %param.13) | copy-start | bytes 393220
  740.3 87.9 %copy-start.9 = (f32[49408]{0:T(1024)S(1)}, f32[49408]{0:T(1024)}, u32[]{:S(2)}) copy-start(f32[49408]{0:T(1024)} %param.10) | copy-start | bytes 592900
  740.3 87.8 %copy-start.19 = (f32[49408]{0:T(1024)S(1)}, f32[49408]{0:T(1024)}, u32[]{:S(2)}) copy-start(f32[49408]{0:T(1024)} %param.12) | copy-start | bytes 592900
  740.3 87.8 %copy-start.20 = (f32[49408]{0:T(1024)S(1)}, f32[49408]{0:T(1024)}, u32[]{:S(2)}) copy-start(f32[49408]{0:T(1024)} %param.11) | copy-start | bytes 592900
  (21 other events, 316.0 us)
Sparse Core Ops, SparseCore 0:
  11.4 72.1 all-gather.2
  581.5 155.8 all-reduce.17
where the time goes:
time: 849 us; the launch traced here: 839 us
  other arithmetic  271 us (32%)
  matrix products  256 us (30%)
  waiting for transfers between devices  219 us (26%)
  blocking collectives  39.9 us (5%)
  local copies, waits for them, and re-layouts  35 us (4%)
  between operations  18.3 us (2%)
    unnamed x3, waiting for transfers between devices  155 us
    dot_general x1, matrix products, body(): jnp.dot(act, w_one, preferred_element_type=jnp.float32)  121 us
    reduce_sum x1, other arithmetic, conv_norm(): summed = summed + conv_w[offset] * padded[:, offset:offset + length, :]  84.4 us
    dot_general x2, matrix products, contract_cols(): lax.dot_general(left, right, (((1,), (1,)), ((), ())), preferred_element_...  70.2 us
    all_gather x1, waiting for transfers between devices, body(): packed = lax.all_gather(rounded, ('dp', 'fsdp'), axis=0, tiled=True)  63.4 us
    all_gather x1, other arithmetic, body(): packed = lax.all_gather(rounded, ('dp', 'fsdp'), axis=0, tiled=True)  58.8 us
    add x1, other arithmetic, body(): input_grad = d_out.reshape(clips, length, width) + mask * d_masked  47.2 us
    reduce_sum x1, other arithmetic, conv_norm(): centre = jnp.mean(summed, axis=-1, keepdims=True)  40.9 us
  transfers between devices with their start and end apart: 2, of which 2 were waited for; matrix products, arithmetic and copies ran while one was open for 1% of the time, Pallas kernels for 0%

commit v1 on v0

v1 whole, which is shorter than its diff:
```python
import functools
import math

import jax
import jax.numpy as jnp
from jax import lax
from jax.experimental import pallas as pl
from jax.experimental.pallas import tpu as pltpu
from jax.sharding import PartitionSpec as P

F32 = jnp.float32
BF16 = jnp.bfloat16
TAPS = 7
HALF = TAPS // 2
PAD = 8


def tdot(x, y):
    return lax.dot_general(x, y, (((0,), (0,)), ((), ())), preferred_element_type=F32)


def ntdot(x, y):
    return lax.dot_general(x, y, (((1,), (1,)), ((), ())), preferred_element_type=F32)


def block_kernel(length, width, hidden, rows):
    nblk = length // rows
    inv_w = 1.0 / width
    sqrt_half = math.sqrt(0.5)
    inv_sqrt_2pi = 1.0 / math.sqrt(2.0 * math.pi)

    def kernel(counts_ref, fr_ref, cot_ref, w1_ref, w2_ref, cw_ref, vec_ref, b1_ref,
               bo_ref, ig_ref, gw1_hbm, gw2_hbm, gcw_ref, gvec_ref, gb1_ref,
               xpad, xhat_s, rstd_s, a_s, da_s, dpad, gw1_s, gw2_s, sems):
        clip = pl.program_id(0)
        count = counts_ref[clip]

        @pl.when(clip == 0)
        def _init():
            gw1_s[...] = jnp.zeros_like(gw1_s)
            gw2_s[...] = jnp.zeros_like(gw2_s)
            gcw_ref[...] = jnp.zeros_like(gcw_ref)
            gvec_ref[...] = jnp.zeros_like(gvec_ref)
            gb1_ref[...] = jnp.zeros_like(gb1_ref)
            xpad[0:PAD, :] = jnp.zeros((PAD, width), F32)
            xpad[PAD + length:, :] = jnp.zeros((PAD, width), F32)
            dpad[0:PAD, :] = jnp.zeros((PAD, width), F32)
            dpad[PAD + length:, :] = jnp.zeros((PAD, width), F32)

        cw = cw_ref[...]
        conv_b = vec_ref[0:1, :]
        ln_g = vec_ref[1:2, :]
        ln_b = vec_ref[2:3, :]
        b_two = vec_ref[3:4, :]
        gamma = vec_ref[4:5, :]
        b_one = b1_ref[0:1, :]

        all_rows = lax.broadcasted_iota(jnp.int32, (length, 1), 0)
        xpad[PAD:PAD + length, :] = jnp.where(all_rows < count, fr_ref[0].astype(F32), 0.0)

        for b in range(nblk):
            r0 = b * rows

            @pl.when(r0 < count)
            def _fwd_block():
                base = PAD + r0 - HALF
                conv = conv_b + cw[0:1, :] * xpad[base:base + rows, :]
                for k in range(1, TAPS):
                    conv = conv + cw[k:k + 1, :] * xpad[base + k:base + k + rows, :]
                centre = jnp.sum(conv, axis=-1, keepdims=True) * inv_w
                shifted = conv - centre
                spread = jnp.sum(shifted * shifted, axis=-1, keepdims=True) * inv_w
                rstd = lax.rsqrt(spread + 1e-6)
                xhat = shifted * rstd
                xhat_s[r0:r0 + rows, :] = xhat
                rstd_s[r0:r0 + rows, :] = rstd
                a_s[r0:r0 + rows, :] = (xhat * ln_g + ln_b).astype(BF16)

        bo_ref[...] = jnp.zeros_like(bo_ref)

        def chunk(c, carry):
            g_gamma, g_b2, g_b1 = carry
            r0 = pl.multiple_of(c * rows, rows)
            a = a_s[pl.ds(r0, rows), :]
            h1 = jnp.dot(a, w1_ref[...], preferred_element_type=F32) + b_one
            cdf = 0.5 * (1.0 + lax.erf(h1 * sqrt_half))
            hh = (h1 * cdf).astype(BF16)
            z = jnp.dot(hh, w2_ref[...], preferred_element_type=F32) + b_two
            live = (r0 + lax.broadcasted_iota(jnp.int32, (rows, 1), 0)) < count
            xin = fr_ref[0, pl.ds(r0, rows), :].astype(F32)
            bo_ref[0, pl.ds(r0, rows), :] = jnp.where(live, xin + gamma * z, 0.0).astype(BF16)
            dout = jnp.where(live, cot_ref[0, pl.ds(r0, rows), :].astype(F32), 0.0)
            g_gamma = g_gamma + jnp.sum(dout * z, axis=0, keepdims=True)
            dz = (gamma * dout).astype(BF16)
            g_b2 = g_b2 + jnp.sum(dz.astype(F32), axis=0, keepdims=True)
            gw2_s[...] += tdot(hh, dz)
            dhh = ntdot(dz, w2_ref[...])
            slope = cdf + h1 * (jnp.exp(-0.5 * (h1 * h1)) * inv_sqrt_2pi)
            dh1 = (dhh * slope).astype(BF16)
            g_b1 = g_b1 + jnp.sum(dh1.astype(F32), axis=0, keepdims=True)
            gw1_s[...] += tdot(a, dh1)
            da_s[pl.ds(r0, rows), :] = ntdot(dh1, w1_ref[...])
            return g_gamma, g_b2, g_b1

        nact = (count + rows - 1) // rows
        zero_d = jnp.zeros((1, width), F32)
        g_gamma, g_b2, g_b1 = lax.fori_loop(
            0, nact, chunk, (zero_d, zero_d, jnp.zeros((1, hidden), F32)))

        def dxm_block(b):
            r0 = b * rows
            base = PAD + r0 + HALF
            dxm = cw[0:1, :] * dpad[base:base + rows, :]
            for k in range(1, TAPS):
                dxm = dxm + cw[k:k + 1, :] * dpad[base - k:base - k + rows, :]
            live = (r0 + lax.broadcasted_iota(jnp.int32, (rows, 1), 0)) < count
            cot = cot_ref[0, r0:r0 + rows, :].astype(F32)
            ig_ref[0, r0:r0 + rows, :] = jnp.where(live, cot + dxm, 0.0)

        sums = [zero_d] * (3 + TAPS)
        for b in range(nblk):
            r0 = b * rows

            def _bwd_block(r0=r0):
                live = (r0 + lax.broadcasted_iota(jnp.int32, (rows, 1), 0)) < count
                da = jnp.where(live, da_s[r0:r0 + rows, :], 0.0)
                xhat = xhat_s[r0:r0 + rows, :]
                rstd = rstd_s[r0:r0 + rows, :]
                dn = da * ln_g
                m1 = jnp.sum(dn, axis=-1, keepdims=True) * inv_w
                m2 = jnp.sum(dn * xhat, axis=-1, keepdims=True) * inv_w
                dconv = jnp.where(live, rstd * (dn - m1 - xhat * m2), 0.0)
                dpad[PAD + r0:PAD + r0 + rows, :] = dconv
                part = [jnp.sum(dconv, axis=0, keepdims=True),
                        jnp.sum(da * xhat, axis=0, keepdims=True),
                        jnp.sum(da, axis=0, keepdims=True)]
                base = PAD + r0 - HALF
                for k in range(TAPS):
                    part.append(jnp.sum(dconv * xpad[base + k:base + k + rows, :], axis=0, keepdims=True))
                return part

            active = r0 < count
            part = lax.cond(active, _bwd_block, lambda: [zero_d] * (3 + TAPS))

            @pl.when(jnp.logical_not(active))
            def _idle():
                dpad[PAD + r0:PAD + r0 + rows, :] = jnp.zeros((rows, width), F32)
                ig_ref[0, r0:r0 + rows, :] = jnp.zeros((rows, width), F32)

            sums = [s + p for s, p in zip(sums, part)]
            if b >= 1:
                @pl.when((b - 1) * rows < count)
                def _prev(b=b):
                    dxm_block(b - 1)

        @pl.when((nblk - 1) * rows < count)
        def _last():
            dxm_block(nblk - 1)

        gvec_ref[0:1, :] += sums[0]
        gvec_ref[1:2, :] += sums[1]
        gvec_ref[2:3, :] += sums[2]
        gvec_ref[3:4, :] += g_b2
        gvec_ref[4:5, :] += g_gamma
        for k in range(TAPS):
            gcw_ref[k:k + 1, :] += sums[3 + k]
        gb1_ref[0:1, :] += g_b1

        @pl.when(clip == pl.num_programs(0) - 1)
        def _flush():
            c1 = pltpu.make_async_copy(gw1_s, gw1_hbm, sems.at[0])
            c2 = pltpu.make_async_copy(gw2_s, gw2_hbm, sems.at[1])
            c1.start()
            c2.start()
            c1.wait()
            c2.wait()

    return kernel


def fused_block(frames, counts, cotangent, w1, w2, cw8, vec8, b1_8, rows=256):
    clips, length, width = frames.shape
    hidden = w1.shape[1]
    kernel = block_kernel(length, width, hidden, rows)
    clip_spec = pl.BlockSpec((1, length, width), lambda i, c: (i, 0, 0))
    fixed = lambda shape: pl.BlockSpec(shape, lambda i, c: (0, 0))
    grid_spec = pltpu.PrefetchScalarGridSpec(
        num_scalar_prefetch=1,
        grid=(clips,),
        in_specs=[clip_spec, clip_spec, fixed((width, hidden)), fixed((hidden, width)),
                  fixed((8, width)), fixed((8, width)), fixed((8, hidden))],
        out_specs=[clip_spec, clip_spec,
                   pl.BlockSpec(memory_space=pl.ANY), pl.BlockSpec(memory_space=pl.ANY),
                   fixed((8, width)), fixed((8, width)), fixed((8, hidden))],
        scratch_shapes=[
            pltpu.VMEM((length + 2 * PAD, width), F32),
            pltpu.VMEM((length, width), F32),
            pltpu.VMEM((length, 1), F32),
            pltpu.VMEM((length, width), BF16),
            pltpu.VMEM((length, width), F32),
            pltpu.VMEM((length + 2 * PAD, width), F32),
            pltpu.VMEM((width, hidden), F32),
            pltpu.VMEM((hidden, width), F32),
            pltpu.SemaphoreType.DMA((2,)),
        ],
    )
    flops = 12 * clips * length * width * hidden
    cost = pl.CostEstimate(flops=flops, transcendentals=2 * clips * length * hidden,
                           bytes_accessed=clips * length * width * 8 + 4 * width * hidden * 4)
    return pl.pallas_call(
        kernel,
        grid_spec=grid_spec,
        out_shape=[
            jax.ShapeDtypeStruct((clips, length, width), BF16),
            jax.ShapeDtypeStruct((clips, length, width), F32),
            jax.ShapeDtypeStruct((width, hidden), F32),
            jax.ShapeDtypeStruct((hidden, width), F32),
            jax.ShapeDtypeStruct((8, width), F32),
            jax.ShapeDtypeStruct((8, width), F32),
            jax.ShapeDtypeStruct((8, hidden), F32),
        ],
        compiler_params=pltpu.CompilerParams(
            dimension_semantics=("arbitrary",), vmem_limit_bytes=60 * 1024 * 1024),
        cost_estimate=cost,
    )(counts, frames, cotangent, w1, w2, cw8, vec8, b1_8)


def unpack(packed, width, hidden):
    shapes = [(width, hidden), (hidden, width), (TAPS, width), (width,), (width,), (width,), (width,), (width,), (hidden,)]
    pieces = []
    start_at = 0
    for shape in shapes:
        entries = 1
        for extent in shape:
            entries = entries * extent
        pieces.append(packed[start_at : start_at + entries].reshape(shape))
        start_at = start_at + entries
    return (tuple(pieces), start_at)


def body(frames, counts, cotangent, master, momentum, average, disc_grads):
    devices = lax.axis_size(("dp", "fsdp"))
    clips, length, width = frames.shape
    hidden = 3 * width
    rows = clips * length
    flat_size = master.shape[0] * devices
    total_frames = jnp.float32(rows * devices)
    rounded = master.astype(BF16)
    packed = lax.all_gather(rounded, ("dp", "fsdp"), axis=0, tiled=True)
    (w_one, w_two, conv_w, conv_b, ln_g, ln_b, b_two, gamma, b_one), used = unpack(packed, width, hidden)
    cw8 = jnp.zeros((8, width), F32).at[:TAPS].set(conv_w.astype(F32))
    vec8 = jnp.concatenate(
        [jnp.stack([conv_b, ln_g, ln_b, b_two, gamma]).astype(F32), jnp.zeros((3, width), F32)])
    b1_8 = jnp.zeros((8, hidden), F32).at[0].set(b_one.astype(F32))
    block_out, input_grad, g_w1, g_w2, gcw, gvec, gb1 = fused_block(
        frames, counts, cotangent, w_one, w_two, cw8, vec8, b1_8)
    grad_full = jnp.concatenate(
        [
            g_w1.reshape(-1),
            g_w2.reshape(-1),
            gcw[:TAPS].reshape(-1),
            gvec[0],
            gvec[1],
            gvec[2],
            gvec[3],
            gvec[4],
            gb1[0],
            jnp.zeros((flat_size - used,), F32),
        ]
    )
    grad_shard = lax.psum_scatter(grad_full, ("dp", "fsdp"), scatter_dimension=0, tiled=True)
    own_sum, disc_sum = lax.psum(
        (jnp.sum(grad_shard * grad_shard), jnp.sum(disc_grads * disc_grads)), ("dp", "fsdp")
    )
    grad_norm = jnp.sqrt(own_sum + disc_sum)
    clipped = grad_shard * jnp.minimum(1.0, 20.0 * jnp.sqrt(total_frames) / (grad_norm + 1e-06))
    new_momentum = 0.9 * momentum + clipped
    new_master = master - (clipped + 0.9 * new_momentum) / jnp.sqrt(total_frames)
    new_average = 0.99 * average + 0.01 * new_master
    return (
        block_out,
        input_grad,
        grad_norm,
        new_master,
        new_momentum,
        new_average,
        new_master.astype(BF16),
        new_average.astype(BF16),
    )


def solution(mesh):
    clip_spec = P(("dp", "fsdp"), None, None)
    flat_spec = P(("dp", "fsdp"))
    return jax.shard_map(
        body,
        mesh=mesh,
        in_specs=(clip_spec, flat_spec, clip_spec, flat_spec, flat_spec, flat_spec, flat_spec),
        out_specs=(clip_spec, clip_spec, P(), flat_spec, flat_spec, flat_spec, flat_spec, flat_spec),
        check_vma=False,
    )
```

time: 849 us -> 553 us (0.65)
  matrix products: 256 us -> 0 us
  other arithmetic: 271 us -> 65.8 us
  Pallas kernels: 0 us -> 111 us
  waiting for transfers between devices: 219 us -> 277 us
    dot_general x6 -> x0, matrix products: 256 us -> none  [the longest x1 121 us: body(): jnp.dot(act, w_one, preferred_element_type=jnp.float32)]
    reduce_sum x4 -> x0, other arithmetic: 145 us -> none  [the longest x1 84.4 us: conv_norm(): summed = summed + conv_w[offset] * padded[:, offset:offset + length, :]]
    pallas_call x0 -> x1, Pallas kernels: none -> 111 us  [fused_block(): pl.pallas_call(kernel, grid_spec=grid_spec, out_shape=[jax.ShapeDtypeStru...]
    add x1 -> x0, other arithmetic: 47.2 us -> none  [body(): input_grad = d_out.reshape(clips, length, width) + mask * d_masked]
    unnamed x3, waiting for transfers between devices: 155 us -> 202 us
    all_gather x1, waiting for transfers between devices: 63.4 us -> 74.5 us  [body(): packed = lax.all_gather(rounded, ('dp', 'fsdp'), axis=0, tiled=True)]
    mul x1 -> x0, other arithmetic: 9.73 us -> none  [body(): masked = floats * mask]
    unnamed x99 -> x22, local copies, waits for them, and re-layouts: 22.2 us -> 22.3 us
  transfers between devices with their start and end apart: 2 -> 2, of which waited for: 2 -> 2; matrix products, arithmetic and copies ran while one was open for 1% -> 0% of each run, Pallas kernels for 0% -> 0%
where the time goes in v1:
time: 553 us; the launch traced here: 549 us
  waiting for transfers between devices  277 us (50%)
  Pallas kernels  111 us (20%)
  other arithmetic  65.8 us (12%)
  blocking collectives  40 us (7%)
  local copies, waits for them, and re-layouts  38.7 us (7%)
  between operations  17.3 us (3%)
    unnamed x3, waiting for transfers between devices  202 us
    pallas_call x1, Pallas kernels, fused_block(): pl.pallas_call(kernel, grid_spec=grid_spec, out_shape=[jax.ShapeDtypeStru...  111 us
    all_gather x1, waiting for transfers between devices, body(): packed = lax.all_gather(rounded, ('dp', 'fsdp'), axis=0, tiled=True)  74.5 us
    all_gather x1, other arithmetic, body(): packed = lax.all_gather(rounded, ('dp', 'fsdp'), axis=0, tiled=True)  58.8 us
    psum x1, blocking collectives, body(): lax.psum((jnp.sum(grad_shard * grad_shard), jnp.sum(disc_grads * disc_gra...  40 us
    unnamed x22, local copies, waits for them, and re-layouts  22.3 us
  transfers between devices with their start and end apart: 2, of which 2 were waited for; matrix products, arithmetic and copies ran while one was open for 0% of the time, Pallas kernels for 0%

profile of v1, /device:TPU:0, one launch (start us, length us, event | category | flops | bytes accessed | tf_op | source)
XLA Modules:
  0.0 549.4 jit_solution(8546456817799358905)
XLA Ops:
  7.2 0.9 convert_element_type.15
  9.0 74.5 %all-gather.3.cloned.1.call-done = bf16[32,1,49408]{2,1,0:T(2,128)(2,1)} async-done(((bf16[1,1,49408]{2,1,0:T(2,128)(2,1)}), bf16[32,1,49408]{2,1,0:T(2,128)(2,1)}) %all-gather.3.cloned.1.call-update) | async-done | bytes 3162128 | tf_op jit(solution)/shard_map/all_gather | solution.py:249
  83.5 58.8 %reduce.4 = bf16[32,49408]{1,0:T(8,128)(2,1)} reduce(bf16[32,1,49408]{2,1,0:T(2,128)(2,1)} %all-gather.3.cloned.1.call-done, bf16[]{:T(256)} %constant.83), dimensions={1}, to_apply=%all-gather.reduce_sub_computation | reduce | bytes 6324226 | tf_op jit(solution)/shard_map/all_gather | solution.py:249
  142.3 6.0 %reshape.107 = bf16[1581056]{0:T(1024)(128)(2,1)S(1)} reshape(bf16[32,49408]{1,0:T(8,128)(2,1)} %reduce.4) | data formatting | bytes 6324224
  148.3 1.9 fusion.2
  150.2 3.8 slice.98.w2_ref
  154.7 4.2 reshape.101.w1_ref
  159.6 110.6 %shard_map.134 = (bf16[8,1024,512]{2,1,0:T(8,128)(2,1)}, f32[8,1024,512]{2,1,0:T(8,128)}, f32[512,1536]{1,0:T(8,128)}, f32[1536,512]{1,0:T(8,128)}, f32[8,512]{1...) custom-call(s32[8]{0:T(128)} %counts_ref.1, bf16[8,1024,512]{2,1,0:T(8,128)(2,1)} %fr_ref.1, ...), custom_call_target="tpu_custom_call" | custom-call | flops 77309411328 | bytes 46137344 | tf_op jit(solution)/shard_map/pallas_call | solution.py:210
  272.6 2.7 reshape.103
  275.3 2.7 copy.15
  278.0 1.9 constant_dynamic-update-slice_fusion.9
  279.9 1.8 constant_dynamic-update-slice_fusion.8
  281.7 1.3 constant_dynamic-update-slice_fusion.7
  283.1 1.3 constant_dynamic-update-slice_fusion.6
  284.4 1.3 constant_dynamic-update-slice_fusion.5
  285.7 1.3 constant_dynamic-update-slice_fusion.4
  286.9 1.3 constant_dynamic-update-slice_fusion.3
  288.2 1.3 constant_dynamic-update-slice_fusion.2
  289.5 1.3 constant_dynamic-update-slice_fusion.1
  290.8 1.3 constant_dynamic-update-slice_fusion
  292.8 202.5 %all-reduce.6.cloned.1.call-done = f32[1581056]{0:T(1024)} async-done(((f32[1581056]{0:T(1024)}), f32[1581056]{0:T(1024)}) %all-reduce.6.cloned.1.call-update) | async-done | bytes 6324240
  495.2 1.7 multiply_reduce_fusion
  498.2 40.0 %psum.16 = f32[]{:T(128)} all-reduce(f32[]{:T(128)S(6)} %add.31), channel_id=1, replica_groups=mesh['dp'=4,'fsdp'=8] {'dp','fsdp'}, use_global_device_ids=true, to_apply=%region_2.0 | all-reduce | flops 1 | bytes 8 | tf_op jit(solution)/shard_map/psum | solution.py:272
  538.9 1.9 fusion
  (33 shorter events, 6.0 us)
Async XLA Ops:
  7.2 76.4 %all-gather.3.cloned.1.call-start = ((), (), s32[]{:S(2)}) async-start(), calls=%async_computation | async-start | bytes 6521856 | tf_op jit(solution)/shard_map/all_gather | solution.py:249
  9.0 486.3 %all-reduce.6.cloned.1.call-start = ((), (), s32[]{:S(2)}) async-start(), calls=%async_computation.1 | async-start | bytes 12648448
  279.9 12.2 %copy-start.4 = (f32[32768]{0:T(1024)S(1)}, f32[32768]{0:T(1024)}, u32[]{:S(2)}) copy-start(f32[32768]{0:T(1024)} %param.17) | copy-start | bytes 393220
  279.9 259.0 %copy-start = (f32[49408]{0:T(1024)S(1)}, f32[49408]{0:T(1024)}, u32[]{:S(2)}) copy-start(f32[49408]{0:T(1024)} %param.14) | copy-start | bytes 592900
  279.9 259.0 %copy-start.2 = (f32[49408]{0:T(1024)S(1)}, f32[49408]{0:T(1024)}, u32[]{:S(2)}) copy-start(f32[49408]{0:T(1024)} %param.16) | copy-start | bytes 592900
  279.9 259.0 %copy-start.3 = (f32[49408]{0:T(1024)S(1)}, f32[49408]{0:T(1024)}, u32[]{:S(2)}) copy-start(f32[49408]{0:T(1024)} %param.15) | copy-start | bytes 592900
  540.8 0.7 copy-start.1
Sparse Core Ops, SparseCore 0:
  11.4 72.1 all-gather.2
  292.2 202.9 all-reduce.5

commit v2 on v1

--- a/solution.py
+++ b/solution.py
@@ -238,15 +238,71 @@
     return (tuple(pieces), start_at)
 
 
-def body(frames, counts, cotangent, master, momentum, average, disc_grads):
-    devices = lax.axis_size(("dp", "fsdp"))
+AXES = ("dp", "fsdp")
+LANES = 128
+
+
+def bit_order(mesh_sizes):
+    dp_size, fsdp_size = mesh_sizes
+    fsdp_bits = int(math.log2(fsdp_size))
+    dp_bits = int(math.log2(dp_size))
+    order = [0] + [fsdp_bits + b for b in range(dp_bits)] + list(range(1, fsdp_bits))
+    return order, fsdp_bits + dp_bits
+
+
+def swap_perm(devices, bit):
+    return [(i, i ^ (1 << bit)) for i in range(devices)]
+
+
+def tree_all_gather(shard, order, nbits):
+    me = lax.axis_index(AXES)
+    devices = 1 << nbits
+    held = shard
+    held_bits = []
+    for bit in order:
+        other = lax.ppermute(held, AXES, swap_perm(devices, bit))
+        upper = ((me >> bit) & 1) == 1
+        held = jnp.stack([jnp.where(upper, other, held), jnp.where(upper, held, other)])
+        held_bits.insert(0, bit)
+    axes = [held_bits.index(b) for b in sorted(held_bits, reverse=True)]
+    held = jnp.transpose(held, axes + [nbits, nbits + 1])
+    return held.reshape(devices * shard.shape[0], LANES)
+
+
+def tree_reduce_scatter(full, order, nbits):
+    me = lax.axis_index(AXES)
+    devices = 1 << nbits
+    rows = full.shape[0] // devices
+    held = full.reshape([2] * nbits + [rows, LANES])
+    held_bits = [nbits - 1 - a for a in range(nbits)]
+    for bit in order:
+        axis = held_bits.index(bit)
+        mine = (me >> bit) & 1
+        keep = lax.dynamic_index_in_dim(held, mine, axis=axis, keepdims=False)
+        send = lax.dynamic_index_in_dim(held, 1 - mine, axis=axis, keepdims=False)
+        held = keep + lax.ppermute(send, AXES, swap_perm(devices, bit))
+        held_bits.pop(axis)
+    return held
+
+
+def tree_all_sum(value, order, nbits):
+    devices = 1 << nbits
+    for bit in reversed(order):
+        value = value + lax.ppermute(value, AXES, swap_perm(devices, bit))
+    return value
+
+
+def body(frames, counts, cotangent, master, momentum, average, disc_grads, mesh_sizes=None):
+    order, nbits = bit_order(mesh_sizes)
+    devices = 1 << nbits
     clips, length, width = frames.shape
     hidden = 3 * width
     rows = clips * length
-    flat_size = master.shape[0] * devices
+    local = master.shape[0]
+    flat_size = local * devices
     total_frames = jnp.float32(rows * devices)
-    rounded = master.astype(BF16)
-    packed = lax.all_gather(rounded, ("dp", "fsdp"), axis=0, tiled=True)
+    rounded = master.astype(BF16).reshape(local // LANES, LANES)
+    packed = tree_all_gather(rounded, order[::-1], nbits).reshape(-1)
     (w_one, w_two, conv_w, conv_b, ln_g, ln_b, b_two, gamma, b_one), used = unpack(packed, width, hidden)
     cw8 = jnp.zeros((8, width), F32).at[:TAPS].set(conv_w.astype(F32))
     vec8 = jnp.concatenate(
@@ -267,12 +323,14 @@
             gb1[0],
             jnp.zeros((flat_size - used,), F32),
         ]
-    )
-    grad_shard = lax.psum_scatter(grad_full, ("dp", "fsdp"), scatter_dimension=0, tiled=True)
-    own_sum, disc_sum = lax.psum(
-        (jnp.sum(grad_shard * grad_shard), jnp.sum(disc_grads * disc_grads)), ("dp", "fsdp")
-    )
-    grad_norm = jnp.sqrt(own_sum + disc_sum)
+    ).reshape(flat_size // LANES, LANES)
+    grad_shard = tree_reduce_scatter(grad_full, order, nbits)
+    disc_rows = jnp.sum((disc_grads * disc_grads).reshape(-1, LANES), axis=0, keepdims=True)
+    own_rows = jnp.sum(grad_shard * grad_shard, axis=0, keepdims=True)
+    squares = jnp.broadcast_to(own_rows + disc_rows, (8, LANES))
+    squares = tree_all_sum(squares, order, nbits)
+    grad_norm = jnp.sqrt(jnp.sum(squares[0]))
+    grad_shard = grad_shard.reshape(-1)
     clipped = grad_shard * jnp.minimum(1.0, 20.0 * jnp.sqrt(total_frames) / (grad_norm + 1e-06))
     new_momentum = 0.9 * momentum + clipped
     new_master = master - (clipped + 0.9 * new_momentum) / jnp.sqrt(total_frames)
@@ -292,8 +350,9 @@
 def solution(mesh):
     clip_spec = P(("dp", "fsdp"), None, None)
     flat_spec = P(("dp", "fsdp"))
+    mesh_sizes = (mesh.shape["dp"], mesh.shape["fsdp"])
     return jax.shard_map(
-        body,
+        functools.partial(body, mesh_sizes=mesh_sizes),
         mesh=mesh,
         in_specs=(clip_spec, flat_spec, clip_spec, flat_spec, flat_spec, flat_spec, flat_spec),
         out_specs=(clip_spec, clip_spec, P(), flat_spec, flat_spec, flat_spec, flat_spec, flat_spec),

time: 553 us -> 371 us (0.67)
  waiting for transfers between devices: 277 us -> 126 us
  other arithmetic: 65.8 us -> 12.7 us
  blocking collectives: 40 us -> 0 us
  starting transfers between devices: 0.08 us -> 36.9 us
  Pallas kernels: 111 us -> 137 us
  between operations: 17.3 us -> 2.81 us
  local copies, waits for them, and re-layouts: 38.7 us -> 51 us
    unnamed x3 -> x0, waiting for transfers between devices: 202 us -> none
    ppermute x0 -> x15, waiting for transfers between devices: none -> 126 us  [the longest x5 74.9 us: tree_reduce_scatter(): held = keep + lax.ppermute(send, AXES, swap_perm(devices, bit))]
    all_gather x1 -> x0, waiting for transfers between devices: 74.5 us -> none  [body(): packed = lax.all_gather(rounded, ('dp', 'fsdp'), axis=0, tiled=True)]
    all_gather x1 -> x0, other arithmetic: 58.8 us -> none  [body(): packed = lax.all_gather(rounded, ('dp', 'fsdp'), axis=0, tiled=True)]
    psum x1 -> x0, blocking collectives: 40 us -> none  [body(): lax.psum((jnp.sum(grad_shard * grad_shard), jnp.sum(disc_grads * disc_gra...]
    ppermute x0 -> x15, starting transfers between devices: none -> 36.9 us  [the longest x5 25.5 us: tree_reduce_scatter(): held = keep + lax.ppermute(send, AXES, swap_perm(devices, bit))]
    pallas_call x1, Pallas kernels: 111 us -> 137 us  [fused_block(): pl.pallas_call(kernel, grid_spec=grid_spec, out_shape=[jax.ShapeDtypeStru...]
    another operation x1 -> x5, local copies, waits for them, and re-layouts: 0.01 us -> 11.4 us  [the longest x1 5.99 us: tree_reduce_scatter(): held = full.reshape([2] * nbits + [rows, LANES])]
  transfers between devices with their start and end apart: 2 -> 15, of which waited for: 2 -> 15; matrix products, arithmetic and copies ran while one was open for 0% -> 0% of each run, Pallas kernels for 0% -> 0%
where the time goes in v2:
time: 371 us; the launch traced here: 367 us
  Pallas kernels  137 us (37%)
  waiting for transfers between devices  126 us (34%)
  local copies, waits for them, and re-layouts  51 us (14%)
  starting transfers between devices  36.9 us (10%)
  other arithmetic  12.7 us (3%)
    pallas_call x1, Pallas kernels, fused_block(): pl.pallas_call(kernel, grid_spec=grid_spec, out_shape=[jax.ShapeDtypeStru...  137 us
    ppermute x5, waiting for transfers between devices, tree_reduce_scatter(): held = keep + lax.ppermute(send, AXES, swap_perm(devices, bit))  74.9 us
    ppermute x5, waiting for transfers between devices, tree_all_gather(): other = lax.ppermute(held, AXES, swap_perm(devices, bit))  38.2 us
    ppermute x5, starting transfers between devices, tree_reduce_scatter(): held = keep + lax.ppermute(send, AXES, swap_perm(devices, bit))  25.5 us
    unnamed x22, local copies, waits for them, and re-layouts  16.8 us
    ppermute x5, waiting for transfers between devices, tree_all_sum(): value = value + lax.ppermute(value, AXES, swap_perm(devices, bit))  12.7 us
    ppermute x5, starting transfers between devices, tree_all_gather(): other = lax.ppermute(held, AXES, swap_perm(devices, bit))  7.56 us
  transfers between devices with their start and end apart: 15, of which 15 were waited for; matrix products, arithmetic and copies ran while one was open for 0% of the time, Pallas kernels for 0%

profile of v2, /device:TPU:0, one launch (start us, length us, event | category | flops | bytes accessed | tf_op | source)
XLA Modules:
  0.0 366.6 jit_solution(12837627755157590198)
XLA Ops:
  1.6 4.1 %collective-permute-start = (bf16[386,128]{1,0:T(8,128)(2,1)S(1)}, bf16[386,128]{1,0:T(8,128)(2,1)S(1)}, u32[]{:S(2)}, u32[]{:S(2)}) collective-permute-start(bf16[386,128]{1,0:T(8,128)(2,1)S(1)} %convert_bitcast_fusion), channel_id=1, source_target_pairs={{0,4},{1,5},{2,6},{3,7},{4,0},{5,1},{6,2},{7,3},{8,12},{9,13},{10,... | collective-permute-start | bytes 296456 | tf_op jit(solution)/shard_map/ppermute | solution.py:263
  5.7 5.0 %collective-permute-done = bf16[386,128]{1,0:T(8,128)(2,1)S(1)} collective-permute-done((bf16[386,128]{1,0:T(8,128)(2,1)S(1)}, bf16[386,128]{1,0:T(8,128)(2,1)S(1)}, u32[]{:S(2)}, u32[]{:S(2)}) %collective-permute-start) | collective-permute-done | bytes 98848 | tf_op jit(solution)/shard_map/ppermute | solution.py:263
  12.5 5.4 %collective-permute-done.1 = bf16[2,386,128]{2,1,0:T(8,128)(2,1)S(1)} collective-permute-done((bf16[2,386,128]{2,1,0:T(8,128)(2,1)S(1)}, bf16[2,386,128]{2,1,0:T(8,128)(2,1)S(1)}, u32[]{:S(2)}, u32[]{:S(2)}) %collective-permute-start.1) | collective-permute-done | bytes 197664 | tf_op jit(solution)/shard_map/ppermute | solution.py:263
  19.3 8.3 %collective-permute-done.2 = bf16[2,2,386,128]{3,2,1,0:T(8,128)(2,1)S(1)} collective-permute-done((bf16[2,2,386,128]{3,2,1,0:T(8,128)(2,1)S(1)}, bf16[2,2,386,128]{3,2,1,0:T(8,128)(2,1)S(1)}, u32[]{:S(2)}, u32[]{:S(2)}) %collective-permute-start.2) | collective-permute-done | bytes 395296 | tf_op jit(solution)/shard_map/ppermute | solution.py:263
  29.7 15.8 %collective-permute-done.3 = bf16[2,2,2,386,128]{4,2,3,1,0:T(2,128)(2,1)S(1)} collective-permute-done((bf16[2,2,2,386,128]{4,2,3,1,0:T(2,128)(2,1)S(1)}, bf16[2,2,2,386,128]{4,2,3,1,0:T(2,128)(2,1)S(1)}, u32[]{:S(2)}, u32[]{:S(2)}) %collective-permute-start.3) | collective-permute-done | bytes 790560 | tf_op jit(solution)/shard_map/ppermute | solution.py:263
  48.3 3.6 collective-permute-done.4
  52.8 2.4 reshape_reshape.6
  55.2 3.2 slice.86
  59.3 2.8 slice.104.w2_ref
  62.1 2.7 reshape.103.w1_ref
  66.2 137.5 %shard_map.134 = (bf16[8,1024,512]{2,1,0:T(8,128)(2,1)}, f32[8,1024,512]{2,1,0:T(8,128)}, f32[512,1536]{1,0:T(8,128)}, f32[1536,512]{1,0:T(8,128)}, f32[8,512]{1...) custom-call(s32[8]{0:T(128)} %counts_ref.1, bf16[8,1024,512]{2,1,0:T(8,128)(2,1)} %fr_ref.1, ...), custom_call_target="tpu_custom_call" | custom-call | flops 77309411328 | bytes 46137344 | tf_op jit(solution)/shard_map/pallas_call | solution.py:210
  206.1 2.7 reshape.105
  208.8 2.7 copy.77
  225.7 6.0 %reshape_reshape.7 = f32[2,2,2,2,2,386,128]{6,5,4,3,2,1,0:T(8,128)} reshape(f32[1581056]{0:T(1024)} %constant_dynamic-update-slice_fusion) | data formatting | bytes 12648448 | tf_op jit(solution)/shard_map/reshape;reshape | solution.py:276
  235.6 5.8 %collective-permute-done.5 = f32[2,2,2,2,386,128]{5,3,4,2,1,0:T(2,128)} collective-permute-done((f32[2,2,2,2,386,128]{5,3,4,2,1,0:T(2,128)S(1)}, f32[2,2,2,2,386,128]{5,3,4,2,1,0:T(2,128)}, u32[]{:S(2)}, u32[]{:S(2)}) %collective-permute-start.5) | collective-permute-done | bytes 3162144 | tf_op jit(solution)/shard_map/ppermute | solution.py:283
  241.4 3.2 bitcast_add_fusion
  247.7 35.9 %collective-permute-done.6 = f32[2,2,2,386,128]{4,2,3,1,0:T(2,128)} collective-permute-done((f32[2,2,2,386,128]{4,2,3,1,0:T(2,128)}, f32[2,2,2,386,128]{4,2,3,1,0:T(2,128)}, u32[]{:S(2)}, u32[]{:S(2)}) %collective-permute-start.6) | collective-permute-done | bytes 1581088 | tf_op jit(solution)/shard_map/ppermute | solution.py:283
  288.3 17.5 %collective-permute-done.7 = f32[2,2,386,128]{3,1,2,0:T(2,128)S(1)} collective-permute-done((f32[2,2,386,128]{3,1,2,0:T(2,128)S(1)}, f32[2,2,386,128]{3,1,2,0:T(2,128)S(1)}, u32[]{:S(2)}, u32[]{:S(2)}) %collective-permute-start.7) | collective-permute-done | bytes 790560 | tf_op jit(solution)/shard_map/ppermute | solution.py:283
  307.1 3.3 collective-permute-start.8
  310.4 8.4 %collective-permute-done.8 = f32[2,386,128]{2,1,0:T(8,128)S(1)} collective-permute-done((f32[2,386,128]{2,1,0:T(8,128)S(1)}, f32[2,386,128]{2,1,0:T(8,128)S(1)}, u32[]{:S(2)}, u32[]{:S(2)}) %collective-permute-start.8) | collective-permute-done | bytes 395296 | tf_op jit(solution)/shard_map/ppermute | solution.py:283
  318.9 19.7 %collective-permute-start.9 = (f32[386,128]{1,0:T(8,128)S(1)}, f32[386,128]{1,0:T(8,128)S(1)}, u32[]{:S(2)}, u32[]{:S(2)}) collective-permute-start(f32[386,128]{1,0:T(8,128)S(1)} %dynamic-slice_bitcast_fusion.4), channel_id=1, source_target_pairs={{0,4},{1,5},{2,6},{3,7},{4,0},{5,1},{6,2},{7,3},{8,12},{9,13},{10,... | collective-permute-start | bytes 592904 | tf_op jit(solution)/shard_map/ppermute | solution.py:283
  338.6 7.3 %collective-permute-done.9 = f32[386,128]{1,0:T(8,128)S(1)} collective-permute-done((f32[386,128]{1,0:T(8,128)S(1)}, f32[386,128]{1,0:T(8,128)S(1)}, u32[]{:S(2)}, u32[]{:S(2)}) %collective-permute-start.9) | collective-permute-done | bytes 197664 | tf_op jit(solution)/shard_map/ppermute | solution.py:283
  346.1 4.5 %collective-permute-done.10 = f32[8,128]{1,0:T(8,128)S(1)} collective-permute-done((f32[8,128]{1,0:T(8,128)S(1)}, f32[8,128]{1,0:T(8,128)S(1)}, u32[]{:S(2)}, u32[]{:S(2)}) %collective-permute-start.10) | collective-permute-done | bytes 4128 | tf_op jit(solution)/shard_map/ppermute | solution.py:291
  358.7 2.7 collective-permute-done.13
  (93 shorter events, 53.2 us)
Async XLA Ops:
  1.6 9.1 %collective-permute-start = (bf16[386,128]{1,0:T(8,128)(2,1)S(1)}, bf16[386,128]{1,0:T(8,128)(2,1)S(1)}, u32[]{:S(2)}, u32[]{:S(2)}) collective-permute-start(bf16[386,128]{1,0:T(8,128)(2,1)S(1)} %convert_bitcast_fusion), channel_id=1, source_target_pairs={{0,4},{1,5},{2,6},{3,7},{4,0},{5,1},{6,2},{7,3},{8,12},{9,13},{10,... | collective-permute-start | bytes 296456 | tf_op jit(solution)/shard_map/ppermute | solution.py:263
  11.7 6.2 %collective-permute-start.1 = (bf16[2,386,128]{2,1,0:T(8,128)(2,1)S(1)}, bf16[2,386,128]{2,1,0:T(8,128)(2,1)S(1)}, u32[]{:S(2)}, u32[]{:S(2)}) collective-permute-start(bf16[2,386,128]{2,1,0:T(8,128)(2,1)S(1)} %pad_maximum_fusion.3), channel_id=1, source_target_pairs={{0,2},{1,3},{2,0},{3,1},{4,6},{5,7},{6,4},{7,5},{8,10},{9,11},{10,... | collective-permute-start | bytes 592904 | tf_op jit(solution)/shard_map/ppermute | solution.py:263
  18.0 9.7 %collective-permute-start.2 = (bf16[2,2,386,128]{3,2,1,0:T(8,128)(2,1)S(1)}, bf16[2,2,386,128]{3,2,1,0:T(8,128)(2,1)S(1)}, u32[]{:S(2)}, u32[]{:S(2)}) collective-permute-start(bf16[2,2,386,128]{3,2,1,0:T(8,128)(2,1)S(1)} %pad_maximum_fusion.2), channel_id=1, source_target_pairs={{0,16},{1,17},{2,18},{3,19},{4,20},{5,21},{6,22},{7,23},{8,24},{9,... | collective-permute-start | bytes 1185800 | tf_op jit(solution)/shard_map/ppermute | solution.py:263
  28.4 17.1 %collective-permute-start.3 = (bf16[2,2,2,386,128]{4,2,3,1,0:T(2,128)(2,1)S(1)}, bf16[2,2,2,386,128]{4,2,3,1,0:T(2,128)(2,1)S(1)}, u32[]{:S(2)}, u32[]{:S(2)}) collective-permute-start(bf16[2,2,2,386,128]{4,2,3,1,0:T(2,128)(2,1)S(1)} %copy.63), channel_id=1, source_target_pairs={{0,8},{1,9},{2,10},{3,11},{4,12},{5,13},{6,14},{7,15},{8,0},{9,1},... | collective-permute-start | bytes 2371592 | tf_op jit(solution)/shard_map/ppermute | solution.py:263
  48.3 3.6 collective-permute-start.4
  58.5 3.7 slice-start
  58.5 3.7 %slice-start.1 = ((bf16[1581056]{0:T(1024)(128)(2,1)}), bf16[786432]{0:T(1024)(128)(2,1)S(1)}, s32[]{:S(2)}) async-start(bf16[1581056]{0:T(1024)(128)(2,1)} %reshape_reshape.6), calls=%async_computation.1 | async-start | bytes 3145728 | tf_op jit(solution)/shard_map/slice | solution.py:236
  59.3 6.2 %slice-start.2 = ((bf16[3088,512]{1,0:T(8,128)(2,1)}), bf16[7,512]{1,0:T(8,128)(2,1)S(1)}, s32[]{:S(2)}) async-start(bf16[3088,512]{1,0:T(8,128)(2,1)} %slice.86), calls=%async_computation.2 | async-start | bytes 16384 | tf_op jit(solution)/shard_map/slice | solution.py:236
  235.5 5.9 %collective-permute-start.5 = (f32[2,2,2,2,386,128]{5,3,4,2,1,0:T(2,128)S(1)}, f32[2,2,2,2,386,128]{5,3,4,2,1,0:T(2,128)}, u32[]{:S(2)}, u32[]{:S(2)}) collective-permute-start(f32[2,2,2,2,386,128]{5,3,4,2,1,0:T(2,128)S(1)} %copy.71), channel_id=1, source_target_pairs={{0,1},{1,0},{2,3},{3,2},{4,5},{5,4},{6,7},{7,6},{8,9},{9,8},{10,11... | collective-permute-start | bytes 9486344 | tf_op jit(solution)/shard_map/ppermute | solution.py:283
  246.7 36.9 %collective-permute-start.6 = (f32[2,2,2,386,128]{4,2,3,1,0:T(2,128)}, f32[2,2,2,386,128]{4,2,3,1,0:T(2,128)}, u32[]{:S(2)}, u32[]{:S(2)}) collective-permute-start(f32[2,2,2,386,128]{4,2,3,1,0:T(2,128)} %copy.73), channel_id=1, source_target_pairs={{0,8},{1,9},{2,10},{3,11},{4,12},{5,13},{6,14},{7,15},{8,0},{9,1},... | collective-permute-start | bytes 4743176 | tf_op jit(solution)/shard_map/ppermute | solution.py:283
  285.2 1.2 copy-start
  286.4 52.2 %copy-start.5 = (f32[32768]{0:T(1024)S(1)}, f32[32768]{0:T(1024)}, u32[]{:S(2)}) copy-start(f32[32768]{0:T(1024)} %param.17) | copy-start | bytes 393220
  286.9 77.0 %copy-start.1 = (f32[49408]{0:T(1024)S(1)}, f32[49408]{0:T(1024)}, u32[]{:S(2)}) copy-start(f32[49408]{0:T(1024)} %param.14) | copy-start | bytes 592900
  286.9 77.0 %copy-start.3 = (f32[49408]{0:T(1024)S(1)}, f32[49408]{0:T(1024)}, u32[]{:S(2)}) copy-start(f32[49408]{0:T(1024)} %param.16) | copy-start | bytes 592900
  286.9 77.0 %copy-start.4 = (f32[49408]{0:T(1024)S(1)}, f32[49408]{0:T(1024)}, u32[]{:S(2)}) copy-start(f32[49408]{0:T(1024)} %param.15) | copy-start | bytes 592900
  286.9 18.9 %collective-permute-start.7 = (f32[2,2,386,128]{3,1,2,0:T(2,128)S(1)}, f32[2,2,386,128]{3,1,2,0:T(2,128)S(1)}, u32[]{:S(2)}, u32[]{:S(2)}) collective-permute-start(f32[2,2,386,128]{3,1,2,0:T(2,128)S(1)} %copy.75), channel_id=1, source_target_pairs={{0,16},{1,17},{2,18},{3,19},{4,20},{5,21},{6,22},{7,23},{8,24},{9,... | collective-permute-start | bytes 2371592 | tf_op jit(solution)/shard_map/ppermute | solution.py:283
  307.1 11.7 %collective-permute-start.8 = (f32[2,386,128]{2,1,0:T(8,128)S(1)}, f32[2,386,128]{2,1,0:T(8,128)S(1)}, u32[]{:S(2)}, u32[]{:S(2)}) collective-permute-start(f32[2,386,128]{2,1,0:T(8,128)S(1)} %dynamic-slice_bitcast_fusion.3), channel_id=1, source_target_pairs={{0,2},{1,3},{2,0},{3,1},{4,6},{5,7},{6,4},{7,5},{8,10},{9,11},{10,... | collective-permute-start | bytes 1185800 | tf_op jit(solution)/shard_map/ppermute | solution.py:283
  318.9 27.0 %collective-permute-start.9 = (f32[386,128]{1,0:T(8,128)S(1)}, f32[386,128]{1,0:T(8,128)S(1)}, u32[]{:S(2)}, u32[]{:S(2)}) collective-permute-start(f32[386,128]{1,0:T(8,128)S(1)} %dynamic-slice_bitcast_fusion.4), channel_id=1, source_target_pairs={{0,4},{1,5},{2,6},{3,7},{4,0},{5,1},{6,2},{7,3},{8,12},{9,13},{10,... | collective-permute-start | bytes 592904 | tf_op jit(solution)/shard_map/ppermute | solution.py:283
  346.0 4.6 %collective-permute-start.10 = (f32[8,128]{1,0:T(8,128)S(1)}, f32[8,128]{1,0:T(8,128)S(1)}, u32[]{:S(2)}, u32[]{:S(2)}) collective-permute-start(f32[8,128]{1,0:T(8,128)S(1)} %broadcast_in_dim.5), channel_id=1, source_target_pairs={{0,4},{1,5},{2,6},{3,7},{4,0},{5,1},{6,2},{7,3},{8,12},{9,13},{10,... | collective-permute-start | bytes 12296 | tf_op jit(solution)/shard_map/ppermute | solution.py:291
  350.6 3.6 collective-permute-start.11
  354.2 3.6 collective-permute-start.12
  357.8 3.6 collective-permute-start.13
  361.4 1.2 collective-permute-start.14
  364.8 0.7 copy-start.2

commit v3 on v2

--- a/solution.py
+++ b/solution.py
@@ -254,35 +254,52 @@
     return [(i, i ^ (1 << bit)) for i in range(devices)]
 
 
-def tree_all_gather(shard, order, nbits):
+def split_orders(order):
+    if len(order) < 3:
+        return [order]
+    other = [order[0], order[2], order[1]] + order[3:]
+    return [order, other]
+
+
+def tree_all_gather(shard, orders, nbits):
     me = lax.axis_index(AXES)
     devices = 1 << nbits
-    held = shard
-    held_bits = []
-    for bit in order:
-        other = lax.ppermute(held, AXES, swap_perm(devices, bit))
-        upper = ((me >> bit) & 1) == 1
-        held = jnp.stack([jnp.where(upper, other, held), jnp.where(upper, held, other)])
-        held_bits.insert(0, bit)
-    axes = [held_bits.index(b) for b in sorted(held_bits, reverse=True)]
-    held = jnp.transpose(held, axes + [nbits, nbits + 1])
-    return held.reshape(devices * shard.shape[0], LANES)
-
-
-def tree_reduce_scatter(full, order, nbits):
+    rows = shard.shape[0]
+    cuts = [rows * p // len(orders) for p in range(len(orders) + 1)]
+    held = [shard[cuts[p]:cuts[p + 1]] for p in range(len(orders))]
+    held_bits = [[] for _ in orders]
+    for step in range(nbits):
+        for p, order in enumerate(orders):
+            bit = order[step]
+            other = lax.ppermute(held[p], AXES, swap_perm(devices, bit))
+            upper = ((me >> bit) & 1) == 1
+            held[p] = jnp.stack([jnp.where(upper, other, held[p]), jnp.where(upper, held[p], other)])
+            held_bits[p].insert(0, bit)
+    parts = []
+    for p in range(len(orders)):
+        axes = [held_bits[p].index(b) for b in sorted(held_bits[p], reverse=True)]
+        parts.append(jnp.transpose(held[p], axes + [nbits, nbits + 1]).reshape(devices, -1, LANES))
+    return jnp.concatenate(parts, axis=1).reshape(devices * rows, LANES)
+
+
+def tree_reduce_scatter(full, orders, nbits):
     me = lax.axis_index(AXES)
     devices = 1 << nbits
     rows = full.shape[0] // devices
-    held = full.reshape([2] * nbits + [rows, LANES])
-    held_bits = [nbits - 1 - a for a in range(nbits)]
-    for bit in order:
-        axis = held_bits.index(bit)
-        mine = (me >> bit) & 1
-        keep = lax.dynamic_index_in_dim(held, mine, axis=axis, keepdims=False)
-        send = lax.dynamic_index_in_dim(held, 1 - mine, axis=axis, keepdims=False)
-        held = keep + lax.ppermute(send, AXES, swap_perm(devices, bit))
-        held_bits.pop(axis)
-    return held
+    cuts = [rows * p // len(orders) for p in range(len(orders) + 1)]
+    shaped = full.reshape([2] * nbits + [rows, LANES])
+    held = [shaped[..., cuts[p]:cuts[p + 1], :] for p in range(len(orders))]
+    held_bits = [[nbits - 1 - a for a in range(nbits)] for _ in orders]
+    for step in range(nbits):
+        for p, order in enumerate(orders):
+            bit = order[step]
+            axis = held_bits[p].index(bit)
+            mine = (me >> bit) & 1
+            keep = lax.dynamic_index_in_dim(held[p], mine, axis=axis, keepdims=False)
+            send = lax.dynamic_index_in_dim(held[p], 1 - mine, axis=axis, keepdims=False)
+            held[p] = keep + lax.ppermute(send, AXES, swap_perm(devices, bit))
+            held_bits[p].pop(axis)
+    return jnp.concatenate(held, axis=0)
 
 
 def tree_all_sum(value, order, nbits):
@@ -302,7 +319,7 @@
     flat_size = local * devices
     total_frames = jnp.float32(rows * devices)
     rounded = master.astype(BF16).reshape(local // LANES, LANES)
-    packed = tree_all_gather(rounded, order[::-1], nbits).reshape(-1)
+    packed = tree_all_gather(rounded, [o[::-1] for o in split_orders(order)], nbits).reshape(-1)
     (w_one, w_two, conv_w, conv_b, ln_g, ln_b, b_two, gamma, b_one), used = unpack(packed, width, hidden)
     cw8 = jnp.zeros((8, width), F32).at[:TAPS].set(conv_w.astype(F32))
     vec8 = jnp.concatenate(
@@ -310,21 +327,18 @@
     b1_8 = jnp.zeros((8, hidden), F32).at[0].set(b_one.astype(F32))
     block_out, input_grad, g_w1, g_w2, gcw, gvec, gb1 = fused_block(
         frames, counts, cotangent, w_one, w_two, cw8, vec8, b1_8)
+    small = jnp.concatenate(
+        [gcw[:TAPS].reshape(-1), gvec[0], gvec[1], gvec[2], gvec[3], gvec[4], gb1[0]]
+    )
     grad_full = jnp.concatenate(
         [
-            g_w1.reshape(-1),
-            g_w2.reshape(-1),
-            gcw[:TAPS].reshape(-1),
-            gvec[0],
-            gvec[1],
-            gvec[2],
-            gvec[3],
-            gvec[4],
-            gb1[0],
-            jnp.zeros((flat_size - used,), F32),
+            g_w1.reshape(-1, LANES),
+            g_w2.reshape(-1, LANES),
+            small.reshape(-1, LANES),
+            jnp.zeros(((flat_size - used) // LANES, LANES), F32),
         ]
-    ).reshape(flat_size // LANES, LANES)
-    grad_shard = tree_reduce_scatter(grad_full, order, nbits)
+    )
+    grad_shard = tree_reduce_scatter(grad_full, split_orders(order), nbits)
     disc_rows = jnp.sum((disc_grads * disc_grads).reshape(-1, LANES), axis=0, keepdims=True)
     own_rows = jnp.sum(grad_shard * grad_shard, axis=0, keepdims=True)
     squares = jnp.broadcast_to(own_rows + disc_rows, (8, LANES))

time: 371 us -> 337 us (0.908)
  waiting for transfers between devices: 126 us -> 80.2 us
  local copies, waits for them, and re-layouts: 51 us -> 64.6 us
  starting transfers between devices: 36.9 us -> 32.3 us
    ppermute x10 -> x20, waiting for transfers between devices: 113 us -> 64.9 us  [the longest x10 44.1 us: tree_reduce_scatter(): held[p] = keep + lax.ppermute(send, AXES, swap_perm(devices, bit))]
    concatenate x1 -> x3, local copies, waits for them, and re-layouts: 1.28 us -> 15.6 us  [the longest x1 14.4 us: body(): jnp.concatenate([g_w1.reshape(-1, LANES), g_w2.reshape(-1, LANES), small....]
    unnamed x22 -> x30, local copies, waits for them, and re-layouts: 16.8 us -> 2.71 us
    reshape x1 -> x3, local copies, waits for them, and re-layouts: 2.66 us -> 13.1 us  [the longest x1 5.98 us: tree_reduce_scatter(): shaped = full.reshape([2] * nbits + [rows, LANES])]
    another operation x5 -> x4, local copies, waits for them, and re-layouts: 11.4 us -> 5.44 us  [the longest x2 2.98 us: tree_all_gather(): jnp.stack([jnp.where(upper, other, held[p]), jnp.where(upper, held[p], ot...]
    ppermute x10 -> x20, starting transfers between devices: 33 us -> 31 us  [the longest x10 18.9 us: tree_reduce_scatter(): held[p] = keep + lax.ppermute(send, AXES, swap_perm(devices, bit))]
    slice x9 -> x8, local copies, waits for them, and re-layouts: 6.91 us -> 8.77 us  [unpack(): pieces.append(packed[start_at:start_at + entries].reshape(shape))]
    add x4 -> x10, other arithmetic: 6.09 us -> 7.52 us  [tree_reduce_scatter(): held[p] = keep + lax.ppermute(send, AXES, swap_perm(devices, bit))]
  transfers between devices with their start and end apart: 15 -> 25, of which waited for: 15 -> 23; matrix products, arithmetic and copies ran while one was open for 0% -> 5% of each run, Pallas kernels for 0% -> 0%
where the time goes in v3:
time: 337 us; the launch traced here: 331 us
  Pallas kernels  137 us (41%)
  waiting for transfers between devices  80.2 us (24%)
  local copies, waits for them, and re-layouts  64.6 us (19%)
  starting transfers between devices  32.3 us (10%)
  other arithmetic  14.2 us (4%)
    pallas_call x1, Pallas kernels, fused_block(): pl.pallas_call(kernel, grid_spec=grid_spec, out_shape=[jax.ShapeDtypeStru...  137 us
    ppermute x10, waiting for transfers between devices, tree_reduce_scatter(): held[p] = keep + lax.ppermute(send, AXES, swap_perm(devices, bit))  44.1 us
    ppermute x10, waiting for transfers between devices, tree_all_gather(): other = lax.ppermute(held[p], AXES, swap_perm(devices, bit))  20.8 us
    ppermute x10, starting transfers between devices, tree_reduce_scatter(): held[p] = keep + lax.ppermute(send, AXES, swap_perm(devices, bit))  18.9 us
    ppermute x5, waiting for transfers between devices, tree_all_sum(): value = value + lax.ppermute(value, AXES, swap_perm(devices, bit))  15.3 us
    concatenate x1, local copies, waits for them, and re-layouts, body(): jnp.concatenate([g_w1.reshape(-1, LANES), g_w2.reshape(-1, LANES), small....  14.4 us
    ppermute x10, starting transfers between devices, tree_all_gather(): other = lax.ppermute(held[p], AXES, swap_perm(devices, bit))  12.1 us
    slice x8, local copies, waits for them, and re-layouts, unpack(): pieces.append(packed[start_at:start_at + entries].reshape(shape))  8.77 us
  transfers between devices with their start and end apart: 25, of which 23 were waited for; matrix products, arithmetic and copies ran while one was open for 5% of the time, Pallas kernels for 0%

profile of v3, /device:TPU:0, one launch (start us, length us, event | category | flops | bytes accessed | tf_op | source)
XLA Modules:
  0.0 331.5 jit_solution(14575798654432783067)
XLA Ops:
  1.6 4.1 %collective-permute-start = (bf16[193,128]{1,0:T(8,128)(2,1)S(1)}, bf16[193,128]{1,0:T(8,128)(2,1)S(1)}, u32[]{:S(2)}, u32[]{:S(2)}) collective-permute-start(bf16[193,128]{1,0:T(8,128)(2,1)S(1)} %get-tuple-element.79), channel_id=1, source_target_pairs={{0,4},{1,5},{2,6},{3,7},{4,0},{5,1},{6,2},{7,3},{8,12},{9,13},{10,... | collective-permute-start | bytes 148232 | tf_op jit(solution)/shard_map/ppermute | solution.py:274
  13.1 3.1 collective-permute-done.6
  27.1 4.8 %collective-permute-done.8 = bf16[2,2,2,193,128]{4,3,2,1,0:T(8,128)(2,1)S(1)} collective-permute-done((bf16[2,2,2,193,128]{4,3,2,1,0:T(8,128)(2,1)S(1)}, bf16[2,2,2,193,128]{4,3,2,1,0:T(8,128)(2,1)S(1)}, u32[]{:S(2)}, u32[]{:S(2)}) %collective-permute-start.8) | collective-permute-done | bytes 395296 | tf_op jit(solution)/shard_map/ppermute | solution.py:274
  46.2 3.2 slice.124
  49.4 2.8 slice.146.w2_ref
  52.2 2.7 slice.145
  54.9 4.3 %reshape.132.w1_ref = bf16[512,1536]{1,0:T(8,128)(2,1)} reshape(bf16[786432]{0:T(1024)(128)(2,1)} %slice.145) | data formatting | bytes 3145728 | tf_op jit(solution)/shard_map/reshape | solution.py:236
  61.2 137.3 %shard_map.134 = (bf16[8,1024,512]{2,1,0:T(8,128)(2,1)}, f32[8,1024,512]{2,1,0:T(8,128)}, f32[512,1536]{1,0:T(8,128)}, f32[1536,512]{1,0:T(8,128)}, f32[8,512]{1...) custom-call(s32[8]{0:T(128)} %counts_ref.1, bf16[8,1024,512]{2,1,0:T(8,128)(2,1)} %fr_ref.1, ...), custom_call_target="tpu_custom_call" | custom-call | flops 77309411328 | bytes 46137344 | tf_op jit(solution)/shard_map/pallas_call | solution.py:210
  198.4 2.7 reshape.134
  201.1 4.4 %reshape.135 = f32[6144,128]{1,0:T(8,128)} reshape(f32[1536,512]{1,0:T(8,128)} %get-tuple-element.42) | data formatting | bytes 6291456 | tf_op jit(solution)/shard_map/reshape | solution.py:336
  206.5 14.4 %concatenate.25 = f32[12352,128]{1,0:T(8,128)} concatenate(f32[6144,128]{1,0:T(8,128)S(1)} %reshape.134, f32[6144,128]{1,0:T(8,128)} %reshape.135, f32[60,128]{1,0:T(8,128)S(1)} %bitcast.118, f32[4,128]{1,0:T(4,128)S(1)} %broadcast_in_dim.4), dimensions={0} | concatenate | bytes 12648448 | tf_op jit(solution)/shard_map/concatenate | solution.py:333
  220.9 6.0 %reshape.138 = f32[2,2,2,2,2,386,128]{6,5,4,3,2,1,0:T(8,128)} reshape(f32[12352,128]{1,0:T(8,128)} %concatenate.25) | data formatting | bytes 12648448 | tf_op jit(solution)/shard_map/reshape | solution.py:290
  226.9 3.4 %fusion.4 = (f32[2,2,2,2,2,193,128]{6,5,4,3,2,1,0:T(8,128)S(1)}, f32[2,2,2,2,2,193,128]{6,5,4,3,2,1,0:T(8,128)S(1)}) fusion(f32[2,2,2,2,2,386,128]{6,5,4,3,2,1,0:T(8,128)} %reshape.138), kind=kLoop, calls=%fused_computation.75 | loop fusion | bytes 12648448 | tf_op jit(solution)/shard_map/slice | solution.py:291
  234.0 5.5 %collective-permute-start.15 = (f32[2,2,2,2,193,128]{5,3,4,2,1,0:T(2,128)}, f32[2,2,2,2,193,128]{5,3,4,2,1,0:T(2,128)}, u32[]{:S(2)}, u32[]{:S(2)}) collective-permute-start(f32[2,2,2,2,193,128]{5,3,4,2,1,0:T(2,128)} %copy.98), channel_id=1, source_target_pairs={{0,1},{1,0},{2,3},{3,2},{4,5},{5,4},{6,7},{7,6},{8,9},{9,8},{10,11... | collective-permute-start | bytes 4743176 | tf_op jit(solution)/shard_map/ppermute | solution.py:300
  246.5 12.3 %collective-permute-start.16 = (f32[2,2,2,193,128]{4,2,3,1,0:T(2,128)}, f32[2,2,2,193,128]{4,2,3,1,0:T(2,128)}, u32[]{:S(2)}, u32[]{:S(2)}) collective-permute-start(f32[2,2,2,193,128]{4,2,3,1,0:T(2,128)} %copy.100), channel_id=1, source_target_pairs={{0,16},{1,17},{2,18},{3,19},{4,20},{5,21},{6,22},{7,23},{8,24},{9,... | collective-permute-start | bytes 2371592 | tf_op jit(solution)/shard_map/ppermute | solution.py:300
  262.0 15.2 %collective-permute-done.16 = f32[2,2,2,193,128]{4,2,3,1,0:T(2,128)} collective-permute-done((f32[2,2,2,193,128]{4,2,3,1,0:T(2,128)}, f32[2,2,2,193,128]{4,2,3,1,0:T(2,128)}, u32[]{:S(2)}, u32[]{:S(2)}) %collective-permute-start.16) | collective-permute-done | bytes 790560 | tf_op jit(solution)/shard_map/ppermute | solution.py:300
  283.5 7.5 %collective-permute-done.17 = f32[2,2,193,128]{3,2,1,0:T(8,128)} collective-permute-done((f32[2,2,193,128]{3,2,1,0:T(8,128)}, f32[2,2,193,128]{3,2,1,0:T(8,128)}, u32[]{:S(2)}, u32[]{:S(2)}) %collective-permute-start.17) | collective-permute-done | bytes 395296 | tf_op jit(solution)/shard_map/ppermute | solution.py:300
  294.3 5.8 %collective-permute-done.18 = f32[2,193,128]{2,1,0:T(8,128)S(1)} collective-permute-done((f32[2,193,128]{2,1,0:T(8,128)S(1)}, f32[2,193,128]{2,1,0:T(8,128)S(1)}, u32[]{:S(2)}, u32[]{:S(2)}) %collective-permute-start.18) | collective-permute-done | bytes 197664 | tf_op jit(solution)/shard_map/ppermute | solution.py:300
  300.3 3.2 collective-permute-done.13
  303.7 5.9 %collective-permute-done.19 = f32[193,128]{1,0:T(8,128)S(1)} collective-permute-done((f32[193,128]{1,0:T(8,128)S(1)}, f32[193,128]{1,0:T(8,128)S(1)}, u32[]{:S(2)}, u32[]{:S(2)}) %collective-permute-start.19) | collective-permute-done | bytes 98848 | tf_op jit(solution)/shard_map/ppermute | solution.py:300
  310.9 4.5 %collective-permute-done.20 = f32[8,128]{1,0:T(8,128)S(1)} collective-permute-done((f32[8,128]{1,0:T(8,128)S(1)}, f32[8,128]{1,0:T(8,128)S(1)}, u32[]{:S(2)}, u32[]{:S(2)}) %collective-permute-start.20) | collective-permute-done | bytes 4128 | tf_op jit(solution)/shard_map/ppermute | solution.py:308
  315.4 3.6 %collective-permute-done.21 = f32[8,128]{1,0:T(8,128)S(1)} collective-permute-done((f32[8,128]{1,0:T(8,128)S(1)}, f32[8,128]{1,0:T(8,128)S(1)}, u32[]{:S(2)}, u32[]{:S(2)}) %collective-permute-start.21) | collective-permute-done | bytes 4128 | tf_op jit(solution)/shard_map/ppermute | solution.py:308
  320.0 2.7 collective-permute-done.22
  322.9 3.4 %collective-permute-done.23 = f32[8,128]{1,0:T(8,128)S(1)} collective-permute-done((f32[8,128]{1,0:T(8,128)S(1)}, f32[8,128]{1,0:T(8,128)S(1)}, u32[]{:S(2)}, u32[]{:S(2)}) %collective-permute-start.23) | collective-permute-done | bytes 4128 | tf_op jit(solution)/shard_map/ppermute | solution.py:308
  (150 shorter events, 65.5 us)
Async XLA Ops:
  1.6 6.8 %collective-permute-start = (bf16[193,128]{1,0:T(8,128)(2,1)S(1)}, bf16[193,128]{1,0:T(8,128)(2,1)S(1)}, u32[]{:S(2)}, u32[]{:S(2)}) collective-permute-start(bf16[193,128]{1,0:T(8,128)(2,1)S(1)} %get-tuple-element.79), channel_id=1, source_target_pairs={{0,4},{1,5},{2,6},{3,7},{4,0},{5,1},{6,2},{7,3},{8,12},{9,13},{10,... | collective-permute-start | bytes 148232 | tf_op jit(solution)/shard_map/ppermute | solution.py:274
  5.7 5.2 %collective-permute-start.5 = (bf16[193,128]{1,0:T(8,128)(2,1)S(1)}, bf16[193,128]{1,0:T(8,128)(2,1)S(1)}, u32[]{:S(2)}, u32[]{:S(2)}) collective-permute-start(bf16[193,128]{1,0:T(8,128)(2,1)S(1)} %get-tuple-element.80), channel_id=1, source_target_pairs={{0,4},{1,5},{2,6},{3,7},{4,0},{5,1},{6,2},{7,3},{8,12},{9,13},{10,... | collective-permute-start | bytes 148232 | tf_op jit(solution)/shard_map/ppermute | solution.py:274
  11.0 5.3 %collective-permute-start.6 = (bf16[2,193,128]{2,1,0:T(8,128)(2,1)S(1)}, bf16[2,193,128]{2,1,0:T(8,128)(2,1)S(1)}, u32[]{:S(2)}, u32[]{:S(2)}) collective-permute-start(bf16[2,193,128]{2,1,0:T(8,128)(2,1)S(1)} %pad_maximum_fusion.9), channel_id=1, source_target_pairs={{0,2},{1,3},{2,0},{3,1},{4,6},{5,7},{6,4},{7,5},{8,10},{9,11},{10,... | collective-permute-start | bytes 296456 | tf_op jit(solution)/shard_map/ppermute | solution.py:274
  12.5 5.4 %collective-permute-start.1 = (bf16[2,193,128]{2,1,0:T(8,128)(2,1)S(1)}, bf16[2,193,128]{2,1,0:T(8,128)(2,1)S(1)}, u32[]{:S(2)}, u32[]{:S(2)}) collective-permute-start(bf16[2,193,128]{2,1,0:T(8,128)(2,1)S(1)} %pad_maximum_fusion.8), channel_id=1, source_target_pairs={{0,2},{1,3},{2,0},{3,1},{4,6},{5,7},{6,4},{7,5},{8,10},{9,11},{10,... | collective-permute-start | bytes 296456 | tf_op jit(solution)/shard_map/ppermute | solution.py:274
  16.3 5.8 %collective-permute-start.7 = (bf16[2,2,193,128]{3,2,1,0:T(8,128)(2,1)S(1)}, bf16[2,2,193,128]{3,2,1,0:T(8,128)(2,1)S(1)}, u32[]{:S(2)}, u32[]{:S(2)}) collective-permute-start(bf16[2,2,193,128]{3,2,1,0:T(8,128)(2,1)S(1)} %pad_maximum_fusion.6), channel_id=1, source_target_pairs={{0,8},{1,9},{2,10},{3,11},{4,12},{5,13},{6,14},{7,15},{8,0},{9,1},... | collective-permute-start | bytes 592904 | tf_op jit(solution)/shard_map/ppermute | solution.py:274
  17.9 8.0 %collective-permute-start.2 = (bf16[2,2,193,128]{3,2,1,0:T(8,128)(2,1)S(1)}, bf16[2,2,193,128]{3,2,1,0:T(8,128)(2,1)S(1)}, u32[]{:S(2)}, u32[]{:S(2)}) collective-permute-start(bf16[2,2,193,128]{3,2,1,0:T(8,128)(2,1)S(1)} %pad_maximum_fusion.5), channel_id=1, source_target_pairs={{0,16},{1,17},{2,18},{3,19},{4,20},{5,21},{6,22},{7,23},{8,24},{9,... | collective-permute-start | bytes 592904 | tf_op jit(solution)/shard_map/ppermute | solution.py:274
  22.2 9.7 %collective-permute-start.8 = (bf16[2,2,2,193,128]{4,3,2,1,0:T(8,128)(2,1)S(1)}, bf16[2,2,2,193,128]{4,3,2,1,0:T(8,128)(2,1)S(1)}, u32[]{:S(2)}, u32[]{:S(2)}) collective-permute-start(bf16[2,2,2,193,128]{4,3,2,1,0:T(8,128)(2,1)S(1)} %pad_maximum_fusion.4), channel_id=1, source_target_pairs={{0,16},{1,17},{2,18},{3,19},{4,20},{5,21},{6,22},{7,23},{8,24},{9,... | collective-permute-start | bytes 1185800 | tf_op jit(solution)/shard_map/ppermute | solution.py:274
  26.0 8.0 %collective-permute-start.3 = (bf16[2,2,2,193,128]{4,3,2,1,0:T(8,128)(2,1)S(1)}, bf16[2,2,2,193,128]{4,3,2,1,0:T(8,128)(2,1)S(1)}, u32[]{:S(2)}, u32[]{:S(2)}) collective-permute-start(bf16[2,2,2,193,128]{4,3,2,1,0:T(8,128)(2,1)S(1)} %pad_maximum_fusion.3), channel_id=1, source_target_pairs={{0,8},{1,9},{2,10},{3,11},{4,12},{5,13},{6,14},{7,15},{8,0},{9,1},... | collective-permute-start | bytes 1185800 | tf_op jit(solution)/shard_map/ppermute | solution.py:274
  33.6 2.5 collective-permute-start.9
  35.7 2.5 collective-permute-start.4
  234.0 8.9 %collective-permute-start.15 = (f32[2,2,2,2,193,128]{5,3,4,2,1,0:T(2,128)}, f32[2,2,2,2,193,128]{5,3,4,2,1,0:T(2,128)}, u32[]{:S(2)}, u32[]{:S(2)}) collective-permute-start(f32[2,2,2,2,193,128]{5,3,4,2,1,0:T(2,128)} %copy.98), channel_id=1, source_target_pairs={{0,1},{1,0},{2,3},{3,2},{4,5},{5,4},{6,7},{7,6},{8,9},{9,8},{10,11... | collective-permute-start | bytes 4743176 | tf_op jit(solution)/shard_map/ppermute | solution.py:300
  241.6 17.2 %collective-permute-start.10 = (f32[2,2,2,2,193,128]{5,3,4,2,1,0:T(2,128)}, f32[2,2,2,2,193,128]{5,3,4,2,1,0:T(2,128)}, u32[]{:S(2)}, u32[]{:S(2)}) collective-permute-start(f32[2,2,2,2,193,128]{5,3,4,2,1,0:T(2,128)} %copy.94), channel_id=1, source_target_pairs={{0,1},{1,0},{2,3},{3,2},{4,5},{5,4},{6,7},{7,6},{8,9},{9,8},{10,11... | collective-permute-start | bytes 4743176 | tf_op jit(solution)/shard_map/ppermute | solution.py:300
  246.5 30.7 %collective-permute-start.16 = (f32[2,2,2,193,128]{4,2,3,1,0:T(2,128)}, f32[2,2,2,193,128]{4,2,3,1,0:T(2,128)}, u32[]{:S(2)}, u32[]{:S(2)}) collective-permute-start(f32[2,2,2,193,128]{4,2,3,1,0:T(2,128)} %copy.100), channel_id=1, source_target_pairs={{0,16},{1,17},{2,18},{3,19},{4,20},{5,21},{6,22},{7,23},{8,24},{9,... | collective-permute-start | bytes 2371592 | tf_op jit(solution)/shard_map/ppermute | solution.py:300
  261.9 19.9 %collective-permute-start.11 = (f32[2,2,2,193,128]{4,2,3,1,0:T(2,128)S(1)}, f32[2,2,2,193,128]{4,2,3,1,0:T(2,128)}, u32[]{:S(2)}, u32[]{:S(2)}) collective-permute-start(f32[2,2,2,193,128]{4,2,3,1,0:T(2,128)S(1)} %copy.96), channel_id=1, source_target_pairs={{0,8},{1,9},{2,10},{3,11},{4,12},{5,13},{6,14},{7,15},{8,0},{9,1},... | collective-permute-start | bytes 2371592 | tf_op jit(solution)/shard_map/ppermute | solution.py:300
  279.5 11.5 %collective-permute-start.17 = (f32[2,2,193,128]{3,2,1,0:T(8,128)}, f32[2,2,193,128]{3,2,1,0:T(8,128)}, u32[]{:S(2)}, u32[]{:S(2)}) collective-permute-start(f32[2,2,193,128]{3,2,1,0:T(8,128)} %dynamic-slice_bitcast_fusion.4), channel_id=1, source_target_pairs={{0,8},{1,9},{2,10},{3,11},{4,12},{5,13},{6,14},{7,15},{8,0},{9,1},... | collective-permute-start | bytes 1185800 | tf_op jit(solution)/shard_map/ppermute | solution.py:300
  283.1 10.7 %collective-permute-start.12 = (f32[2,2,193,128]{3,2,1,0:T(8,128)S(1)}, f32[2,2,193,128]{3,2,1,0:T(8,128)S(1)}, u32[]{:S(2)}, u32[]{:S(2)}) collective-permute-start(f32[2,2,193,128]{3,2,1,0:T(8,128)S(1)} %dynamic-slice_bitcast_fusion.5), channel_id=1, source_target_pairs={{0,16},{1,17},{2,18},{3,19},{4,20},{5,21},{6,22},{7,23},{8,24},{9,... | collective-permute-start | bytes 1185800 | tf_op jit(solution)/shard_map/ppermute | solution.py:300
  292.1 8.1 %collective-permute-start.18 = (f32[2,193,128]{2,1,0:T(8,128)S(1)}, f32[2,193,128]{2,1,0:T(8,128)S(1)}, u32[]{:S(2)}, u32[]{:S(2)}) collective-permute-start(f32[2,193,128]{2,1,0:T(8,128)S(1)} %dynamic-slice_bitcast_fusion.6), channel_id=1, source_target_pairs={{0,2},{1,3},{2,0},{3,1},{4,6},{5,7},{6,4},{7,5},{8,10},{9,11},{10,... | collective-permute-start | bytes 592904 | tf_op jit(solution)/shard_map/ppermute | solution.py:300
  293.9 9.6 %collective-permute-start.13 = (f32[2,193,128]{2,1,0:T(8,128)S(1)}, f32[2,193,128]{2,1,0:T(8,128)S(1)}, u32[]{:S(2)}, u32[]{:S(2)}) collective-permute-start(f32[2,193,128]{2,1,0:T(8,128)S(1)} %dynamic-slice_bitcast_fusion.7), channel_id=1, source_target_pairs={{0,2},{1,3},{2,0},{3,1},{4,6},{5,7},{6,4},{7,5},{8,10},{9,11},{10,... | collective-permute-start | bytes 592904 | tf_op jit(solution)/shard_map/ppermute | solution.py:300
  300.2 9.4 %collective-permute-start.19 = (f32[193,128]{1,0:T(8,128)S(1)}, f32[193,128]{1,0:T(8,128)S(1)}, u32[]{:S(2)}, u32[]{:S(2)}) collective-permute-start(f32[193,128]{1,0:T(8,128)S(1)} %dynamic-slice_bitcast_fusion.8), channel_id=1, source_target_pairs={{0,4},{1,5},{2,6},{3,7},{4,0},{5,1},{6,2},{7,3},{8,12},{9,13},{10,... | collective-permute-start | bytes 296456 | tf_op jit(solution)/shard_map/ppermute | solution.py:300
  303.6 7.1 %collective-permute-start.14 = (f32[193,128]{1,0:T(8,128)S(1)}, f32[193,128]{1,0:T(8,128)S(1)}, u32[]{:S(2)}, u32[]{:S(2)}) collective-permute-start(f32[193,128]{1,0:T(8,128)S(1)} %dynamic-slice_bitcast_fusion.9), channel_id=1, source_target_pairs={{0,4},{1,5},{2,6},{3,7},{4,0},{5,1},{6,2},{7,3},{8,12},{9,13},{10,... | collective-permute-start | bytes 296456 | tf_op jit(solution)/shard_map/ppermute | solution.py:300
  310.8 4.6 %collective-permute-start.20 = (f32[8,128]{1,0:T(8,128)S(1)}, f32[8,128]{1,0:T(8,128)S(1)}, u32[]{:S(2)}, u32[]{:S(2)}) collective-permute-start(f32[8,128]{1,0:T(8,128)S(1)} %broadcast_in_dim.5), channel_id=1, source_target_pairs={{0,4},{1,5},{2,6},{3,7},{4,0},{5,1},{6,2},{7,3},{8,12},{9,13},{10,... | collective-permute-start | bytes 12296 | tf_op jit(solution)/shard_map/ppermute | solution.py:308
  315.4 3.6 %collective-permute-start.21 = (f32[8,128]{1,0:T(8,128)S(1)}, f32[8,128]{1,0:T(8,128)S(1)}, u32[]{:S(2)}, u32[]{:S(2)}) collective-permute-start(f32[8,128]{1,0:T(8,128)S(1)} %broadcast_add_fusion), channel_id=1, source_target_pairs={{0,2},{1,3},{2,0},{3,1},{4,6},{5,7},{6,4},{7,5},{8,10},{9,11},{10,... | collective-permute-start | bytes 12296 | tf_op jit(solution)/shard_map/ppermute | solution.py:308
  319.0 3.6 %collective-permute-start.22 = (f32[8,128]{1,0:T(8,128)S(1)}, f32[8,128]{1,0:T(8,128)S(1)}, u32[]{:S(2)}, u32[]{:S(2)}) collective-permute-start(f32[8,128]{1,0:T(8,128)S(1)} %fusion.7), channel_id=1, source_target_pairs={{0,16},{1,17},{2,18},{3,19},{4,20},{5,21},{6,22},{7,23},{8,24},{9,... | collective-permute-start | bytes 12296 | tf_op jit(solution)/shard_map/ppermute | solution.py:308
  322.6 3.6 %collective-permute-start.23 = (f32[8,128]{1,0:T(8,128)S(1)}, f32[8,128]{1,0:T(8,128)S(1)}, u32[]{:S(2)}, u32[]{:S(2)}) collective-permute-start(f32[8,128]{1,0:T(8,128)S(1)} %add.154), channel_id=1, source_target_pairs={{0,8},{1,9},{2,10},{3,11},{4,12},{5,13},{6,14},{7,15},{8,0},{9,1},... | collective-permute-start | bytes 12296 | tf_op jit(solution)/shard_map/ppermute | solution.py:308
  (15 other events, 172.9 us)

commit v4 on v3

--- a/solution.py
+++ b/solution.py
@@ -13,6 +13,7 @@
 TAPS = 7
 HALF = TAPS // 2
 PAD = 8
+LANE = 128
 
 
 def tdot(x, y):
@@ -25,13 +26,14 @@
 
 def block_kernel(length, width, hidden, rows):
     nblk = length // rows
+    quads = width // LANE
     inv_w = 1.0 / width
     sqrt_half = math.sqrt(0.5)
     inv_sqrt_2pi = 1.0 / math.sqrt(2.0 * math.pi)
 
     def kernel(counts_ref, fr_ref, cot_ref, w1_ref, w2_ref, cw_ref, vec_ref, b1_ref,
                bo_ref, ig_ref, gw1_hbm, gw2_hbm, gcw_ref, gvec_ref, gb1_ref,
-               xpad, xhat_s, rstd_s, a_s, da_s, dpad, gw1_s, gw2_s, sems):
+               xq, xhat_s, rstd_s, a_s, da_s, dq, gw1_s, gw2_s, sems):
         clip = pl.program_id(0)
         count = counts_ref[clip]
 
@@ -42,10 +44,10 @@
             gcw_ref[...] = jnp.zeros_like(gcw_ref)
             gvec_ref[...] = jnp.zeros_like(gvec_ref)
             gb1_ref[...] = jnp.zeros_like(gb1_ref)
-            xpad[0:PAD, :] = jnp.zeros((PAD, width), F32)
-            xpad[PAD + length:, :] = jnp.zeros((PAD, width), F32)
-            dpad[0:PAD, :] = jnp.zeros((PAD, width), F32)
-            dpad[PAD + length:, :] = jnp.zeros((PAD, width), F32)
+            xq[0:PAD * quads, :] = jnp.zeros((PAD * quads, LANE), F32)
+            xq[(PAD + length) * quads:, :] = jnp.zeros((PAD * quads, LANE), F32)
+            dq[0:PAD * quads, :] = jnp.zeros((PAD * quads, LANE), F32)
+            dq[(PAD + length) * quads:, :] = jnp.zeros((PAD * quads, LANE), F32)
 
         cw = cw_ref[...]
         conv_b = vec_ref[0:1, :]
@@ -56,7 +58,13 @@
         b_one = b1_ref[0:1, :]
 
         all_rows = lax.broadcasted_iota(jnp.int32, (length, 1), 0)
-        xpad[PAD:PAD + length, :] = jnp.where(all_rows < count, fr_ref[0].astype(F32), 0.0)
+        xm_all = jnp.where(all_rows < count, fr_ref[0].astype(F32), 0.0)
+        for q in range(quads):
+            xq[pl.ds(PAD * quads + q, length, stride=quads), :] = xm_all[:, q * LANE:(q + 1) * LANE]
+
+        def taps_of(buf, start):
+            return jnp.concatenate(
+                [buf[pl.ds(start * quads + q, rows, stride=quads), :] for q in range(quads)], axis=1)
 
         for b in range(nblk):
             r0 = b * rows
@@ -64,9 +72,9 @@
             @pl.when(r0 < count)
             def _fwd_block():
                 base = PAD + r0 - HALF
-                conv = conv_b + cw[0:1, :] * xpad[base:base + rows, :]
+                conv = conv_b + cw[0:1, :] * taps_of(xq, base)
                 for k in range(1, TAPS):
-                    conv = conv + cw[k:k + 1, :] * xpad[base + k:base + k + rows, :]
+                    conv = conv + cw[k:k + 1, :] * taps_of(xq, base + k)
                 centre = jnp.sum(conv, axis=-1, keepdims=True) * inv_w
                 shifted = conv - centre
                 spread = jnp.sum(shifted * shifted, axis=-1, keepdims=True) * inv_w
@@ -110,9 +118,9 @@
         def dxm_block(b):
             r0 = b * rows
             base = PAD + r0 + HALF
-            dxm = cw[0:1, :] * dpad[base:base + rows, :]
+            dxm = cw[0:1, :] * taps_of(dq, base)
             for k in range(1, TAPS):
-                dxm = dxm + cw[k:k + 1, :] * dpad[base - k:base - k + rows, :]
+                dxm = dxm + cw[k:k + 1, :] * taps_of(dq, base - k)
             live = (r0 + lax.broadcasted_iota(jnp.int32, (rows, 1), 0)) < count
             cot = cot_ref[0, r0:r0 + rows, :].astype(F32)
             ig_ref[0, r0:r0 + rows, :] = jnp.where(live, cot + dxm, 0.0)
@@ -130,13 +138,14 @@
                 m1 = jnp.sum(dn, axis=-1, keepdims=True) * inv_w
                 m2 = jnp.sum(dn * xhat, axis=-1, keepdims=True) * inv_w
                 dconv = jnp.where(live, rstd * (dn - m1 - xhat * m2), 0.0)
-                dpad[PAD + r0:PAD + r0 + rows, :] = dconv
+                for q in range(quads):
+                    dq[pl.ds((PAD + r0) * quads + q, rows, stride=quads), :] = dconv[:, q * LANE:(q + 1) * LANE]
                 part = [jnp.sum(dconv, axis=0, keepdims=True),
                         jnp.sum(da * xhat, axis=0, keepdims=True),
                         jnp.sum(da, axis=0, keepdims=True)]
                 base = PAD + r0 - HALF
                 for k in range(TAPS):
-                    part.append(jnp.sum(dconv * xpad[base + k:base + k + rows, :], axis=0, keepdims=True))
+                    part.append(jnp.sum(dconv * taps_of(xq, base + k), axis=0, keepdims=True))
                 return part
 
             active = r0 < count
@@ -144,7 +153,7 @@
 
             @pl.when(jnp.logical_not(active))
             def _idle():
-                dpad[PAD + r0:PAD + r0 + rows, :] = jnp.zeros((rows, width), F32)
+                dq[(PAD + r0) * quads:(PAD + r0 + rows) * quads, :] = jnp.zeros((rows * quads, LANE), F32)
                 ig_ref[0, r0:r0 + rows, :] = jnp.zeros((rows, width), F32)
 
             sums = [s + p for s, p in zip(sums, part)]
@@ -193,12 +202,12 @@
                    pl.BlockSpec(memory_space=pl.ANY), pl.BlockSpec(memory_space=pl.ANY),
                    fixed((8, width)), fixed((8, width)), fixed((8, hidden))],
         scratch_shapes=[
-            pltpu.VMEM((length + 2 * PAD, width), F32),
+            pltpu.VMEM(((length + 2 * PAD) * (width // LANE), LANE), F32),
             pltpu.VMEM((length, width), F32),
             pltpu.VMEM((length, 1), F32),
             pltpu.VMEM((length, width), BF16),
             pltpu.VMEM((length, width), F32),
-            pltpu.VMEM((length + 2 * PAD, width), F32),
+            pltpu.VMEM(((length + 2 * PAD) * (width // LANE), LANE), F32),
             pltpu.VMEM((width, hidden), F32),
             pltpu.VMEM((hidden, width), F32),
             pltpu.SemaphoreType.DMA((2,)),

time: 337 us -> 309 us (0.917); the launches traced: 331 us -> 312 us
  Pallas kernels: 137 us -> 99.5 us
  starting transfers between devices: 32.3 us -> 59.9 us
  waiting for transfers between devices: 80.2 us -> 71.3 us
    pallas_call x1, Pallas kernels: 137 us -> 99.5 us  [fused_block(): pl.pallas_call(kernel, grid_spec=grid_spec, out_shape=[jax.ShapeDtypeStru...]
    ppermute x10, starting transfers between devices: 18.9 us -> 44.1 us  [tree_reduce_scatter(): held[p] = keep + lax.ppermute(send, AXES, swap_perm(devices, bit))]
    ppermute x10, waiting for transfers between devices: 44.1 us -> 37.5 us  [tree_reduce_scatter(): held[p] = keep + lax.ppermute(send, AXES, swap_perm(devices, bit))]
  transfers between devices with their start and end apart: 25 -> 25, of which waited for: 23 -> 22; matrix products, arithmetic and copies ran while one was open for 5% -> 5% of each run, Pallas kernels for 0% -> 0%
where the time goes in v4:
time: 309 us; the launch traced here: 312 us
  Pallas kernels  99.5 us (32%)
  waiting for transfers between devices  71.3 us (23%)
  local copies, waits for them, and re-layouts  64.6 us (21%)
  starting transfers between devices  59.9 us (19%)
  other arithmetic  14.2 us (5%)
    pallas_call x1, Pallas kernels, fused_block(): pl.pallas_call(kernel, grid_spec=grid_spec, out_shape=[jax.ShapeDtypeStru...  99.5 us
    ppermute x10, starting transfers between devices, tree_reduce_scatter(): held[p] = keep + lax.ppermute(send, AXES, swap_perm(devices, bit))  44.1 us
    ppermute x10, waiting for transfers between devices, tree_reduce_scatter(): held[p] = keep + lax.ppermute(send, AXES, swap_perm(devices, bit))  37.5 us
    ppermute x10, waiting for transfers between devices, tree_all_gather(): other = lax.ppermute(held[p], AXES, swap_perm(devices, bit))  20.8 us
    concatenate x1, local copies, waits for them, and re-layouts, body(): jnp.concatenate([g_w1.reshape(-1, LANES), g_w2.reshape(-1, LANES), small....  14.4 us
    ppermute x5, waiting for transfers between devices, tree_all_sum(): value = value + lax.ppermute(value, AXES, swap_perm(devices, bit))  13 us
    ppermute x10, starting transfers between devices, tree_all_gather(): other = lax.ppermute(held[p], AXES, swap_perm(devices, bit))  12.1 us
    slice x8, local copies, waits for them, and re-layouts, unpack(): pieces.append(packed[start_at:start_at + entries].reshape(shape))  8.77 us
  transfers between devices with their start and end apart: 25, of which 22 were waited for; matrix products, arithmetic and copies ran while one was open for 5% of the time, Pallas kernels for 0%

profile of v4, /device:TPU:0, one launch (start us, length us, event | category | flops | bytes accessed | tf_op | source)
XLA Modules:
  0.0 312.4 jit_solution(6580053447447951474)
XLA Ops:
  1.6 4.1 %collective-permute-start = (bf16[193,128]{1,0:T(8,128)(2,1)S(1)}, bf16[193,128]{1,0:T(8,128)(2,1)S(1)}, u32[]{:S(2)}, u32[]{:S(2)}) collective-permute-start(bf16[193,128]{1,0:T(8,128)(2,1)S(1)} %get-tuple-element.79), channel_id=1, source_target_pairs={{0,4},{1,5},{2,6},{3,7},{4,0},{5,1},{6,2},{7,3},{8,12},{9,13},{10,... | collective-permute-start | bytes 148232 | tf_op jit(solution)/shard_map/ppermute | solution.py:283
  13.1 3.1 %collective-permute-done.6 = bf16[2,193,128]{2,1,0:T(8,128)(2,1)S(1)} collective-permute-done((bf16[2,193,128]{2,1,0:T(8,128)(2,1)S(1)}, bf16[2,193,128]{2,1,0:T(8,128)(2,1)S(1)}, u32[]{:S(2)}, u32[]{:S(2)}) %collective-permute-start.6) | collective-permute-done | bytes 98848 | tf_op jit(solution)/shard_map/ppermute | solution.py:283
  27.1 4.8 %collective-permute-done.8 = bf16[2,2,2,193,128]{4,3,2,1,0:T(8,128)(2,1)S(1)} collective-permute-done((bf16[2,2,2,193,128]{4,3,2,1,0:T(8,128)(2,1)S(1)}, bf16[2,2,2,193,128]{4,3,2,1,0:T(8,128)(2,1)S(1)}, u32[]{:S(2)}, u32[]{:S(2)}) %collective-permute-start.8) | collective-permute-done | bytes 395296 | tf_op jit(solution)/shard_map/ppermute | solution.py:283
  46.2 3.2 %slice.124 = bf16[3088,512]{1,0:T(8,128)(2,1)} reshape(bf16[32,386,128]{2,1,0:T(8,128)(2,1)S(1)} %copy.92) | data formatting | bytes 6324224 | tf_op jit(solution)/shard_map/slice | solution.py:245
  49.4 2.8 slice.146.w2_ref
  52.2 2.7 slice.145
  54.9 4.3 %reshape.132.w1_ref = bf16[512,1536]{1,0:T(8,128)(2,1)} reshape(bf16[786432]{0:T(1024)(128)(2,1)} %slice.145) | data formatting | bytes 3145728 | tf_op jit(solution)/shard_map/reshape | solution.py:245
  61.2 99.5 %shard_map.134 = (bf16[8,1024,512]{2,1,0:T(8,128)(2,1)}, f32[8,1024,512]{2,1,0:T(8,128)}, f32[512,1536]{1,0:T(8,128)}, f32[1536,512]{1,0:T(8,128)}, f32[8,512]{1...) custom-call(s32[8]{0:T(128)} %counts_ref.1, bf16[8,1024,512]{2,1,0:T(8,128)(2,1)} %fr_ref.1, ...), custom_call_target="tpu_custom_call" | custom-call | flops 77309411328 | bytes 46137344 | tf_op jit(solution)/shard_map/pallas_call | solution.py:219
  160.7 2.7 reshape.134
  163.4 4.4 %reshape.135 = f32[6144,128]{1,0:T(8,128)} reshape(f32[1536,512]{1,0:T(8,128)} %get-tuple-element.42) | data formatting | bytes 6291456 | tf_op jit(solution)/shard_map/reshape | solution.py:345
  168.8 14.4 %concatenate.25 = f32[12352,128]{1,0:T(8,128)} concatenate(f32[6144,128]{1,0:T(8,128)S(1)} %reshape.134, f32[6144,128]{1,0:T(8,128)} %reshape.135, f32[60,128]{1,0:T(8,128)S(1)} %bitcast.118, f32[4,128]{1,0:T(4,128)S(1)} %broadcast_in_dim.4), dimensions={0} | concatenate | bytes 12648448 | tf_op jit(solution)/shard_map/concatenate | solution.py:342
  183.2 6.0 %reshape.138 = f32[2,2,2,2,2,386,128]{6,5,4,3,2,1,0:T(8,128)} reshape(f32[12352,128]{1,0:T(8,128)} %concatenate.25) | data formatting | bytes 12648448 | tf_op jit(solution)/shard_map/reshape | solution.py:299
  189.2 3.4 %fusion.4 = (f32[2,2,2,2,2,193,128]{6,5,4,3,2,1,0:T(8,128)S(1)}, f32[2,2,2,2,2,193,128]{6,5,4,3,2,1,0:T(8,128)S(1)}) fusion(f32[2,2,2,2,2,386,128]{6,5,4,3,2,1,0:T(8,128)} %reshape.138), kind=kLoop, calls=%fused_computation.75 | loop fusion | bytes 12648448 | tf_op jit(solution)/shard_map/slice | solution.py:300
  196.2 25.5 %collective-permute-start.15 = (f32[2,2,2,2,193,128]{5,3,4,2,1,0:T(2,128)}, f32[2,2,2,2,193,128]{5,3,4,2,1,0:T(2,128)}, u32[]{:S(2)}, u32[]{:S(2)}) collective-permute-start(f32[2,2,2,2,193,128]{5,3,4,2,1,0:T(2,128)} %copy.98), channel_id=1, source_target_pairs={{0,1},{1,0},{2,3},{3,2},{4,5},{5,4},{6,7},{7,6},{8,9},{9,8},{10,11... | collective-permute-start | bytes 4743176 | tf_op jit(solution)/shard_map/ppermute | solution.py:309
  228.8 10.2 %collective-permute-start.16 = (f32[2,2,2,193,128]{4,2,3,1,0:T(2,128)}, f32[2,2,2,193,128]{4,2,3,1,0:T(2,128)}, u32[]{:S(2)}, u32[]{:S(2)}) collective-permute-start(f32[2,2,2,193,128]{4,2,3,1,0:T(2,128)} %copy.100), channel_id=1, source_target_pairs={{0,16},{1,17},{2,18},{3,19},{4,20},{5,21},{6,22},{7,23},{8,24},{9,... | collective-permute-start | bytes 2371592 | tf_op jit(solution)/shard_map/ppermute | solution.py:309
  242.3 15.0 %collective-permute-done.16 = f32[2,2,2,193,128]{4,2,3,1,0:T(2,128)} collective-permute-done((f32[2,2,2,193,128]{4,2,3,1,0:T(2,128)}, f32[2,2,2,193,128]{4,2,3,1,0:T(2,128)}, u32[]{:S(2)}, u32[]{:S(2)}) %collective-permute-start.16) | collective-permute-done | bytes 790560 | tf_op jit(solution)/shard_map/ppermute | solution.py:309
  263.5 7.3 %collective-permute-done.17 = f32[2,2,193,128]{3,2,1,0:T(8,128)} collective-permute-done((f32[2,2,193,128]{3,2,1,0:T(8,128)}, f32[2,2,193,128]{3,2,1,0:T(8,128)}, u32[]{:S(2)}, u32[]{:S(2)}) %collective-permute-start.17) | collective-permute-done | bytes 395296 | tf_op jit(solution)/shard_map/ppermute | solution.py:309
  274.1 5.7 %collective-permute-done.18 = f32[2,193,128]{2,1,0:T(8,128)S(1)} collective-permute-done((f32[2,193,128]{2,1,0:T(8,128)S(1)}, f32[2,193,128]{2,1,0:T(8,128)S(1)}, u32[]{:S(2)}, u32[]{:S(2)}) %collective-permute-start.18) | collective-permute-done | bytes 197664 | tf_op jit(solution)/shard_map/ppermute | solution.py:309
  279.8 3.7 %collective-permute-start.19 = (f32[193,128]{1,0:T(8,128)S(1)}, f32[193,128]{1,0:T(8,128)S(1)}, u32[]{:S(2)}, u32[]{:S(2)}) collective-permute-start(f32[193,128]{1,0:T(8,128)S(1)} %dynamic-slice_bitcast_fusion.8), channel_id=1, source_target_pairs={{0,4},{1,5},{2,6},{3,7},{4,0},{5,1},{6,2},{7,3},{8,12},{9,13},{10,... | collective-permute-start | bytes 296456 | tf_op jit(solution)/shard_map/ppermute | solution.py:309
  283.6 3.8 %collective-permute-start.14 = (f32[193,128]{1,0:T(8,128)S(1)}, f32[193,128]{1,0:T(8,128)S(1)}, u32[]{:S(2)}, u32[]{:S(2)}) collective-permute-start(f32[193,128]{1,0:T(8,128)S(1)} %dynamic-slice_bitcast_fusion.9), channel_id=1, source_target_pairs={{0,4},{1,5},{2,6},{3,7},{4,0},{5,1},{6,2},{7,3},{8,12},{9,13},{10,... | collective-permute-start | bytes 296456 | tf_op jit(solution)/shard_map/ppermute | solution.py:309
  287.3 3.2 %collective-permute-done.19 = f32[193,128]{1,0:T(8,128)S(1)} collective-permute-done((f32[193,128]{1,0:T(8,128)S(1)}, f32[193,128]{1,0:T(8,128)S(1)}, u32[]{:S(2)}, u32[]{:S(2)}) %collective-permute-start.19) | collective-permute-done | bytes 98848 | tf_op jit(solution)/shard_map/ppermute | solution.py:309
  293.2 3.2 %collective-permute-done.20 = f32[8,128]{1,0:T(8,128)S(1)} collective-permute-done((f32[8,128]{1,0:T(8,128)S(1)}, f32[8,128]{1,0:T(8,128)S(1)}, u32[]{:S(2)}, u32[]{:S(2)}) %collective-permute-start.20) | collective-permute-done | bytes 4128 | tf_op jit(solution)/shard_map/ppermute | solution.py:317
  296.3 3.6 %collective-permute-done.21 = f32[8,128]{1,0:T(8,128)S(1)} collective-permute-done((f32[8,128]{1,0:T(8,128)S(1)}, f32[8,128]{1,0:T(8,128)S(1)}, u32[]{:S(2)}, u32[]{:S(2)}) %collective-permute-start.21) | collective-permute-done | bytes 4128 | tf_op jit(solution)/shard_map/ppermute | solution.py:317
  300.9 2.6 collective-permute-done.22
  (150 shorter events, 70.1 us)
Async XLA Ops:
  1.6 6.8 %collective-permute-start = (bf16[193,128]{1,0:T(8,128)(2,1)S(1)}, bf16[193,128]{1,0:T(8,128)(2,1)S(1)}, u32[]{:S(2)}, u32[]{:S(2)}) collective-permute-start(bf16[193,128]{1,0:T(8,128)(2,1)S(1)} %get-tuple-element.79), channel_id=1, source_target_pairs={{0,4},{1,5},{2,6},{3,7},{4,0},{5,1},{6,2},{7,3},{8,12},{9,13},{10,... | collective-permute-start | bytes 148232 | tf_op jit(solution)/shard_map/ppermute | solution.py:283
  5.7 5.2 %collective-permute-start.5 = (bf16[193,128]{1,0:T(8,128)(2,1)S(1)}, bf16[193,128]{1,0:T(8,128)(2,1)S(1)}, u32[]{:S(2)}, u32[]{:S(2)}) collective-permute-start(bf16[193,128]{1,0:T(8,128)(2,1)S(1)} %get-tuple-element.80), channel_id=1, source_target_pairs={{0,4},{1,5},{2,6},{3,7},{4,0},{5,1},{6,2},{7,3},{8,12},{9,13},{10,... | collective-permute-start | bytes 148232 | tf_op jit(solution)/shard_map/ppermute | solution.py:283
  11.0 5.3 %collective-permute-start.6 = (bf16[2,193,128]{2,1,0:T(8,128)(2,1)S(1)}, bf16[2,193,128]{2,1,0:T(8,128)(2,1)S(1)}, u32[]{:S(2)}, u32[]{:S(2)}) collective-permute-start(bf16[2,193,128]{2,1,0:T(8,128)(2,1)S(1)} %pad_maximum_fusion.9), channel_id=1, source_target_pairs={{0,2},{1,3},{2,0},{3,1},{4,6},{5,7},{6,4},{7,5},{8,10},{9,11},{10,... | collective-permute-start | bytes 296456 | tf_op jit(solution)/shard_map/ppermute | solution.py:283
  12.5 5.4 %collective-permute-start.1 = (bf16[2,193,128]{2,1,0:T(8,128)(2,1)S(1)}, bf16[2,193,128]{2,1,0:T(8,128)(2,1)S(1)}, u32[]{:S(2)}, u32[]{:S(2)}) collective-permute-start(bf16[2,193,128]{2,1,0:T(8,128)(2,1)S(1)} %pad_maximum_fusion.8), channel_id=1, source_target_pairs={{0,2},{1,3},{2,0},{3,1},{4,6},{5,7},{6,4},{7,5},{8,10},{9,11},{10,... | collective-permute-start | bytes 296456 | tf_op jit(solution)/shard_map/ppermute | solution.py:283
  16.3 5.8 %collective-permute-start.7 = (bf16[2,2,193,128]{3,2,1,0:T(8,128)(2,1)S(1)}, bf16[2,2,193,128]{3,2,1,0:T(8,128)(2,1)S(1)}, u32[]{:S(2)}, u32[]{:S(2)}) collective-permute-start(bf16[2,2,193,128]{3,2,1,0:T(8,128)(2,1)S(1)} %pad_maximum_fusion.6), channel_id=1, source_target_pairs={{0,8},{1,9},{2,10},{3,11},{4,12},{5,13},{6,14},{7,15},{8,0},{9,1},... | collective-permute-start | bytes 592904 | tf_op jit(solution)/shard_map/ppermute | solution.py:283
  17.9 8.0 %collective-permute-start.2 = (bf16[2,2,193,128]{3,2,1,0:T(8,128)(2,1)S(1)}, bf16[2,2,193,128]{3,2,1,0:T(8,128)(2,1)S(1)}, u32[]{:S(2)}, u32[]{:S(2)}) collective-permute-start(bf16[2,2,193,128]{3,2,1,0:T(8,128)(2,1)S(1)} %pad_maximum_fusion.5), channel_id=1, source_target_pairs={{0,16},{1,17},{2,18},{3,19},{4,20},{5,21},{6,22},{7,23},{8,24},{9,... | collective-permute-start | bytes 592904 | tf_op jit(solution)/shard_map/ppermute | solution.py:283
  22.2 9.7 %collective-permute-start.8 = (bf16[2,2,2,193,128]{4,3,2,1,0:T(8,128)(2,1)S(1)}, bf16[2,2,2,193,128]{4,3,2,1,0:T(8,128)(2,1)S(1)}, u32[]{:S(2)}, u32[]{:S(2)}) collective-permute-start(bf16[2,2,2,193,128]{4,3,2,1,0:T(8,128)(2,1)S(1)} %pad_maximum_fusion.4), channel_id=1, source_target_pairs={{0,16},{1,17},{2,18},{3,19},{4,20},{5,21},{6,22},{7,23},{8,24},{9,... | collective-permute-start | bytes 1185800 | tf_op jit(solution)/shard_map/ppermute | solution.py:283
  26.0 8.0 %collective-permute-start.3 = (bf16[2,2,2,193,128]{4,3,2,1,0:T(8,128)(2,1)S(1)}, bf16[2,2,2,193,128]{4,3,2,1,0:T(8,128)(2,1)S(1)}, u32[]{:S(2)}, u32[]{:S(2)}) collective-permute-start(bf16[2,2,2,193,128]{4,3,2,1,0:T(8,128)(2,1)S(1)} %pad_maximum_fusion.3), channel_id=1, source_target_pairs={{0,8},{1,9},{2,10},{3,11},{4,12},{5,13},{6,14},{7,15},{8,0},{9,1},... | collective-permute-start | bytes 1185800 | tf_op jit(solution)/shard_map/ppermute | solution.py:283
  33.6 2.5 collective-permute-start.9
  35.7 2.5 collective-permute-start.4
  196.2 28.9 %collective-permute-start.15 = (f32[2,2,2,2,193,128]{5,3,4,2,1,0:T(2,128)}, f32[2,2,2,2,193,128]{5,3,4,2,1,0:T(2,128)}, u32[]{:S(2)}, u32[]{:S(2)}) collective-permute-start(f32[2,2,2,2,193,128]{5,3,4,2,1,0:T(2,128)} %copy.98), channel_id=1, source_target_pairs={{0,1},{1,0},{2,3},{3,2},{4,5},{5,4},{6,7},{7,6},{8,9},{9,8},{10,11... | collective-permute-start | bytes 4743176 | tf_op jit(solution)/shard_map/ppermute | solution.py:309
  223.9 15.1 %collective-permute-start.10 = (f32[2,2,2,2,193,128]{5,3,4,2,1,0:T(2,128)}, f32[2,2,2,2,193,128]{5,3,4,2,1,0:T(2,128)}, u32[]{:S(2)}, u32[]{:S(2)}) collective-permute-start(f32[2,2,2,2,193,128]{5,3,4,2,1,0:T(2,128)} %copy.94), channel_id=1, source_target_pairs={{0,1},{1,0},{2,3},{3,2},{4,5},{5,4},{6,7},{7,6},{8,9},{9,8},{10,11... | collective-permute-start | bytes 4743176 | tf_op jit(solution)/shard_map/ppermute | solution.py:309
  228.8 28.5 %collective-permute-start.16 = (f32[2,2,2,193,128]{4,2,3,1,0:T(2,128)}, f32[2,2,2,193,128]{4,2,3,1,0:T(2,128)}, u32[]{:S(2)}, u32[]{:S(2)}) collective-permute-start(f32[2,2,2,193,128]{4,2,3,1,0:T(2,128)} %copy.100), channel_id=1, source_target_pairs={{0,16},{1,17},{2,18},{3,19},{4,20},{5,21},{6,22},{7,23},{8,24},{9,... | collective-permute-start | bytes 2371592 | tf_op jit(solution)/shard_map/ppermute | solution.py:309
  242.2 19.6 %collective-permute-start.11 = (f32[2,2,2,193,128]{4,2,3,1,0:T(2,128)S(1)}, f32[2,2,2,193,128]{4,2,3,1,0:T(2,128)}, u32[]{:S(2)}, u32[]{:S(2)}) collective-permute-start(f32[2,2,2,193,128]{4,2,3,1,0:T(2,128)S(1)} %copy.96), channel_id=1, source_target_pairs={{0,8},{1,9},{2,10},{3,11},{4,12},{5,13},{6,14},{7,15},{8,0},{9,1},... | collective-permute-start | bytes 2371592 | tf_op jit(solution)/shard_map/ppermute | solution.py:309
  259.5 11.2 %collective-permute-start.17 = (f32[2,2,193,128]{3,2,1,0:T(8,128)}, f32[2,2,193,128]{3,2,1,0:T(8,128)}, u32[]{:S(2)}, u32[]{:S(2)}) collective-permute-start(f32[2,2,193,128]{3,2,1,0:T(8,128)} %dynamic-slice_bitcast_fusion.4), channel_id=1, source_target_pairs={{0,8},{1,9},{2,10},{3,11},{4,12},{5,13},{6,14},{7,15},{8,0},{9,1},... | collective-permute-start | bytes 1185800 | tf_op jit(solution)/shard_map/ppermute | solution.py:309
  263.1 10.5 %collective-permute-start.12 = (f32[2,2,193,128]{3,2,1,0:T(8,128)S(1)}, f32[2,2,193,128]{3,2,1,0:T(8,128)S(1)}, u32[]{:S(2)}, u32[]{:S(2)}) collective-permute-start(f32[2,2,193,128]{3,2,1,0:T(8,128)S(1)} %dynamic-slice_bitcast_fusion.5), channel_id=1, source_target_pairs={{0,16},{1,17},{2,18},{3,19},{4,20},{5,21},{6,22},{7,23},{8,24},{9,... | collective-permute-start | bytes 1185800 | tf_op jit(solution)/shard_map/ppermute | solution.py:309
  271.8 7.9 %collective-permute-start.18 = (f32[2,193,128]{2,1,0:T(8,128)S(1)}, f32[2,193,128]{2,1,0:T(8,128)S(1)}, u32[]{:S(2)}, u32[]{:S(2)}) collective-permute-start(f32[2,193,128]{2,1,0:T(8,128)S(1)} %dynamic-slice_bitcast_fusion.6), channel_id=1, source_target_pairs={{0,2},{1,3},{2,0},{3,1},{4,6},{5,7},{6,4},{7,5},{8,10},{9,11},{10,... | collective-permute-start | bytes 592904 | tf_op jit(solution)/shard_map/ppermute | solution.py:309
  273.7 9.8 %collective-permute-start.13 = (f32[2,193,128]{2,1,0:T(8,128)S(1)}, f32[2,193,128]{2,1,0:T(8,128)S(1)}, u32[]{:S(2)}, u32[]{:S(2)}) collective-permute-start(f32[2,193,128]{2,1,0:T(8,128)S(1)} %dynamic-slice_bitcast_fusion.7), channel_id=1, source_target_pairs={{0,2},{1,3},{2,0},{3,1},{4,6},{5,7},{6,4},{7,5},{8,10},{9,11},{10,... | collective-permute-start | bytes 592904 | tf_op jit(solution)/shard_map/ppermute | solution.py:309
  279.8 10.7 %collective-permute-start.19 = (f32[193,128]{1,0:T(8,128)S(1)}, f32[193,128]{1,0:T(8,128)S(1)}, u32[]{:S(2)}, u32[]{:S(2)}) collective-permute-start(f32[193,128]{1,0:T(8,128)S(1)} %dynamic-slice_bitcast_fusion.8), channel_id=1, source_target_pairs={{0,4},{1,5},{2,6},{3,7},{4,0},{5,1},{6,2},{7,3},{8,12},{9,13},{10,... | collective-permute-start | bytes 296456 | tf_op jit(solution)/shard_map/ppermute | solution.py:309
  283.6 8.1 %collective-permute-start.14 = (f32[193,128]{1,0:T(8,128)S(1)}, f32[193,128]{1,0:T(8,128)S(1)}, u32[]{:S(2)}, u32[]{:S(2)}) collective-permute-start(f32[193,128]{1,0:T(8,128)S(1)} %dynamic-slice_bitcast_fusion.9), channel_id=1, source_target_pairs={{0,4},{1,5},{2,6},{3,7},{4,0},{5,1},{6,2},{7,3},{8,12},{9,13},{10,... | collective-permute-start | bytes 296456 | tf_op jit(solution)/shard_map/ppermute | solution.py:309
  291.8 4.6 %collective-permute-start.20 = (f32[8,128]{1,0:T(8,128)S(1)}, f32[8,128]{1,0:T(8,128)S(1)}, u32[]{:S(2)}, u32[]{:S(2)}) collective-permute-start(f32[8,128]{1,0:T(8,128)S(1)} %broadcast_in_dim.5), channel_id=1, source_target_pairs={{0,4},{1,5},{2,6},{3,7},{4,0},{5,1},{6,2},{7,3},{8,12},{9,13},{10,... | collective-permute-start | bytes 12296 | tf_op jit(solution)/shard_map/ppermute | solution.py:317
  296.3 3.6 %collective-permute-start.21 = (f32[8,128]{1,0:T(8,128)S(1)}, f32[8,128]{1,0:T(8,128)S(1)}, u32[]{:S(2)}, u32[]{:S(2)}) collective-permute-start(f32[8,128]{1,0:T(8,128)S(1)} %broadcast_add_fusion), channel_id=1, source_target_pairs={{0,2},{1,3},{2,0},{3,1},{4,6},{5,7},{6,4},{7,5},{8,10},{9,11},{10,... | collective-permute-start | bytes 12296 | tf_op jit(solution)/shard_map/ppermute | solution.py:317
  299.9 3.6 %collective-permute-start.22 = (f32[8,128]{1,0:T(8,128)S(1)}, f32[8,128]{1,0:T(8,128)S(1)}, u32[]{:S(2)}, u32[]{:S(2)}) collective-permute-start(f32[8,128]{1,0:T(8,128)S(1)} %fusion.7), channel_id=1, source_target_pairs={{0,16},{1,17},{2,18},{3,19},{4,20},{5,21},{6,22},{7,23},{8,24},{9,... | collective-permute-start | bytes 12296 | tf_op jit(solution)/shard_map/ppermute | solution.py:317
  303.6 3.6 %collective-permute-start.23 = (f32[8,128]{1,0:T(8,128)S(1)}, f32[8,128]{1,0:T(8,128)S(1)}, u32[]{:S(2)}, u32[]{:S(2)}) collective-permute-start(f32[8,128]{1,0:T(8,128)S(1)} %add.154), channel_id=1, source_target_pairs={{0,8},{1,9},{2,10},{3,11},{4,12},{5,13},{6,14},{7,15},{8,0},{9,1},... | collective-permute-start | bytes 12296 | tf_op jit(solution)/shard_map/ppermute | solution.py:317
  (15 other events, 174.1 us)

commit v5 on v4

--- a/solution.py
+++ b/solution.py
@@ -24,7 +24,7 @@
     return lax.dot_general(x, y, (((1,), (1,)), ((), ())), preferred_element_type=F32)
 
 
-def block_kernel(length, width, hidden, rows):
+def block_kernel(length, width, hidden, rows, flat_rows):
     nblk = length // rows
     quads = width // LANE
     inv_w = 1.0 / width
@@ -32,8 +32,8 @@
     inv_sqrt_2pi = 1.0 / math.sqrt(2.0 * math.pi)
 
     def kernel(counts_ref, fr_ref, cot_ref, w1_ref, w2_ref, cw_ref, vec_ref, b1_ref,
-               bo_ref, ig_ref, gw1_hbm, gw2_hbm, gcw_ref, gvec_ref, gb1_ref,
-               xq, xhat_s, rstd_s, a_s, da_s, dq, gw1_s, gw2_s, sems):
+               bo_ref, ig_ref, gflat_hbm, gcw_ref, gvec_ref, gb1_ref,
+               xq, xhat_s, rstd_s, a_s, da_s, dq, gw1_s, gw2_s, flat_s, sems):
         clip = pl.program_id(0)
         count = counts_ref[clip]
 
@@ -177,20 +177,35 @@
 
         @pl.when(clip == pl.num_programs(0) - 1)
         def _flush():
-            c1 = pltpu.make_async_copy(gw1_s, gw1_hbm, sems.at[0])
-            c2 = pltpu.make_async_copy(gw2_s, gw2_hbm, sems.at[1])
-            c1.start()
-            c2.start()
-            c1.wait()
-            c2.wait()
+            per1 = hidden // LANE
+            per2 = width // LANE
+            for j in range(per1):
+                flat_s[pl.ds(j, width, stride=per1), :] = gw1_s[:, j * LANE:(j + 1) * LANE]
+            at = width * hidden // LANE
+            for j in range(per2):
+                flat_s[pl.ds(at + j, hidden, stride=per2), :] = gw2_s[:, j * LANE:(j + 1) * LANE]
+            at = 2 * at
+            for q in range(per2):
+                flat_s[pl.ds(at + q, TAPS, stride=per2), :] = gcw_ref[0:TAPS, q * LANE:(q + 1) * LANE]
+            at = at + TAPS * per2
+            for q in range(per2):
+                flat_s[pl.ds(at + q, 5, stride=per2), :] = gvec_ref[0:5, q * LANE:(q + 1) * LANE]
+            at = at + 5 * per2
+            for j in range(per1):
+                flat_s[at + j:at + j + 1, :] = gb1_ref[0:1, j * LANE:(j + 1) * LANE]
+            at = at + per1
+            flat_s[at:, :] = jnp.zeros((flat_rows - at, LANE), F32)
+            out = pltpu.make_async_copy(flat_s, gflat_hbm, sems.at[0])
+            out.start()
+            out.wait()
 
     return kernel
 
 
-def fused_block(frames, counts, cotangent, w1, w2, cw8, vec8, b1_8, rows=256):
+def fused_block(frames, counts, cotangent, w1, w2, cw8, vec8, b1_8, flat_rows, rows=256):
     clips, length, width = frames.shape
     hidden = w1.shape[1]
-    kernel = block_kernel(length, width, hidden, rows)
+    kernel = block_kernel(length, width, hidden, rows, flat_rows)
     clip_spec = pl.BlockSpec((1, length, width), lambda i, c: (i, 0, 0))
     fixed = lambda shape: pl.BlockSpec(shape, lambda i, c: (0, 0))
     grid_spec = pltpu.PrefetchScalarGridSpec(
@@ -199,7 +214,7 @@
         in_specs=[clip_spec, clip_spec, fixed((width, hidden)), fixed((hidden, width)),
                   fixed((8, width)), fixed((8, width)), fixed((8, hidden))],
         out_specs=[clip_spec, clip_spec,
-                   pl.BlockSpec(memory_space=pl.ANY), pl.BlockSpec(memory_space=pl.ANY),
+                   pl.BlockSpec(memory_space=pl.ANY),
                    fixed((8, width)), fixed((8, width)), fixed((8, hidden))],
         scratch_shapes=[
             pltpu.VMEM(((length + 2 * PAD) * (width // LANE), LANE), F32),
@@ -210,6 +225,7 @@
             pltpu.VMEM(((length + 2 * PAD) * (width // LANE), LANE), F32),
             pltpu.VMEM((width, hidden), F32),
             pltpu.VMEM((hidden, width), F32),
+            pltpu.VMEM((flat_rows, LANE), F32),
             pltpu.SemaphoreType.DMA((2,)),
         ],
     )
@@ -222,8 +238,7 @@
         out_shape=[
             jax.ShapeDtypeStruct((clips, length, width), BF16),
             jax.ShapeDtypeStruct((clips, length, width), F32),
-            jax.ShapeDtypeStruct((width, hidden), F32),
-            jax.ShapeDtypeStruct((hidden, width), F32),
+            jax.ShapeDtypeStruct((flat_rows, LANE), F32),
             jax.ShapeDtypeStruct((8, width), F32),
             jax.ShapeDtypeStruct((8, width), F32),
             jax.ShapeDtypeStruct((8, hidden), F32),
@@ -296,6 +311,8 @@
     devices = 1 << nbits
     rows = full.shape[0] // devices
     cuts = [rows * p // len(orders) for p in range(len(orders) + 1)]
+    if rows % 8 == 0:
+        cuts = [c // 8 * 8 for c in cuts]
     shaped = full.reshape([2] * nbits + [rows, LANES])
     held = [shaped[..., cuts[p]:cuts[p + 1], :] for p in range(len(orders))]
     held_bits = [[nbits - 1 - a for a in range(nbits)] for _ in orders]
@@ -334,20 +351,20 @@
     vec8 = jnp.concatenate(
         [jnp.stack([conv_b, ln_g, ln_b, b_two, gamma]).astype(F32), jnp.zeros((3, width), F32)])
     b1_8 = jnp.zeros((8, hidden), F32).at[0].set(b_one.astype(F32))
-    block_out, input_grad, g_w1, g_w2, gcw, gvec, gb1 = fused_block(
-        frames, counts, cotangent, w_one, w_two, cw8, vec8, b1_8)
-    small = jnp.concatenate(
-        [gcw[:TAPS].reshape(-1), gvec[0], gvec[1], gvec[2], gvec[3], gvec[4], gb1[0]]
-    )
-    grad_full = jnp.concatenate(
-        [
-            g_w1.reshape(-1, LANES),
-            g_w2.reshape(-1, LANES),
-            small.reshape(-1, LANES),
-            jnp.zeros(((flat_size - used) // LANES, LANES), F32),
-        ]
-    )
-    grad_shard = tree_reduce_scatter(grad_full, split_orders(order), nbits)
+    shard_rows = local // LANES
+    padded_rows = -(-shard_rows // 8) * 8
+    aligned = padded_rows != shard_rows and (padded_rows - shard_rows) * (devices - 1) <= padded_rows
+    block = padded_rows if aligned else shard_rows
+    block_out, input_grad, grad_full, _, _, _ = fused_block(
+        frames, counts, cotangent, w_one, w_two, cw8, vec8, b1_8, devices * block)
+    grad_block = tree_reduce_scatter(grad_full, split_orders(order), nbits)
+    if aligned:
+        me = lax.axis_index(AXES)
+        prev = lax.ppermute(grad_block, AXES, [(i, (i + 1) % devices) for i in range(devices)])
+        both = jnp.concatenate([prev, grad_block])
+        grad_shard = lax.dynamic_slice_in_dim(both, block - (block - shard_rows) * me, shard_rows, axis=0)
+    else:
+        grad_shard = grad_block
     disc_rows = jnp.sum((disc_grads * disc_grads).reshape(-1, LANES), axis=0, keepdims=True)
     own_rows = jnp.sum(grad_shard * grad_shard, axis=0, keepdims=True)
     squares = jnp.broadcast_to(own_rows + disc_rows, (8, LANES))

time: 309 us -> 285 us (0.922); the launches traced: 312 us -> 283 us
  local copies, waits for them, and re-layouts: 64.6 us -> 29.8 us
  starting transfers between devices: 59.9 us -> 69.6 us
  Pallas kernels: 99.5 us -> 96.2 us
    concatenate x2 -> x0, local copies, waits for them, and re-layouts: 14.4 us -> none  [the longest x1 14.4 us: body(): jnp.concatenate([g_w1.reshape(-1, LANES), g_w2.reshape(-1, LANES), small....]
    reshape x4 -> x0, local copies, waits for them, and re-layouts: 13.1 us -> none  [the longest x1 5.98 us: tree_reduce_scatter(): shaped = full.reshape([2] * nbits + [rows, LANES])]
    ppermute x10, starting transfers between devices: 44.1 us -> 56.8 us  [tree_reduce_scatter(): held[p] = keep + lax.ppermute(send, AXES, swap_perm(devices, bit))]
    ppermute x10, waiting for transfers between devices: 37.5 us -> 25.1 us  [tree_reduce_scatter(): held[p] = keep + lax.ppermute(send, AXES, swap_perm(devices, bit))]
    ppermute x0 -> x1, waiting for transfers between devices: none -> 8.7 us  [body(): lax.ppermute(grad_block, AXES, [(i, (i + 1) % devices) for i in range(dev...]
    pallas_call x1, Pallas kernels: 99.5 us -> 96.2 us  [fused_block(): pl.pallas_call(kernel, grid_spec=grid_spec, out_shape=[jax.ShapeDtypeStru...]
    slice x8 -> x9, local copies, waits for them, and re-layouts: 8.77 us -> 6.86 us  [unpack(): pieces.append(packed[start_at:start_at + entries].reshape(shape))]
    squeeze x14 -> x10, local copies, waits for them, and re-layouts: 7.08 us -> 5.6 us  [tree_reduce_scatter(): lax.dynamic_index_in_dim(held[p], 1 - mine, axis=axis, keepdims=False)]
  transfers between devices with their start and end apart: 25 -> 26, of which waited for: 22 -> 22; matrix products, arithmetic and copies ran while one was open for 5% -> 5% of each run, Pallas kernels for 0% -> 0%
where the time goes in v5:
time: 285 us; the launch traced here: 283 us
  Pallas kernels  96.2 us (34%)
  waiting for transfers between devices  70.6 us (25%)
  starting transfers between devices  69.6 us (24%)
  local copies, waits for them, and re-layouts  29.8 us (10%)
  other arithmetic  14.1 us (5%)
  between operations  2.95 us (1%)
    pallas_call x1, Pallas kernels, fused_block(): pl.pallas_call(kernel, grid_spec=grid_spec, out_shape=[jax.ShapeDtypeStru...  96.2 us
    ppermute x10, starting transfers between devices, tree_reduce_scatter(): held[p] = keep + lax.ppermute(send, AXES, swap_perm(devices, bit))  56.8 us
    ppermute x10, waiting for transfers between devices, tree_reduce_scatter(): held[p] = keep + lax.ppermute(send, AXES, swap_perm(devices, bit))  25.1 us
    ppermute x10, waiting for transfers between devices, tree_all_gather(): other = lax.ppermute(held[p], AXES, swap_perm(devices, bit))  20.9 us
    ppermute x5, waiting for transfers between devices, tree_all_sum(): value = value + lax.ppermute(value, AXES, swap_perm(devices, bit))  16 us
    ppermute x10, starting transfers between devices, tree_all_gather(): other = lax.ppermute(held[p], AXES, swap_perm(devices, bit))  12.1 us
    ppermute x1, waiting for transfers between devices, body(): lax.ppermute(grad_block, AXES, [(i, (i + 1) % devices) for i in range(dev...  8.7 us
    add x10, other arithmetic, tree_reduce_scatter(): held[p] = keep + lax.ppermute(send, AXES, swap_perm(devices, bit))  7.33 us
  transfers between devices with their start and end apart: 26, of which 22 were waited for; matrix products, arithmetic and copies ran while one was open for 5% of the time, Pallas kernels for 0%

profile of v5, /device:TPU:0, one launch (start us, length us, event | category | flops | bytes accessed | tf_op | source)
XLA Modules:
  0.0 283.3 jit_solution(15650393336498075948)
XLA Ops:
  1.6 4.1 %collective-permute-start = (bf16[193,128]{1,0:T(8,128)(2,1)S(1)}, bf16[193,128]{1,0:T(8,128)(2,1)S(1)}, u32[]{:S(2)}, u32[]{:S(2)}) collective-permute-start(bf16[193,128]{1,0:T(8,128)(2,1)S(1)} %get-tuple-element.71), channel_id=1, source_target_pairs={{0,4},{1,5},{2,6},{3,7},{4,0},{5,1},{6,2},{7,3},{8,12},{9,13},{10,... | collective-permute-start | bytes 148232 | tf_op jit(solution)/shard_map/ppermute | solution.py:298
  5.8 2.6 collective-permute-done
  13.1 3.1 %collective-permute-done.1 = bf16[2,193,128]{2,1,0:T(8,128)(2,1)S(1)} collective-permute-done((bf16[2,193,128]{2,1,0:T(8,128)(2,1)S(1)}, bf16[2,193,128]{2,1,0:T(8,128)(2,1)S(1)}, u32[]{:S(2)}, u32[]{:S(2)}) %collective-permute-start.1) | collective-permute-done | bytes 98848 | tf_op jit(solution)/shard_map/ppermute | solution.py:298
  19.5 2.6 collective-permute-done.2
  27.1 4.8 %collective-permute-done.3 = bf16[2,2,2,193,128]{4,3,2,1,0:T(8,128)(2,1)S(1)} collective-permute-done((bf16[2,2,2,193,128]{4,3,2,1,0:T(8,128)(2,1)S(1)}, bf16[2,2,2,193,128]{4,3,2,1,0:T(8,128)(2,1)S(1)}, u32[]{:S(2)}, u32[]{:S(2)}) %collective-permute-start.3) | collective-permute-done | bytes 395296 | tf_op jit(solution)/shard_map/ppermute | solution.py:298
  47.0 3.3 %slice.103 = bf16[3088,512]{1,0:T(8,128)(2,1)} reshape(bf16[32,386,128]{2,1,0:T(8,128)(2,1)S(1)} %copy.48) | data formatting | bytes 6324224 | tf_op jit(solution)/shard_map/slice | solution.py:260
  50.2 2.8 slice.118.w2_ref
  53.7 2.7 reshape.120.w1_ref
  57.7 96.2 %shard_map.134 = (bf16[8,1024,512]{2,1,0:T(8,128)(2,1)}, f32[8,1024,512]{2,1,0:T(8,128)}, f32[12544,128]{1,0:T(8,128)}, f32[8,512]{1,0:T(8,128)}, f32[8,512]{1,0:T(8,128)}, /*index=5*/f32[8,1536]{1,0:T(8,128)}) custom-call(s32[8]{0:T(128)} %counts_ref.1, bf16[8,1024,512]{2,1,0:T(8,128)(2,1)} %fr_ref.1, bf16[8,1024,512]{2,1,0:T(8,128)(2,1)} %cot_ref.1, ...), custom_call_target="tpu_custom_call" | custom-call | flops 77309411328 | bytes 46137344 | tf_op jit(solution)/shard_map/pallas_call | solution.py:235
  158.4 4.4 %collective-permute-start.10 = (f32[2,2,2,2,192,128]{5,4,3,2,1,0:T(8,128)}, f32[2,2,2,2,192,128]{5,4,3,2,1,0:T(8,128)}, u32[]{:S(2)}, u32[]{:S(2)}) collective-permute-start(f32[2,2,2,2,192,128]{5,4,3,2,1,0:T(8,128)} %dynamic-slice_bitcast_fusion.1), channel_id=1, source_target_pairs={{0,1},{1,0},{2,3},{3,2},{4,5},{5,4},{6,7},{7,6},{8,9},{9,8},{10,11... | collective-permute-start | bytes 4718600 | tf_op jit(solution)/shard_map/ppermute | solution.py:326
  169.2 10.2 %collective-permute-start.11 = (f32[2,2,2,192,128]{4,3,2,1,0:T(8,128)}, f32[2,2,2,192,128]{4,3,2,1,0:T(8,128)}, u32[]{:S(2)}, u32[]{:S(2)}) collective-permute-start(f32[2,2,2,192,128]{4,3,2,1,0:T(8,128)} %dynamic-slice_bitcast_fusion.3), channel_id=1, source_target_pairs={{0,8},{1,9},{2,10},{3,11},{4,12},{5,13},{6,14},{7,15},{8,0},{9,1},... | collective-permute-start | bytes 2359304 | tf_op jit(solution)/shard_map/ppermute | solution.py:326
  183.2 4.3 %collective-permute-start.16 = (f32[2,2,2,200,128]{4,3,2,1,0:T(8,128)}, f32[2,2,2,200,128]{4,3,2,1,0:T(8,128)}, u32[]{:S(2)}, u32[]{:S(2)}) collective-permute-start(f32[2,2,2,200,128]{4,3,2,1,0:T(8,128)} %dynamic-slice_bitcast_fusion.2), channel_id=1, source_target_pairs={{0,16},{1,17},{2,18},{3,19},{4,20},{5,21},{6,22},{7,23},{8,24},{9,... | collective-permute-start | bytes 2457608 | tf_op jit(solution)/shard_map/ppermute | solution.py:326
  187.4 10.2 %collective-permute-done.11 = f32[2,2,2,192,128]{4,3,2,1,0:T(8,128)} collective-permute-done((f32[2,2,2,192,128]{4,3,2,1,0:T(8,128)}, f32[2,2,2,192,128]{4,3,2,1,0:T(8,128)}, u32[]{:S(2)}, u32[]{:S(2)}) %collective-permute-start.11) | collective-permute-done | bytes 786464 | tf_op jit(solution)/shard_map/ppermute | solution.py:326
  199.7 5.6 %collective-permute-start.12 = (f32[2,2,192,128]{3,2,1,0:T(8,128)}, f32[2,2,192,128]{3,2,1,0:T(8,128)}, u32[]{:S(2)}, u32[]{:S(2)}) collective-permute-start(f32[2,2,192,128]{3,2,1,0:T(8,128)} %dynamic-slice_bitcast_fusion.5), channel_id=1, source_target_pairs={{0,16},{1,17},{2,18},{3,19},{4,20},{5,21},{6,22},{7,23},{8,24},{9,... | collective-permute-start | bytes 1179656 | tf_op jit(solution)/shard_map/ppermute | solution.py:326
  209.9 4.9 %collective-permute-done.12 = f32[2,2,192,128]{3,2,1,0:T(8,128)} collective-permute-done((f32[2,2,192,128]{3,2,1,0:T(8,128)}, f32[2,2,192,128]{3,2,1,0:T(8,128)}, u32[]{:S(2)}, u32[]{:S(2)}) %collective-permute-start.12) | collective-permute-done | bytes 393248 | tf_op jit(solution)/shard_map/ppermute | solution.py:326
  215.9 18.7 %collective-permute-start.13 = (f32[2,192,128]{2,1,0:T(8,128)S(1)}, f32[2,192,128]{2,1,0:T(8,128)S(1)}, u32[]{:S(2)}, u32[]{:S(2)}) collective-permute-start(f32[2,192,128]{2,1,0:T(8,128)S(1)} %dynamic-slice_bitcast_fusion.7), channel_id=1, source_target_pairs={{0,2},{1,3},{2,0},{3,1},{4,6},{5,7},{6,4},{7,5},{8,10},{9,11},{10,... | collective-permute-start | bytes 589832 | tf_op jit(solution)/shard_map/ppermute | solution.py:326
  234.7 3.1 %collective-permute-start.18 = (f32[2,200,128]{2,1,0:T(8,128)S(1)}, f32[2,200,128]{2,1,0:T(8,128)S(1)}, u32[]{:S(2)}, u32[]{:S(2)}) collective-permute-start(f32[2,200,128]{2,1,0:T(8,128)S(1)} %dynamic-slice_bitcast_fusion.6), channel_id=1, source_target_pairs={{0,2},{1,3},{2,0},{3,1},{4,6},{5,7},{6,4},{7,5},{8,10},{9,11},{10,... | collective-permute-start | bytes 614408 | tf_op jit(solution)/shard_map/ppermute | solution.py:326
  240.3 4.7 %collective-permute-start.14 = (f32[192,128]{1,0:T(8,128)S(1)}, f32[192,128]{1,0:T(8,128)S(1)}, u32[]{:S(2)}, u32[]{:S(2)}) collective-permute-start(f32[192,128]{1,0:T(8,128)S(1)} %dynamic-slice_bitcast_fusion.9), channel_id=1, source_target_pairs={{0,4},{1,5},{2,6},{3,7},{4,0},{5,1},{6,2},{7,3},{8,12},{9,13},{10,... | collective-permute-start | bytes 294920 | tf_op jit(solution)/shard_map/ppermute | solution.py:326
  245.1 3.8 %collective-permute-start.19 = (f32[200,128]{1,0:T(8,128)S(1)}, f32[200,128]{1,0:T(8,128)S(1)}, u32[]{:S(2)}, u32[]{:S(2)}) collective-permute-start(f32[200,128]{1,0:T(8,128)S(1)} %dynamic-slice_bitcast_fusion.8), channel_id=1, source_target_pairs={{0,4},{1,5},{2,6},{3,7},{4,0},{5,1},{6,2},{7,3},{8,12},{9,13},{10,... | collective-permute-start | bytes 307208 | tf_op jit(solution)/shard_map/ppermute | solution.py:326
  253.7 8.7 %collective-permute-done.20 = f32[392,128]{1,0:T(8,128)S(1)} collective-permute-done((f32[392,128]{1,0:T(8,128)S(1)}, f32[392,128]{1,0:T(8,128)S(1)}, u32[]{:S(2)}, u32[]{:S(2)}) %collective-permute-start.20) | collective-permute-done | bytes 200736 | tf_op jit(solution)/shard_map/ppermute | solution.py:363
  262.8 4.5 %collective-permute-done.21 = f32[8,128]{1,0:T(8,128)S(1)} collective-permute-done((f32[8,128]{1,0:T(8,128)S(1)}, f32[8,128]{1,0:T(8,128)S(1)}, u32[]{:S(2)}, u32[]{:S(2)}) %collective-permute-start.21) | collective-permute-done | bytes 4128 | tf_op jit(solution)/shard_map/ppermute | solution.py:334
  267.3 3.6 %collective-permute-done.22 = f32[8,128]{1,0:T(8,128)S(1)} collective-permute-done((f32[8,128]{1,0:T(8,128)S(1)}, f32[8,128]{1,0:T(8,128)S(1)}, u32[]{:S(2)}, u32[]{:S(2)}) %collective-permute-start.22) | collective-permute-done | bytes 4128 | tf_op jit(solution)/shard_map/ppermute | solution.py:334
  271.4 3.1 %collective-permute-done.23 = f32[8,128]{1,0:T(8,128)S(1)} collective-permute-done((f32[8,128]{1,0:T(8,128)S(1)}, f32[8,128]{1,0:T(8,128)S(1)}, u32[]{:S(2)}, u32[]{:S(2)}) %collective-permute-start.23) | collective-permute-done | bytes 4128 | tf_op jit(solution)/shard_map/ppermute | solution.py:334
  274.5 3.6 %collective-permute-done.24 = f32[8,128]{1,0:T(8,128)S(1)} collective-permute-done((f32[8,128]{1,0:T(8,128)S(1)}, f32[8,128]{1,0:T(8,128)S(1)}, u32[]{:S(2)}, u32[]{:S(2)}) %collective-permute-start.24) | collective-permute-done | bytes 4128 | tf_op jit(solution)/shard_map/ppermute | solution.py:334
  (137 shorter events, 65.0 us)
Async XLA Ops:
  1.6 6.8 %collective-permute-start = (bf16[193,128]{1,0:T(8,128)(2,1)S(1)}, bf16[193,128]{1,0:T(8,128)(2,1)S(1)}, u32[]{:S(2)}, u32[]{:S(2)}) collective-permute-start(bf16[193,128]{1,0:T(8,128)(2,1)S(1)} %get-tuple-element.71), channel_id=1, source_target_pairs={{0,4},{1,5},{2,6},{3,7},{4,0},{5,1},{6,2},{7,3},{8,12},{9,13},{10,... | collective-permute-start | bytes 148232 | tf_op jit(solution)/shard_map/ppermute | solution.py:298
  5.7 5.2 %collective-permute-start.5 = (bf16[193,128]{1,0:T(8,128)(2,1)S(1)}, bf16[193,128]{1,0:T(8,128)(2,1)S(1)}, u32[]{:S(2)}, u32[]{:S(2)}) collective-permute-start(bf16[193,128]{1,0:T(8,128)(2,1)S(1)} %get-tuple-element.72), channel_id=1, source_target_pairs={{0,4},{1,5},{2,6},{3,7},{4,0},{5,1},{6,2},{7,3},{8,12},{9,13},{10,... | collective-permute-start | bytes 148232 | tf_op jit(solution)/shard_map/ppermute | solution.py:298
  11.0 5.3 %collective-permute-start.1 = (bf16[2,193,128]{2,1,0:T(8,128)(2,1)S(1)}, bf16[2,193,128]{2,1,0:T(8,128)(2,1)S(1)}, u32[]{:S(2)}, u32[]{:S(2)}) collective-permute-start(bf16[2,193,128]{2,1,0:T(8,128)(2,1)S(1)} %pad_maximum_fusion.8), channel_id=1, source_target_pairs={{0,2},{1,3},{2,0},{3,1},{4,6},{5,7},{6,4},{7,5},{8,10},{9,11},{10,... | collective-permute-start | bytes 296456 | tf_op jit(solution)/shard_map/ppermute | solution.py:298
  12.5 5.4 %collective-permute-start.6 = (bf16[2,193,128]{2,1,0:T(8,128)(2,1)S(1)}, bf16[2,193,128]{2,1,0:T(8,128)(2,1)S(1)}, u32[]{:S(2)}, u32[]{:S(2)}) collective-permute-start(bf16[2,193,128]{2,1,0:T(8,128)(2,1)S(1)} %pad_maximum_fusion.9), channel_id=1, source_target_pairs={{0,2},{1,3},{2,0},{3,1},{4,6},{5,7},{6,4},{7,5},{8,10},{9,11},{10,... | collective-permute-start | bytes 296456 | tf_op jit(solution)/shard_map/ppermute | solution.py:298
  16.3 5.8 %collective-permute-start.2 = (bf16[2,2,193,128]{3,2,1,0:T(8,128)(2,1)S(1)}, bf16[2,2,193,128]{3,2,1,0:T(8,128)(2,1)S(1)}, u32[]{:S(2)}, u32[]{:S(2)}) collective-permute-start(bf16[2,2,193,128]{3,2,1,0:T(8,128)(2,1)S(1)} %pad_maximum_fusion.5), channel_id=1, source_target_pairs={{0,16},{1,17},{2,18},{3,19},{4,20},{5,21},{6,22},{7,23},{8,24},{9,... | collective-permute-start | bytes 592904 | tf_op jit(solution)/shard_map/ppermute | solution.py:298
  18.0 8.0 %collective-permute-start.7 = (bf16[2,2,193,128]{3,2,1,0:T(8,128)(2,1)S(1)}, bf16[2,2,193,128]{3,2,1,0:T(8,128)(2,1)S(1)}, u32[]{:S(2)}, u32[]{:S(2)}) collective-permute-start(bf16[2,2,193,128]{3,2,1,0:T(8,128)(2,1)S(1)} %pad_maximum_fusion.6), channel_id=1, source_target_pairs={{0,8},{1,9},{2,10},{3,11},{4,12},{5,13},{6,14},{7,15},{8,0},{9,1},... | collective-permute-start | bytes 592904 | tf_op jit(solution)/shard_map/ppermute | solution.py:298
  22.2 9.7 %collective-permute-start.3 = (bf16[2,2,2,193,128]{4,3,2,1,0:T(8,128)(2,1)S(1)}, bf16[2,2,2,193,128]{4,3,2,1,0:T(8,128)(2,1)S(1)}, u32[]{:S(2)}, u32[]{:S(2)}) collective-permute-start(bf16[2,2,2,193,128]{4,3,2,1,0:T(8,128)(2,1)S(1)} %pad_maximum_fusion.3), channel_id=1, source_target_pairs={{0,8},{1,9},{2,10},{3,11},{4,12},{5,13},{6,14},{7,15},{8,0},{9,1},... | collective-permute-start | bytes 1185800 | tf_op jit(solution)/shard_map/ppermute | solution.py:298
  26.1 8.0 %collective-permute-start.8 = (bf16[2,2,2,193,128]{4,3,2,1,0:T(8,128)(2,1)S(1)}, bf16[2,2,2,193,128]{4,3,2,1,0:T(8,128)(2,1)S(1)}, u32[]{:S(2)}, u32[]{:S(2)}) collective-permute-start(bf16[2,2,2,193,128]{4,3,2,1,0:T(8,128)(2,1)S(1)} %pad_maximum_fusion.4), channel_id=1, source_target_pairs={{0,16},{1,17},{2,18},{3,19},{4,20},{5,21},{6,22},{7,23},{8,24},{9,... | collective-permute-start | bytes 1185800 | tf_op jit(solution)/shard_map/ppermute | solution.py:298
  35.7 2.5 collective-permute-start.9
  158.4 7.7 %collective-permute-start.10 = (f32[2,2,2,2,192,128]{5,4,3,2,1,0:T(8,128)}, f32[2,2,2,2,192,128]{5,4,3,2,1,0:T(8,128)}, u32[]{:S(2)}, u32[]{:S(2)}) collective-permute-start(f32[2,2,2,2,192,128]{5,4,3,2,1,0:T(8,128)} %dynamic-slice_bitcast_fusion.1), channel_id=1, source_target_pairs={{0,1},{1,0},{2,3},{3,2},{4,5},{5,4},{6,7},{7,6},{8,9},{9,8},{10,11... | collective-permute-start | bytes 4718600 | tf_op jit(solution)/shard_map/ppermute | solution.py:326
  164.3 15.1 %collective-permute-start.15 = (f32[2,2,2,2,200,128]{5,4,3,2,1,0:T(8,128)}, f32[2,2,2,2,200,128]{5,4,3,2,1,0:T(8,128)}, u32[]{:S(2)}, u32[]{:S(2)}) collective-permute-start(f32[2,2,2,2,200,128]{5,4,3,2,1,0:T(8,128)} %dynamic-slice_bitcast_fusion), channel_id=1, source_target_pairs={{0,1},{1,0},{2,3},{3,2},{4,5},{5,4},{6,7},{7,6},{8,9},{9,8},{10,11... | collective-permute-start | bytes 4915208 | tf_op jit(solution)/shard_map/ppermute | solution.py:326
  169.2 28.4 %collective-permute-start.11 = (f32[2,2,2,192,128]{4,3,2,1,0:T(8,128)}, f32[2,2,2,192,128]{4,3,2,1,0:T(8,128)}, u32[]{:S(2)}, u32[]{:S(2)}) collective-permute-start(f32[2,2,2,192,128]{4,3,2,1,0:T(8,128)} %dynamic-slice_bitcast_fusion.3), channel_id=1, source_target_pairs={{0,8},{1,9},{2,10},{3,11},{4,12},{5,13},{6,14},{7,15},{8,0},{9,1},... | collective-permute-start | bytes 2359304 | tf_op jit(solution)/shard_map/ppermute | solution.py:326
  183.2 23.7 %collective-permute-start.16 = (f32[2,2,2,200,128]{4,3,2,1,0:T(8,128)}, f32[2,2,2,200,128]{4,3,2,1,0:T(8,128)}, u32[]{:S(2)}, u32[]{:S(2)}) collective-permute-start(f32[2,2,2,200,128]{4,3,2,1,0:T(8,128)} %dynamic-slice_bitcast_fusion.2), channel_id=1, source_target_pairs={{0,16},{1,17},{2,18},{3,19},{4,20},{5,21},{6,22},{7,23},{8,24},{9,... | collective-permute-start | bytes 2457608 | tf_op jit(solution)/shard_map/ppermute | solution.py:326
  199.7 15.1 %collective-permute-start.12 = (f32[2,2,192,128]{3,2,1,0:T(8,128)}, f32[2,2,192,128]{3,2,1,0:T(8,128)}, u32[]{:S(2)}, u32[]{:S(2)}) collective-permute-start(f32[2,2,192,128]{3,2,1,0:T(8,128)} %dynamic-slice_bitcast_fusion.5), channel_id=1, source_target_pairs={{0,16},{1,17},{2,18},{3,19},{4,20},{5,21},{6,22},{7,23},{8,24},{9,... | collective-permute-start | bytes 1179656 | tf_op jit(solution)/shard_map/ppermute | solution.py:326
  208.2 26.3 %collective-permute-start.17 = (f32[2,2,200,128]{3,2,1,0:T(8,128)S(1)}, f32[2,2,200,128]{3,2,1,0:T(8,128)S(1)}, u32[]{:S(2)}, u32[]{:S(2)}) collective-permute-start(f32[2,2,200,128]{3,2,1,0:T(8,128)S(1)} %dynamic-slice_bitcast_fusion.4), channel_id=1, source_target_pairs={{0,8},{1,9},{2,10},{3,11},{4,12},{5,13},{6,14},{7,15},{8,0},{9,1},... | collective-permute-start | bytes 1228808 | tf_op jit(solution)/shard_map/ppermute | solution.py:326
  215.9 24.4 %collective-permute-start.13 = (f32[2,192,128]{2,1,0:T(8,128)S(1)}, f32[2,192,128]{2,1,0:T(8,128)S(1)}, u32[]{:S(2)}, u32[]{:S(2)}) collective-permute-start(f32[2,192,128]{2,1,0:T(8,128)S(1)} %dynamic-slice_bitcast_fusion.7), channel_id=1, source_target_pairs={{0,2},{1,3},{2,0},{3,1},{4,6},{5,7},{6,4},{7,5},{8,10},{9,11},{10,... | collective-permute-start | bytes 589832 | tf_op jit(solution)/shard_map/ppermute | solution.py:326
  234.7 10.3 %collective-permute-start.18 = (f32[2,200,128]{2,1,0:T(8,128)S(1)}, f32[2,200,128]{2,1,0:T(8,128)S(1)}, u32[]{:S(2)}, u32[]{:S(2)}) collective-permute-start(f32[2,200,128]{2,1,0:T(8,128)S(1)} %dynamic-slice_bitcast_fusion.6), channel_id=1, source_target_pairs={{0,2},{1,3},{2,0},{3,1},{4,6},{5,7},{6,4},{7,5},{8,10},{9,11},{10,... | collective-permute-start | bytes 614408 | tf_op jit(solution)/shard_map/ppermute | solution.py:326
  240.3 10.7 %collective-permute-start.14 = (f32[192,128]{1,0:T(8,128)S(1)}, f32[192,128]{1,0:T(8,128)S(1)}, u32[]{:S(2)}, u32[]{:S(2)}) collective-permute-start(f32[192,128]{1,0:T(8,128)S(1)} %dynamic-slice_bitcast_fusion.9), channel_id=1, source_target_pairs={{0,4},{1,5},{2,6},{3,7},{4,0},{5,1},{6,2},{7,3},{8,12},{9,13},{10,... | collective-permute-start | bytes 294920 | tf_op jit(solution)/shard_map/ppermute | solution.py:326
  245.1 8.5 %collective-permute-start.19 = (f32[200,128]{1,0:T(8,128)S(1)}, f32[200,128]{1,0:T(8,128)S(1)}, u32[]{:S(2)}, u32[]{:S(2)}) collective-permute-start(f32[200,128]{1,0:T(8,128)S(1)} %dynamic-slice_bitcast_fusion.8), channel_id=1, source_target_pairs={{0,4},{1,5},{2,6},{3,7},{4,0},{5,1},{6,2},{7,3},{8,12},{9,13},{10,... | collective-permute-start | bytes 307208 | tf_op jit(solution)/shard_map/ppermute | solution.py:326
  253.6 8.8 %collective-permute-start.20 = (f32[392,128]{1,0:T(8,128)S(1)}, f32[392,128]{1,0:T(8,128)S(1)}, u32[]{:S(2)}, u32[]{:S(2)}) collective-permute-start(f32[392,128]{1,0:T(8,128)S(1)} %pad_maximum_fusion.7), channel_id=1, source_target_pairs={{0,1},{1,2},{2,3},{3,4},{4,5},{5,6},{6,7},{7,8},{8,9},{9,10},{10,1... | collective-permute-start | bytes 602120 | tf_op jit(solution)/shard_map/ppermute | solution.py:363
  262.7 4.6 %collective-permute-start.21 = (f32[8,128]{1,0:T(8,128)S(1)}, f32[8,128]{1,0:T(8,128)S(1)}, u32[]{:S(2)}, u32[]{:S(2)}) collective-permute-start(f32[8,128]{1,0:T(8,128)S(1)} %broadcast_in_dim.2), channel_id=1, source_target_pairs={{0,4},{1,5},{2,6},{3,7},{4,0},{5,1},{6,2},{7,3},{8,12},{9,13},{10,... | collective-permute-start | bytes 12296 | tf_op jit(solution)/shard_map/ppermute | solution.py:334
  267.3 3.6 %collective-permute-start.22 = (f32[8,128]{1,0:T(8,128)S(1)}, f32[8,128]{1,0:T(8,128)S(1)}, u32[]{:S(2)}, u32[]{:S(2)}) collective-permute-start(f32[8,128]{1,0:T(8,128)S(1)} %broadcast_add_fusion), channel_id=1, source_target_pairs={{0,2},{1,3},{2,0},{3,1},{4,6},{5,7},{6,4},{7,5},{8,10},{9,11},{10,... | collective-permute-start | bytes 12296 | tf_op jit(solution)/shard_map/ppermute | solution.py:334
  270.9 3.6 %collective-permute-start.23 = (f32[8,128]{1,0:T(8,128)S(1)}, f32[8,128]{1,0:T(8,128)S(1)}, u32[]{:S(2)}, u32[]{:S(2)}) collective-permute-start(f32[8,128]{1,0:T(8,128)S(1)} %fusion.8), channel_id=1, source_target_pairs={{0,16},{1,17},{2,18},{3,19},{4,20},{5,21},{6,22},{7,23},{8,24},{9,... | collective-permute-start | bytes 12296 | tf_op jit(solution)/shard_map/ppermute | solution.py:334
  274.5 3.6 %collective-permute-start.24 = (f32[8,128]{1,0:T(8,128)S(1)}, f32[8,128]{1,0:T(8,128)S(1)}, u32[]{:S(2)}, u32[]{:S(2)}) collective-permute-start(f32[8,128]{1,0:T(8,128)S(1)} %add.164), channel_id=1, source_target_pairs={{0,8},{1,9},{2,10},{3,11},{4,12},{5,13},{6,14},{7,15},{8,0},{9,1},... | collective-permute-start | bytes 12296 | tf_op jit(solution)/shard_map/ppermute | solution.py:334
  (18 other events, 249.4 us)

commit v6 on v5

--- a/solution.py
+++ b/solution.py
@@ -328,10 +328,22 @@
     return jnp.concatenate(held, axis=0)
 
 
-def tree_all_sum(value, order, nbits):
+def tree_all_sum(value, order, nbits, group=3):
+    me = lax.axis_index(AXES)
     devices = 1 << nbits
-    for bit in reversed(order):
-        value = value + lax.ppermute(value, AXES, swap_perm(devices, bit))
+    for g0 in range(0, len(order), group):
+        bits = order[g0:g0 + group]
+        got = []
+        for m in range(1 << len(bits)):
+            mask = sum(1 << b for i, b in enumerate(bits) if (m >> i) & 1)
+            got.append(value if mask == 0 else lax.ppermute(value, AXES, [(i, i ^ mask) for i in range(devices)]))
+        got = jnp.stack(got)
+        mine = sum(((me >> b) & 1) << i for i, b in enumerate(bits))
+        total = None
+        for p in range(1 << len(bits)):
+            term = lax.dynamic_index_in_dim(got, mine ^ p, axis=0, keepdims=False)
+            total = term if total is None else total + term
+        value = total
     return value
 
 

time: 285 us -> 278 us (0.975); the launches traced: 283 us -> 282 us
  starting transfers between devices: 69.6 us -> 79.5 us
  Pallas kernels: 96.2 us -> 87.7 us
  waiting for transfers between devices: 70.6 us -> 67.3 us
    ppermute x5 -> x10, waiting for transfers between devices: 16 us -> 4.07 us  [tree_all_sum(): lax.ppermute(value, AXES, [(i, i ^ mask) for i in range(devices)])]
    ppermute x5 -> x10, starting transfers between devices: 0.6 us -> 10.7 us  [tree_all_sum(): lax.ppermute(value, AXES, [(i, i ^ mask) for i in range(devices)])]
    ppermute x10, waiting for transfers between devices: 25.1 us -> 33.8 us  [tree_reduce_scatter(): held[p] = keep + lax.ppermute(send, AXES, swap_perm(devices, bit))]
    pallas_call x1, Pallas kernels: 96.2 us -> 87.7 us  [fused_block(): pl.pallas_call(kernel, grid_spec=grid_spec, out_shape=[jax.ShapeDtypeStru...]
  transfers between devices with their start and end apart: 26 -> 31, of which waited for: 22 -> 22; matrix products, arithmetic and copies ran while one was open for 5% -> 5% of each run, Pallas kernels for 0% -> 0%
where the time goes in v6:
time: 278 us; the launch traced here: 282 us
  Pallas kernels  87.7 us (32%)
  starting transfers between devices  79.5 us (29%)
  waiting for transfers between devices  67.3 us (24%)
  local copies, waits for them, and re-layouts  30.1 us (11%)
  other arithmetic  14.2 us (5%)
  between operations  3.07 us (1%)
    pallas_call x1, Pallas kernels, fused_block(): pl.pallas_call(kernel, grid_spec=grid_spec, out_shape=[jax.ShapeDtypeStru...  87.7 us
    ppermute x10, starting transfers between devices, tree_reduce_scatter(): held[p] = keep + lax.ppermute(send, AXES, swap_perm(devices, bit))  56.6 us
    ppermute x10, waiting for transfers between devices, tree_reduce_scatter(): held[p] = keep + lax.ppermute(send, AXES, swap_perm(devices, bit))  33.8 us
    ppermute x10, waiting for transfers between devices, tree_all_gather(): other = lax.ppermute(held[p], AXES, swap_perm(devices, bit))  20.9 us
    ppermute x10, starting transfers between devices, tree_all_gather(): other = lax.ppermute(held[p], AXES, swap_perm(devices, bit))  12.1 us
    ppermute x10, starting transfers between devices, tree_all_sum(): lax.ppermute(value, AXES, [(i, i ^ mask) for i in range(devices)])  10.7 us
    ppermute x1, waiting for transfers between devices, body(): lax.ppermute(grad_block, AXES, [(i, (i + 1) % devices) for i in range(dev...  8.58 us
    add x10, other arithmetic, tree_reduce_scatter(): held[p] = keep + lax.ppermute(send, AXES, swap_perm(devices, bit))  7.33 us
  transfers between devices with their start and end apart: 31, of which 22 were waited for; matrix products, arithmetic and copies ran while one was open for 5% of the time, Pallas kernels for 0%

profile of v6, /device:TPU:0, one launch (start us, length us, event | category | flops | bytes accessed | tf_op | source)
XLA Modules:
  0.0 281.7 jit_solution(2518996965712214518)
XLA Ops:
  1.6 4.1 %collective-permute-start = (bf16[193,128]{1,0:T(8,128)(2,1)S(1)}, bf16[193,128]{1,0:T(8,128)(2,1)S(1)}, u32[]{:S(2)}, u32[]{:S(2)}) collective-permute-start(bf16[193,128]{1,0:T(8,128)(2,1)S(1)} %get-tuple-element.71), channel_id=1, source_target_pairs={{0,4},{1,5},{2,6},{3,7},{4,0},{5,1},{6,2},{7,3},{8,12},{9,13},{10,... | collective-permute-start | bytes 148232 | tf_op jit(solution)/shard_map/ppermute | solution.py:298
  5.8 2.6 collective-permute-done
  8.4 2.5 collective-permute-done.5
  13.1 3.1 %collective-permute-done.1 = bf16[2,193,128]{2,1,0:T(8,128)(2,1)S(1)} collective-permute-done((bf16[2,193,128]{2,1,0:T(8,128)(2,1)S(1)}, bf16[2,193,128]{2,1,0:T(8,128)(2,1)S(1)}, u32[]{:S(2)}, u32[]{:S(2)}) %collective-permute-start.1) | collective-permute-done | bytes 98848 | tf_op jit(solution)/shard_map/ppermute | solution.py:298
  19.5 2.6 collective-permute-done.2
  27.1 4.8 %collective-permute-done.3 = bf16[2,2,2,193,128]{4,3,2,1,0:T(8,128)(2,1)S(1)} collective-permute-done((bf16[2,2,2,193,128]{4,3,2,1,0:T(8,128)(2,1)S(1)}, bf16[2,2,2,193,128]{4,3,2,1,0:T(8,128)(2,1)S(1)}, u32[]{:S(2)}, u32[]{:S(2)}) %collective-permute-start.3) | collective-permute-done | bytes 395296 | tf_op jit(solution)/shard_map/ppermute | solution.py:298
  43.7 2.4 reshape_reshape.3
  47.0 3.3 %slice.104 = bf16[3088,512]{1,0:T(8,128)(2,1)} reshape(bf16[32,386,128]{2,1,0:T(8,128)(2,1)S(1)} %copy.48) | data formatting | bytes 6324224 | tf_op jit(solution)/shard_map/slice | solution.py:260
  50.2 2.8 %slice.119.w2_ref = bf16[1536,512]{1,0:T(8,128)(2,1)} slice(bf16[3088,512]{1,0:T(8,128)(2,1)} %slice.104), slice={[1536:3072], [0:512]} | slice | bytes 3145728 | tf_op jit(solution)/shard_map/slice | solution.py:260
  53.8 2.7 reshape.131.w1_ref
  57.7 87.7 %shard_map.134 = (bf16[8,1024,512]{2,1,0:T(8,128)(2,1)}, f32[8,1024,512]{2,1,0:T(8,128)}, f32[12544,128]{1,0:T(8,128)}, f32[8,512]{1,0:T(8,128)}, f32[8,512]{1,0:T(8,128)}, /*index=5*/f32[8,1536]{1,0:T(8,128)}) custom-call(s32[8]{0:T(128)} %counts_ref.1, bf16[8,1024,512]{2,1,0:T(8,128)(2,1)} %fr_ref.1, bf16[8,1024,512]{2,1,0:T(8,128)(2,1)} %cot_ref.1, ...), custom_call_target="tpu_custom_call" | custom-call | flops 77309411328 | bytes 46137344 | tf_op jit(solution)/shard_map/pallas_call | solution.py:235
  149.9 8.6 %collective-permute-start.10 = (f32[2,2,2,2,192,128]{5,4,3,2,1,0:T(8,128)}, f32[2,2,2,2,192,128]{5,4,3,2,1,0:T(8,128)}, u32[]{:S(2)}, u32[]{:S(2)}) collective-permute-start(f32[2,2,2,2,192,128]{5,4,3,2,1,0:T(8,128)} %dynamic-slice_bitcast_fusion.1), channel_id=1, source_target_pairs={{0,1},{1,0},{2,3},{3,2},{4,5},{5,4},{6,7},{7,6},{8,9},{9,8},{10,11... | collective-permute-start | bytes 4718600 | tf_op jit(solution)/shard_map/ppermute | solution.py:326
  165.0 22.9 %collective-permute-start.11 = (f32[2,2,2,192,128]{4,3,2,1,0:T(8,128)}, f32[2,2,2,192,128]{4,3,2,1,0:T(8,128)}, u32[]{:S(2)}, u32[]{:S(2)}) collective-permute-start(f32[2,2,2,192,128]{4,3,2,1,0:T(8,128)} %dynamic-slice_bitcast_fusion.3), channel_id=1, source_target_pairs={{0,8},{1,9},{2,10},{3,11},{4,12},{5,13},{6,14},{7,15},{8,0},{9,1},... | collective-permute-start | bytes 2359304 | tf_op jit(solution)/shard_map/ppermute | solution.py:326
  191.7 14.4 %collective-permute-done.11 = f32[2,2,2,192,128]{4,3,2,1,0:T(8,128)} collective-permute-done((f32[2,2,2,192,128]{4,3,2,1,0:T(8,128)}, f32[2,2,2,192,128]{4,3,2,1,0:T(8,128)}, u32[]{:S(2)}, u32[]{:S(2)}) %collective-permute-start.11) | collective-permute-done | bytes 786464 | tf_op jit(solution)/shard_map/ppermute | solution.py:326
  208.4 4.8 %collective-permute-done.16 = f32[2,2,2,200,128]{4,3,2,1,0:T(8,128)} collective-permute-done((f32[2,2,2,200,128]{4,3,2,1,0:T(8,128)}, f32[2,2,2,200,128]{4,3,2,1,0:T(8,128)}, u32[]{:S(2)}, u32[]{:S(2)}) %collective-permute-start.16) | collective-permute-done | bytes 819232 | tf_op jit(solution)/shard_map/ppermute | solution.py:326
  214.8 5.8 %collective-permute-done.12 = f32[2,2,192,128]{3,2,1,0:T(8,128)} collective-permute-done((f32[2,2,192,128]{3,2,1,0:T(8,128)}, f32[2,2,192,128]{3,2,1,0:T(8,128)}, u32[]{:S(2)}, u32[]{:S(2)}) %collective-permute-start.12) | collective-permute-done | bytes 393248 | tf_op jit(solution)/shard_map/ppermute | solution.py:326
  221.6 4.2 %collective-permute-start.13 = (f32[2,192,128]{2,1,0:T(8,128)S(1)}, f32[2,192,128]{2,1,0:T(8,128)S(1)}, u32[]{:S(2)}, u32[]{:S(2)}) collective-permute-start(f32[2,192,128]{2,1,0:T(8,128)S(1)} %dynamic-slice_bitcast_fusion.7), channel_id=1, source_target_pairs={{0,2},{1,3},{2,0},{3,1},{4,6},{5,7},{6,4},{7,5},{8,10},{9,11},{10,... | collective-permute-start | bytes 589832 | tf_op jit(solution)/shard_map/ppermute | solution.py:326
  225.9 2.9 %collective-permute-start.18 = (f32[2,200,128]{2,1,0:T(8,128)S(1)}, f32[2,200,128]{2,1,0:T(8,128)S(1)}, u32[]{:S(2)}, u32[]{:S(2)}) collective-permute-start(f32[2,200,128]{2,1,0:T(8,128)S(1)} %dynamic-slice_bitcast_fusion.6), channel_id=1, source_target_pairs={{0,2},{1,3},{2,0},{3,1},{4,6},{5,7},{6,4},{7,5},{8,10},{9,11},{10,... | collective-permute-start | bytes 614408 | tf_op jit(solution)/shard_map/ppermute | solution.py:326
  228.8 2.7 collective-permute-done.13
  231.7 13.3 %collective-permute-start.14 = (f32[192,128]{1,0:T(8,128)S(1)}, f32[192,128]{1,0:T(8,128)S(1)}, u32[]{:S(2)}, u32[]{:S(2)}) collective-permute-start(f32[192,128]{1,0:T(8,128)S(1)} %dynamic-slice_bitcast_fusion.9), channel_id=1, source_target_pairs={{0,4},{1,5},{2,6},{3,7},{4,0},{5,1},{6,2},{7,3},{8,12},{9,13},{10,... | collective-permute-start | bytes 294920 | tf_op jit(solution)/shard_map/ppermute | solution.py:326
  245.1 3.8 %collective-permute-start.19 = (f32[200,128]{1,0:T(8,128)S(1)}, f32[200,128]{1,0:T(8,128)S(1)}, u32[]{:S(2)}, u32[]{:S(2)}) collective-permute-start(f32[200,128]{1,0:T(8,128)S(1)} %dynamic-slice_bitcast_fusion.8), channel_id=1, source_target_pairs={{0,4},{1,5},{2,6},{3,7},{4,0},{5,1},{6,2},{7,3},{8,12},{9,13},{10,... | collective-permute-start | bytes 307208 | tf_op jit(solution)/shard_map/ppermute | solution.py:326
  251.0 2.6 collective-permute-done.19
  253.9 8.6 %collective-permute-done.20 = f32[392,128]{1,0:T(8,128)S(1)} collective-permute-done((f32[392,128]{1,0:T(8,128)S(1)}, f32[392,128]{1,0:T(8,128)S(1)}, u32[]{:S(2)}, u32[]{:S(2)}) %collective-permute-start.20) | collective-permute-done | bytes 200736 | tf_op jit(solution)/shard_map/ppermute | solution.py:375
  272.2 3.5 %collective-permute-start.30 = (f32[8,128]{1,0:T(8,128)S(1)}, f32[8,128]{1,0:T(8,128)S(1)}, u32[]{:S(2)}, u32[]{:S(2)}) collective-permute-start(f32[8,128]{1,0:T(8,128)S(1)} %fusion.18), channel_id=1, source_target_pairs={{0,6},{1,7},{2,4},{3,5},{4,2},{5,3},{6,0},{7,1},{8,14},{9,15},{10,... | collective-permute-start | bytes 12296 | tf_op jit(solution)/shard_map/ppermute | solution.py:339
  (154 shorter events, 61.7 us)
Async XLA Ops:
  1.6 6.8 %collective-permute-start = (bf16[193,128]{1,0:T(8,128)(2,1)S(1)}, bf16[193,128]{1,0:T(8,128)(2,1)S(1)}, u32[]{:S(2)}, u32[]{:S(2)}) collective-permute-start(bf16[193,128]{1,0:T(8,128)(2,1)S(1)} %get-tuple-element.71), channel_id=1, source_target_pairs={{0,4},{1,5},{2,6},{3,7},{4,0},{5,1},{6,2},{7,3},{8,12},{9,13},{10,... | collective-permute-start | bytes 148232 | tf_op jit(solution)/shard_map/ppermute | solution.py:298
  5.7 5.2 %collective-permute-start.5 = (bf16[193,128]{1,0:T(8,128)(2,1)S(1)}, bf16[193,128]{1,0:T(8,128)(2,1)S(1)}, u32[]{:S(2)}, u32[]{:S(2)}) collective-permute-start(bf16[193,128]{1,0:T(8,128)(2,1)S(1)} %get-tuple-element.72), channel_id=1, source_target_pairs={{0,4},{1,5},{2,6},{3,7},{4,0},{5,1},{6,2},{7,3},{8,12},{9,13},{10,... | collective-permute-start | bytes 148232 | tf_op jit(solution)/shard_map/ppermute | solution.py:298
  11.0 5.3 %collective-permute-start.1 = (bf16[2,193,128]{2,1,0:T(8,128)(2,1)S(1)}, bf16[2,193,128]{2,1,0:T(8,128)(2,1)S(1)}, u32[]{:S(2)}, u32[]{:S(2)}) collective-permute-start(bf16[2,193,128]{2,1,0:T(8,128)(2,1)S(1)} %pad_maximum_fusion.8), channel_id=1, source_target_pairs={{0,2},{1,3},{2,0},{3,1},{4,6},{5,7},{6,4},{7,5},{8,10},{9,11},{10,... | collective-permute-start | bytes 296456 | tf_op jit(solution)/shard_map/ppermute | solution.py:298
  12.5 5.4 %collective-permute-start.6 = (bf16[2,193,128]{2,1,0:T(8,128)(2,1)S(1)}, bf16[2,193,128]{2,1,0:T(8,128)(2,1)S(1)}, u32[]{:S(2)}, u32[]{:S(2)}) collective-permute-start(bf16[2,193,128]{2,1,0:T(8,128)(2,1)S(1)} %pad_maximum_fusion.9), channel_id=1, source_target_pairs={{0,2},{1,3},{2,0},{3,1},{4,6},{5,7},{6,4},{7,5},{8,10},{9,11},{10,... | collective-permute-start | bytes 296456 | tf_op jit(solution)/shard_map/ppermute | solution.py:298
  16.3 5.8 %collective-permute-start.2 = (bf16[2,2,193,128]{3,2,1,0:T(8,128)(2,1)S(1)}, bf16[2,2,193,128]{3,2,1,0:T(8,128)(2,1)S(1)}, u32[]{:S(2)}, u32[]{:S(2)}) collective-permute-start(bf16[2,2,193,128]{3,2,1,0:T(8,128)(2,1)S(1)} %pad_maximum_fusion.5), channel_id=1, source_target_pairs={{0,16},{1,17},{2,18},{3,19},{4,20},{5,21},{6,22},{7,23},{8,24},{9,... | collective-permute-start | bytes 592904 | tf_op jit(solution)/shard_map/ppermute | solution.py:298
  18.0 8.0 %collective-permute-start.7 = (bf16[2,2,193,128]{3,2,1,0:T(8,128)(2,1)S(1)}, bf16[2,2,193,128]{3,2,1,0:T(8,128)(2,1)S(1)}, u32[]{:S(2)}, u32[]{:S(2)}) collective-permute-start(bf16[2,2,193,128]{3,2,1,0:T(8,128)(2,1)S(1)} %pad_maximum_fusion.6), channel_id=1, source_target_pairs={{0,8},{1,9},{2,10},{3,11},{4,12},{5,13},{6,14},{7,15},{8,0},{9,1},... | collective-permute-start | bytes 592904 | tf_op jit(solution)/shard_map/ppermute | solution.py:298
  22.2 9.7 %collective-permute-start.3 = (bf16[2,2,2,193,128]{4,3,2,1,0:T(8,128)(2,1)S(1)}, bf16[2,2,2,193,128]{4,3,2,1,0:T(8,128)(2,1)S(1)}, u32[]{:S(2)}, u32[]{:S(2)}) collective-permute-start(bf16[2,2,2,193,128]{4,3,2,1,0:T(8,128)(2,1)S(1)} %pad_maximum_fusion.3), channel_id=1, source_target_pairs={{0,8},{1,9},{2,10},{3,11},{4,12},{5,13},{6,14},{7,15},{8,0},{9,1},... | collective-permute-start | bytes 1185800 | tf_op jit(solution)/shard_map/ppermute | solution.py:298
  26.1 8.0 %collective-permute-start.8 = (bf16[2,2,2,193,128]{4,3,2,1,0:T(8,128)(2,1)S(1)}, bf16[2,2,2,193,128]{4,3,2,1,0:T(8,128)(2,1)S(1)}, u32[]{:S(2)}, u32[]{:S(2)}) collective-permute-start(bf16[2,2,2,193,128]{4,3,2,1,0:T(8,128)(2,1)S(1)} %pad_maximum_fusion.4), channel_id=1, source_target_pairs={{0,16},{1,17},{2,18},{3,19},{4,20},{5,21},{6,22},{7,23},{8,24},{9,... | collective-permute-start | bytes 1185800 | tf_op jit(solution)/shard_map/ppermute | solution.py:298
  149.9 12.0 %collective-permute-start.10 = (f32[2,2,2,2,192,128]{5,4,3,2,1,0:T(8,128)}, f32[2,2,2,2,192,128]{5,4,3,2,1,0:T(8,128)}, u32[]{:S(2)}, u32[]{:S(2)}) collective-permute-start(f32[2,2,2,2,192,128]{5,4,3,2,1,0:T(8,128)} %dynamic-slice_bitcast_fusion.1), channel_id=1, source_target_pairs={{0,1},{1,0},{2,3},{3,2},{4,5},{5,4},{6,7},{7,6},{8,9},{9,8},{10,11... | collective-permute-start | bytes 4718600 | tf_op jit(solution)/shard_map/ppermute | solution.py:326
  160.1 27.8 %collective-permute-start.15 = (f32[2,2,2,2,200,128]{5,4,3,2,1,0:T(8,128)}, f32[2,2,2,2,200,128]{5,4,3,2,1,0:T(8,128)}, u32[]{:S(2)}, u32[]{:S(2)}) collective-permute-start(f32[2,2,2,2,200,128]{5,4,3,2,1,0:T(8,128)} %dynamic-slice_bitcast_fusion), channel_id=1, source_target_pairs={{0,1},{1,0},{2,3},{3,2},{4,5},{5,4},{6,7},{7,6},{8,9},{9,8},{10,11... | collective-permute-start | bytes 4915208 | tf_op jit(solution)/shard_map/ppermute | solution.py:326
  165.0 41.1 %collective-permute-start.11 = (f32[2,2,2,192,128]{4,3,2,1,0:T(8,128)}, f32[2,2,2,192,128]{4,3,2,1,0:T(8,128)}, u32[]{:S(2)}, u32[]{:S(2)}) collective-permute-start(f32[2,2,2,192,128]{4,3,2,1,0:T(8,128)} %dynamic-slice_bitcast_fusion.3), channel_id=1, source_target_pairs={{0,8},{1,9},{2,10},{3,11},{4,12},{5,13},{6,14},{7,15},{8,0},{9,1},... | collective-permute-start | bytes 2359304 | tf_op jit(solution)/shard_map/ppermute | solution.py:326
  191.7 21.4 %collective-permute-start.16 = (f32[2,2,2,200,128]{4,3,2,1,0:T(8,128)}, f32[2,2,2,200,128]{4,3,2,1,0:T(8,128)}, u32[]{:S(2)}, u32[]{:S(2)}) collective-permute-start(f32[2,2,2,200,128]{4,3,2,1,0:T(8,128)} %dynamic-slice_bitcast_fusion.2), channel_id=1, source_target_pairs={{0,16},{1,17},{2,18},{3,19},{4,20},{5,21},{6,22},{7,23},{8,24},{9,... | collective-permute-start | bytes 2457608 | tf_op jit(solution)/shard_map/ppermute | solution.py:326
  208.2 12.3 %collective-permute-start.12 = (f32[2,2,192,128]{3,2,1,0:T(8,128)}, f32[2,2,192,128]{3,2,1,0:T(8,128)}, u32[]{:S(2)}, u32[]{:S(2)}) collective-permute-start(f32[2,2,192,128]{3,2,1,0:T(8,128)} %dynamic-slice_bitcast_fusion.5), channel_id=1, source_target_pairs={{0,16},{1,17},{2,18},{3,19},{4,20},{5,21},{6,22},{7,23},{8,24},{9,... | collective-permute-start | bytes 1179656 | tf_op jit(solution)/shard_map/ppermute | solution.py:326
  214.5 11.3 %collective-permute-start.17 = (f32[2,2,200,128]{3,2,1,0:T(8,128)S(1)}, f32[2,2,200,128]{3,2,1,0:T(8,128)S(1)}, u32[]{:S(2)}, u32[]{:S(2)}) collective-permute-start(f32[2,2,200,128]{3,2,1,0:T(8,128)S(1)} %dynamic-slice_bitcast_fusion.4), channel_id=1, source_target_pairs={{0,8},{1,9},{2,10},{3,11},{4,12},{5,13},{6,14},{7,15},{8,0},{9,1},... | collective-permute-start | bytes 1228808 | tf_op jit(solution)/shard_map/ppermute | solution.py:326
  221.6 10.0 %collective-permute-start.13 = (f32[2,192,128]{2,1,0:T(8,128)S(1)}, f32[2,192,128]{2,1,0:T(8,128)S(1)}, u32[]{:S(2)}, u32[]{:S(2)}) collective-permute-start(f32[2,192,128]{2,1,0:T(8,128)S(1)} %dynamic-slice_bitcast_fusion.7), channel_id=1, source_target_pairs={{0,2},{1,3},{2,0},{3,1},{4,6},{5,7},{6,4},{7,5},{8,10},{9,11},{10,... | collective-permute-start | bytes 589832 | tf_op jit(solution)/shard_map/ppermute | solution.py:326
  225.9 19.1 %collective-permute-start.18 = (f32[2,200,128]{2,1,0:T(8,128)S(1)}, f32[2,200,128]{2,1,0:T(8,128)S(1)}, u32[]{:S(2)}, u32[]{:S(2)}) collective-permute-start(f32[2,200,128]{2,1,0:T(8,128)S(1)} %dynamic-slice_bitcast_fusion.6), channel_id=1, source_target_pairs={{0,2},{1,3},{2,0},{3,1},{4,6},{5,7},{6,4},{7,5},{8,10},{9,11},{10,... | collective-permute-start | bytes 614408 | tf_op jit(solution)/shard_map/ppermute | solution.py:326
  231.7 19.4 %collective-permute-start.14 = (f32[192,128]{1,0:T(8,128)S(1)}, f32[192,128]{1,0:T(8,128)S(1)}, u32[]{:S(2)}, u32[]{:S(2)}) collective-permute-start(f32[192,128]{1,0:T(8,128)S(1)} %dynamic-slice_bitcast_fusion.9), channel_id=1, source_target_pairs={{0,4},{1,5},{2,6},{3,7},{4,0},{5,1},{6,2},{7,3},{8,12},{9,13},{10,... | collective-permute-start | bytes 294920 | tf_op jit(solution)/shard_map/ppermute | solution.py:326
  245.1 8.6 %collective-permute-start.19 = (f32[200,128]{1,0:T(8,128)S(1)}, f32[200,128]{1,0:T(8,128)S(1)}, u32[]{:S(2)}, u32[]{:S(2)}) collective-permute-start(f32[200,128]{1,0:T(8,128)S(1)} %dynamic-slice_bitcast_fusion.8), channel_id=1, source_target_pairs={{0,4},{1,5},{2,6},{3,7},{4,0},{5,1},{6,2},{7,3},{8,12},{9,13},{10,... | collective-permute-start | bytes 307208 | tf_op jit(solution)/shard_map/ppermute | solution.py:326
  253.7 8.8 %collective-permute-start.20 = (f32[392,128]{1,0:T(8,128)S(1)}, f32[392,128]{1,0:T(8,128)S(1)}, u32[]{:S(2)}, u32[]{:S(2)}) collective-permute-start(f32[392,128]{1,0:T(8,128)S(1)} %pad_maximum_fusion.7), channel_id=1, source_target_pairs={{0,1},{1,2},{2,3},{3,4},{4,5},{5,6},{6,7},{7,8},{8,9},{9,10},{10,1... | collective-permute-start | bytes 602120 | tf_op jit(solution)/shard_map/ppermute | solution.py:375
  262.8 4.5 %collective-permute-start.22 = (f32[8,128]{1,0:T(8,128)S(1)}, f32[8,128]{1,0:T(8,128)S(1)}, u32[]{:S(2)}, u32[]{:S(2)}) collective-permute-start(f32[8,128]{1,0:T(8,128)S(1)} %broadcast_in_dim.2), channel_id=1, source_target_pairs={{0,8},{1,9},{2,10},{3,11},{4,12},{5,13},{6,14},{7,15},{8,0},{9,1},... | collective-permute-start | bytes 12296 | tf_op jit(solution)/shard_map/ppermute | solution.py:339
  263.2 5.8 %collective-permute-start.23 = (f32[8,128]{1,0:T(8,128)S(1)}, f32[8,128]{1,0:T(8,128)S(1)}, u32[]{:S(2)}, u32[]{:S(2)}) collective-permute-start(f32[8,128]{1,0:T(8,128)S(1)} %broadcast_in_dim.2), channel_id=1, source_target_pairs={{0,9},{1,8},{2,11},{3,10},{4,13},{5,12},{6,15},{7,14},{8,1},{9,0},... | collective-permute-start | bytes 12296 | tf_op jit(solution)/shard_map/ppermute | solution.py:339
  266.4 4.5 %collective-permute-start.26 = (f32[8,128]{1,0:T(8,128)S(1)}, f32[8,128]{1,0:T(8,128)S(1)}, u32[]{:S(2)}, u32[]{:S(2)}) collective-permute-start(f32[8,128]{1,0:T(8,128)S(1)} %broadcast_in_dim.2), channel_id=1, source_target_pairs={{0,24},{1,25},{2,26},{3,27},{4,28},{5,29},{6,30},{7,31},{8,16},{9,... | collective-permute-start | bytes 12296 | tf_op jit(solution)/shard_map/ppermute | solution.py:339
  271.4 4.6 %collective-permute-start.29 = (f32[8,128]{1,0:T(8,128)S(1)}, f32[8,128]{1,0:T(8,128)S(1)}, u32[]{:S(2)}, u32[]{:S(2)}) collective-permute-start(f32[8,128]{1,0:T(8,128)S(1)} %fusion.18), channel_id=1, source_target_pairs={{0,4},{1,5},{2,6},{3,7},{4,0},{5,1},{6,2},{7,3},{8,12},{9,13},{10,... | collective-permute-start | bytes 12296 | tf_op jit(solution)/shard_map/ppermute | solution.py:339
  272.2 5.4 %collective-permute-start.30 = (f32[8,128]{1,0:T(8,128)S(1)}, f32[8,128]{1,0:T(8,128)S(1)}, u32[]{:S(2)}, u32[]{:S(2)}) collective-permute-start(f32[8,128]{1,0:T(8,128)S(1)} %fusion.18), channel_id=1, source_target_pairs={{0,6},{1,7},{2,4},{3,5},{4,2},{5,3},{6,0},{7,1},{8,14},{9,15},{10,... | collective-permute-start | bytes 12296 | tf_op jit(solution)/shard_map/ppermute | solution.py:339
  (23 other events, 292.1 us)

commit v7 on v5

--- a/solution.py
+++ b/solution.py
@@ -31,11 +31,26 @@
     sqrt_half = math.sqrt(0.5)
     inv_sqrt_2pi = 1.0 / math.sqrt(2.0 * math.pi)
 
-    def kernel(counts_ref, fr_ref, cot_ref, w1_ref, w2_ref, cw_ref, vec_ref, b1_ref,
+    def kernel(counts_ref, fr_ref, cot_ref, wrows_hbm, cw_ref, vec_ref, b1_ref,
                bo_ref, ig_ref, gflat_hbm, gcw_ref, gvec_ref, gb1_ref,
-               xq, xhat_s, rstd_s, a_s, da_s, dq, gw1_s, gw2_s, flat_s, sems):
+               xq, xhat_s, rstd_s, a_s, da_s, dq, gw1_s, gw2_s, flat_s, wb_s, w1_ref, w2_ref, sems):
         clip = pl.program_id(0)
         count = counts_ref[clip]
+
+        @pl.when(clip == 0)
+        def _weights():
+            load = pltpu.make_async_copy(wrows_hbm, wb_s, sems.at[1])
+            load.start()
+            load.wait()
+            wide = flat_s.at[0:wb_s.shape[0], :]
+            wide[...] = wb_s[...].astype(F32)
+            per1 = hidden // LANE
+            per2 = width // LANE
+            for j in range(per1):
+                w1_ref[:, j * LANE:(j + 1) * LANE] = wide[pl.ds(j, width, stride=per1), :].astype(BF16)
+            at = width * hidden // LANE
+            for j in range(per2):
+                w2_ref[:, j * LANE:(j + 1) * LANE] = wide[pl.ds(at + j, hidden, stride=per2), :].astype(BF16)
 
         @pl.when(clip == 0)
         def _init():
@@ -202,16 +217,16 @@
     return kernel
 
 
-def fused_block(frames, counts, cotangent, w1, w2, cw8, vec8, b1_8, flat_rows, rows=256):
+def fused_block(frames, counts, cotangent, wrows, cw8, vec8, b1_8, flat_rows, rows=256):
     clips, length, width = frames.shape
-    hidden = w1.shape[1]
+    hidden = cw8.shape[1] * 3
     kernel = block_kernel(length, width, hidden, rows, flat_rows)
     clip_spec = pl.BlockSpec((1, length, width), lambda i, c: (i, 0, 0))
     fixed = lambda shape: pl.BlockSpec(shape, lambda i, c: (0, 0))
     grid_spec = pltpu.PrefetchScalarGridSpec(
         num_scalar_prefetch=1,
         grid=(clips,),
-        in_specs=[clip_spec, clip_spec, fixed((width, hidden)), fixed((hidden, width)),
+        in_specs=[clip_spec, clip_spec, pl.BlockSpec(memory_space=pl.ANY),
                   fixed((8, width)), fixed((8, width)), fixed((8, hidden))],
         out_specs=[clip_spec, clip_spec,
                    pl.BlockSpec(memory_space=pl.ANY),
@@ -226,6 +241,9 @@
             pltpu.VMEM((width, hidden), F32),
             pltpu.VMEM((hidden, width), F32),
             pltpu.VMEM((flat_rows, LANE), F32),
+            pltpu.VMEM(wrows.shape, BF16),
+            pltpu.VMEM((width, hidden), BF16),
+            pltpu.VMEM((hidden, width), BF16),
             pltpu.SemaphoreType.DMA((2,)),
         ],
     )
@@ -246,7 +264,7 @@
         compiler_params=pltpu.CompilerParams(
             dimension_semantics=("arbitrary",), vmem_limit_bytes=60 * 1024 * 1024),
         cost_estimate=cost,
-    )(counts, frames, cotangent, w1, w2, cw8, vec8, b1_8)
+    )(counts, frames, cotangent, wrows, cw8, vec8, b1_8)
 
 
 def unpack(packed, width, hidden):
@@ -345,7 +363,9 @@
     flat_size = local * devices
     total_frames = jnp.float32(rows * devices)
     rounded = master.astype(BF16).reshape(local // LANES, LANES)
-    packed = tree_all_gather(rounded, [o[::-1] for o in split_orders(order)], nbits).reshape(-1)
+    packed_rows = tree_all_gather(rounded, [o[::-1] for o in split_orders(order)], nbits)
+    wrows = packed_rows[: 2 * width * hidden // LANES]
+    packed = packed_rows.reshape(-1)
     (w_one, w_two, conv_w, conv_b, ln_g, ln_b, b_two, gamma, b_one), used = unpack(packed, width, hidden)
     cw8 = jnp.zeros((8, width), F32).at[:TAPS].set(conv_w.astype(F32))
     vec8 = jnp.concatenate(
@@ -356,7 +376,7 @@
     aligned = padded_rows != shard_rows and (padded_rows - shard_rows) * (devices - 1) <= padded_rows
     block = padded_rows if aligned else shard_rows
     block_out, input_grad, grad_full, _, _, _ = fused_block(
-        frames, counts, cotangent, w_one, w_two, cw8, vec8, b1_8, devices * block)
+        frames, counts, cotangent, wrows, cw8, vec8, b1_8, devices * block)
     grad_block = tree_reduce_scatter(grad_full, split_orders(order), nbits)
     if aligned:
         me = lax.axis_index(AXES)

time: 285 us -> 288 us (1.011); the launches traced: 283 us -> 290 us
  Pallas kernels: 96.2 us -> 115 us
  starting transfers between devices: 69.6 us -> 57.3 us
    pallas_call x1, Pallas kernels: 96.2 us -> 115 us  [fused_block(): pl.pallas_call(kernel, grid_spec=grid_spec, out_shape=[jax.ShapeDtypeStru...]
    ppermute x10, starting transfers between devices: 56.8 us -> 43.6 us  [tree_reduce_scatter(): held[p] = keep + lax.ppermute(send, AXES, swap_perm(devices, bit))]
    slice x0 -> x1, local copies, waits for them, and re-layouts: none -> 3.23 us  [body(): wrows = packed_rows[:2 * width * hidden // LANES]]
    slice x9 -> x6, local copies, waits for them, and re-layouts: 6.86 us -> 4.04 us  [unpack(): pieces.append(packed[start_at:start_at + entries].reshape(shape))]
where the time goes in v7:
time: 288 us; the launch traced here: 290 us
  Pallas kernels  115 us (40%)
  waiting for transfers between devices  70.6 us (25%)
  starting transfers between devices  57.3 us (20%)
  local copies, waits for them, and re-layouts  30.4 us (11%)
  other arithmetic  14.1 us (5%)
  between operations  2.93 us (1%)
    pallas_call x1, Pallas kernels, fused_block(): pl.pallas_call(kernel, grid_spec=grid_spec, out_shape=[jax.ShapeDtypeStru...  115 us
    ppermute x10, starting transfers between devices, tree_reduce_scatter(): held[p] = keep + lax.ppermute(send, AXES, swap_perm(devices, bit))  43.6 us
    ppermute x10, waiting for transfers between devices, tree_reduce_scatter(): held[p] = keep + lax.ppermute(send, AXES, swap_perm(devices, bit))  26 us
    ppermute x10, waiting for transfers between devices, tree_all_gather(): other = lax.ppermute(held[p], AXES, swap_perm(devices, bit))  20.9 us
    ppermute x5, waiting for transfers between devices, tree_all_sum(): value = value + lax.ppermute(value, AXES, swap_perm(devices, bit))  15.1 us
    ppermute x10, starting transfers between devices, tree_all_gather(): other = lax.ppermute(held[p], AXES, swap_perm(devices, bit))  12.1 us
    ppermute x1, waiting for transfers between devices, body(): lax.ppermute(grad_block, AXES, [(i, (i + 1) % devices) for i in range(dev...  8.7 us
    add x10, other arithmetic, tree_reduce_scatter(): held[p] = keep + lax.ppermute(send, AXES, swap_perm(devices, bit))  7.33 us
  transfers between devices with their start and end apart: 26, of which 22 were waited for; matrix products, arithmetic and copies ran while one was open for 5% of the time, Pallas kernels for 0%

profile of v7, /device:TPU:0, one launch (start us, length us, event | category | flops | bytes accessed | tf_op | source)
XLA Modules:
  0.0 290.5 jit_solution(17382557845662636960)
XLA Ops:
  1.6 4.1 %collective-permute-start = (bf16[193,128]{1,0:T(8,128)(2,1)S(1)}, bf16[193,128]{1,0:T(8,128)(2,1)S(1)}, u32[]{:S(2)}, u32[]{:S(2)}) collective-permute-start(bf16[193,128]{1,0:T(8,128)(2,1)S(1)} %get-tuple-element.71), channel_id=1, source_target_pairs={{0,4},{1,5},{2,6},{3,7},{4,0},{5,1},{6,2},{7,3},{8,12},{9,13},{10,... | collective-permute-start | bytes 148232 | tf_op jit(solution)/shard_map/ppermute | solution.py:316
  5.8 2.6 collective-permute-done
  8.4 2.5 collective-permute-done.5
  13.1 3.1 %collective-permute-done.1 = bf16[2,193,128]{2,1,0:T(8,128)(2,1)S(1)} collective-permute-done((bf16[2,193,128]{2,1,0:T(8,128)(2,1)S(1)}, bf16[2,193,128]{2,1,0:T(8,128)(2,1)S(1)}, u32[]{:S(2)}, u32[]{:S(2)}) %collective-permute-start.1) | collective-permute-done | bytes 98848 | tf_op jit(solution)/shard_map/ppermute | solution.py:316
  19.5 2.6 collective-permute-done.2
  27.1 4.8 %collective-permute-done.3 = bf16[2,2,2,193,128]{4,3,2,1,0:T(8,128)(2,1)S(1)} collective-permute-done((bf16[2,2,2,193,128]{4,3,2,1,0:T(8,128)(2,1)S(1)}, bf16[2,2,2,193,128]{4,3,2,1,0:T(8,128)(2,1)S(1)}, u32[]{:S(2)}, u32[]{:S(2)}) %collective-permute-start.3) | collective-permute-done | bytes 395296 | tf_op jit(solution)/shard_map/ppermute | solution.py:316
  49.4 3.3 %slice.99 = bf16[3088,512]{1,0:T(8,128)(2,1)} reshape(bf16[32,386,128]{2,1,0:T(8,128)(2,1)S(1)} %copy.49) | data formatting | bytes 6324224 | tf_op jit(solution)/shard_map/slice | solution.py:278
  53.3 3.2 %slice.112.wrows_hbm = bf16[12288,128]{1,0:T(8,128)(2,1)} slice(bf16[12352,128]{1,0:T(8,128)(2,1)} %reshape.117), slice={[0:12288], [0:128]} | slice | bytes 6291456 | tf_op jit(solution)/shard_map/slice | solution.py:367
  57.8 115.1 %shard_map.134 = (bf16[8,1024,512]{2,1,0:T(8,128)(2,1)}, f32[8,1024,512]{2,1,0:T(8,128)}, f32[12544,128]{1,0:T(8,128)}, f32[8,512]{1,0:T(8,128)}, f32[8,512]{1,0:T(8,128)}, /*index=5*/f32[8,1536]{1,0:T(8,128)}) custom-call(s32[8]{0:T(128)} %counts_ref.1, bf16[8,1024,512]{2,1,0:T(8,128)(2,1)} %fr_ref.1, bf16[8,1024,512]{2,1,0:T(8,128)(2,1)} %cot_ref.1, ...), custom_call_target="tpu_custom_call" | custom-call | flops 77309411328 | bytes 46137344 | tf_op jit(solution)/shard_map/pallas_call | solution.py:253
  184.3 5.5 %collective-permute-start.11 = (f32[2,2,2,192,128]{4,3,2,1,0:T(8,128)}, f32[2,2,2,192,128]{4,3,2,1,0:T(8,128)}, u32[]{:S(2)}, u32[]{:S(2)}) collective-permute-start(f32[2,2,2,192,128]{4,3,2,1,0:T(8,128)} %dynamic-slice_bitcast_fusion.3), channel_id=1, source_target_pairs={{0,8},{1,9},{2,10},{3,11},{4,12},{5,13},{6,14},{7,15},{8,0},{9,1},... | collective-permute-start | bytes 2359304 | tf_op jit(solution)/shard_map/ppermute | solution.py:344
  193.5 4.5 %collective-permute-start.16 = (f32[2,2,2,200,128]{4,3,2,1,0:T(8,128)}, f32[2,2,2,200,128]{4,3,2,1,0:T(8,128)}, u32[]{:S(2)}, u32[]{:S(2)}) collective-permute-start(f32[2,2,2,200,128]{4,3,2,1,0:T(8,128)} %dynamic-slice_bitcast_fusion.2), channel_id=1, source_target_pairs={{0,16},{1,17},{2,18},{3,19},{4,20},{5,21},{6,22},{7,23},{8,24},{9,... | collective-permute-start | bytes 2457608 | tf_op jit(solution)/shard_map/ppermute | solution.py:344
  198.0 10.2 %collective-permute-done.11 = f32[2,2,2,192,128]{4,3,2,1,0:T(8,128)} collective-permute-done((f32[2,2,2,192,128]{4,3,2,1,0:T(8,128)}, f32[2,2,2,192,128]{4,3,2,1,0:T(8,128)}, u32[]{:S(2)}, u32[]{:S(2)}) %collective-permute-start.11) | collective-permute-done | bytes 786464 | tf_op jit(solution)/shard_map/ppermute | solution.py:344
  210.2 5.8 %collective-permute-start.12 = (f32[2,2,192,128]{3,2,1,0:T(8,128)}, f32[2,2,192,128]{3,2,1,0:T(8,128)}, u32[]{:S(2)}, u32[]{:S(2)}) collective-permute-start(f32[2,2,192,128]{3,2,1,0:T(8,128)} %dynamic-slice_bitcast_fusion.5), channel_id=1, source_target_pairs={{0,16},{1,17},{2,18},{3,19},{4,20},{5,21},{6,22},{7,23},{8,24},{9,... | collective-permute-start | bytes 1179656 | tf_op jit(solution)/shard_map/ppermute | solution.py:344
  220.5 5.1 %collective-permute-done.12 = f32[2,2,192,128]{3,2,1,0:T(8,128)} collective-permute-done((f32[2,2,192,128]{3,2,1,0:T(8,128)}, f32[2,2,192,128]{3,2,1,0:T(8,128)}, u32[]{:S(2)}, u32[]{:S(2)}) %collective-permute-start.12) | collective-permute-done | bytes 393248 | tf_op jit(solution)/shard_map/ppermute | solution.py:344
  226.7 6.3 %collective-permute-start.13 = (f32[2,192,128]{2,1,0:T(8,128)S(1)}, f32[2,192,128]{2,1,0:T(8,128)S(1)}, u32[]{:S(2)}, u32[]{:S(2)}) collective-permute-start(f32[2,192,128]{2,1,0:T(8,128)S(1)} %dynamic-slice_bitcast_fusion.7), channel_id=1, source_target_pairs={{0,2},{1,3},{2,0},{3,1},{4,6},{5,7},{6,4},{7,5},{8,10},{9,11},{10,... | collective-permute-start | bytes 589832 | tf_op jit(solution)/shard_map/ppermute | solution.py:344
  233.1 2.6 collective-permute-start.18
  235.7 3.0 %collective-permute-done.13 = f32[2,192,128]{2,1,0:T(8,128)S(1)} collective-permute-done((f32[2,192,128]{2,1,0:T(8,128)S(1)}, f32[2,192,128]{2,1,0:T(8,128)S(1)}, u32[]{:S(2)}, u32[]{:S(2)}) %collective-permute-start.13) | collective-permute-done | bytes 196640 | tf_op jit(solution)/shard_map/ppermute | solution.py:344
  238.8 13.1 %collective-permute-start.14 = (f32[192,128]{1,0:T(8,128)S(1)}, f32[192,128]{1,0:T(8,128)S(1)}, u32[]{:S(2)}, u32[]{:S(2)}) collective-permute-start(f32[192,128]{1,0:T(8,128)S(1)} %dynamic-slice_bitcast_fusion.9), channel_id=1, source_target_pairs={{0,4},{1,5},{2,6},{3,7},{4,0},{5,1},{6,2},{7,3},{8,12},{9,13},{10,... | collective-permute-start | bytes 294920 | tf_op jit(solution)/shard_map/ppermute | solution.py:344
  252.0 4.0 %collective-permute-start.19 = (f32[200,128]{1,0:T(8,128)S(1)}, f32[200,128]{1,0:T(8,128)S(1)}, u32[]{:S(2)}, u32[]{:S(2)}) collective-permute-start(f32[200,128]{1,0:T(8,128)S(1)} %dynamic-slice_bitcast_fusion.8), channel_id=1, source_target_pairs={{0,4},{1,5},{2,6},{3,7},{4,0},{5,1},{6,2},{7,3},{8,12},{9,13},{10,... | collective-permute-start | bytes 307208 | tf_op jit(solution)/shard_map/ppermute | solution.py:344
  256.0 3.1 %collective-permute-done.14 = f32[192,128]{1,0:T(8,128)S(1)} collective-permute-done((f32[192,128]{1,0:T(8,128)S(1)}, f32[192,128]{1,0:T(8,128)S(1)}, u32[]{:S(2)}, u32[]{:S(2)}) %collective-permute-start.14) | collective-permute-done | bytes 98336 | tf_op jit(solution)/shard_map/ppermute | solution.py:344
  260.9 8.7 %collective-permute-done.20 = f32[392,128]{1,0:T(8,128)S(1)} collective-permute-done((f32[392,128]{1,0:T(8,128)S(1)}, f32[392,128]{1,0:T(8,128)S(1)}, u32[]{:S(2)}, u32[]{:S(2)}) %collective-permute-start.20) | collective-permute-done | bytes 200736 | tf_op jit(solution)/shard_map/ppermute | solution.py:383
  269.9 4.5 %collective-permute-done.21 = f32[8,128]{1,0:T(8,128)S(1)} collective-permute-done((f32[8,128]{1,0:T(8,128)S(1)}, f32[8,128]{1,0:T(8,128)S(1)}, u32[]{:S(2)}, u32[]{:S(2)}) %collective-permute-start.21) | collective-permute-done | bytes 4128 | tf_op jit(solution)/shard_map/ppermute | solution.py:352
  274.4 3.6 %collective-permute-done.22 = f32[8,128]{1,0:T(8,128)S(1)} collective-permute-done((f32[8,128]{1,0:T(8,128)S(1)}, f32[8,128]{1,0:T(8,128)S(1)}, u32[]{:S(2)}, u32[]{:S(2)}) %collective-permute-start.22) | collective-permute-done | bytes 4128 | tf_op jit(solution)/shard_map/ppermute | solution.py:352
  281.6 3.6 %collective-permute-done.24 = f32[8,128]{1,0:T(8,128)S(1)} collective-permute-done((f32[8,128]{1,0:T(8,128)S(1)}, f32[8,128]{1,0:T(8,128)S(1)}, u32[]{:S(2)}, u32[]{:S(2)}) %collective-permute-start.24) | collective-permute-done | bytes 4128 | tf_op jit(solution)/shard_map/ppermute | solution.py:352
  (135 shorter events, 62.5 us)
Async XLA Ops:
  1.6 6.8 %collective-permute-start = (bf16[193,128]{1,0:T(8,128)(2,1)S(1)}, bf16[193,128]{1,0:T(8,128)(2,1)S(1)}, u32[]{:S(2)}, u32[]{:S(2)}) collective-permute-start(bf16[193,128]{1,0:T(8,128)(2,1)S(1)} %get-tuple-element.71), channel_id=1, source_target_pairs={{0,4},{1,5},{2,6},{3,7},{4,0},{5,1},{6,2},{7,3},{8,12},{9,13},{10,... | collective-permute-start | bytes 148232 | tf_op jit(solution)/shard_map/ppermute | solution.py:316
  5.7 5.2 %collective-permute-start.5 = (bf16[193,128]{1,0:T(8,128)(2,1)S(1)}, bf16[193,128]{1,0:T(8,128)(2,1)S(1)}, u32[]{:S(2)}, u32[]{:S(2)}) collective-permute-start(bf16[193,128]{1,0:T(8,128)(2,1)S(1)} %get-tuple-element.72), channel_id=1, source_target_pairs={{0,4},{1,5},{2,6},{3,7},{4,0},{5,1},{6,2},{7,3},{8,12},{9,13},{10,... | collective-permute-start | bytes 148232 | tf_op jit(solution)/shard_map/ppermute | solution.py:316
  11.0 5.3 %collective-permute-start.1 = (bf16[2,193,128]{2,1,0:T(8,128)(2,1)S(1)}, bf16[2,193,128]{2,1,0:T(8,128)(2,1)S(1)}, u32[]{:S(2)}, u32[]{:S(2)}) collective-permute-start(bf16[2,193,128]{2,1,0:T(8,128)(2,1)S(1)} %pad_maximum_fusion.8), channel_id=1, source_target_pairs={{0,2},{1,3},{2,0},{3,1},{4,6},{5,7},{6,4},{7,5},{8,10},{9,11},{10,... | collective-permute-start | bytes 296456 | tf_op jit(solution)/shard_map/ppermute | solution.py:316
  12.5 5.4 %collective-permute-start.6 = (bf16[2,193,128]{2,1,0:T(8,128)(2,1)S(1)}, bf16[2,193,128]{2,1,0:T(8,128)(2,1)S(1)}, u32[]{:S(2)}, u32[]{:S(2)}) collective-permute-start(bf16[2,193,128]{2,1,0:T(8,128)(2,1)S(1)} %pad_maximum_fusion.9), channel_id=1, source_target_pairs={{0,2},{1,3},{2,0},{3,1},{4,6},{5,7},{6,4},{7,5},{8,10},{9,11},{10,... | collective-permute-start | bytes 296456 | tf_op jit(solution)/shard_map/ppermute | solution.py:316
  16.3 5.8 %collective-permute-start.2 = (bf16[2,2,193,128]{3,2,1,0:T(8,128)(2,1)S(1)}, bf16[2,2,193,128]{3,2,1,0:T(8,128)(2,1)S(1)}, u32[]{:S(2)}, u32[]{:S(2)}) collective-permute-start(bf16[2,2,193,128]{3,2,1,0:T(8,128)(2,1)S(1)} %pad_maximum_fusion.5), channel_id=1, source_target_pairs={{0,16},{1,17},{2,18},{3,19},{4,20},{5,21},{6,22},{7,23},{8,24},{9,... | collective-permute-start | bytes 592904 | tf_op jit(solution)/shard_map/ppermute | solution.py:316
  18.0 8.0 %collective-permute-start.7 = (bf16[2,2,193,128]{3,2,1,0:T(8,128)(2,1)S(1)}, bf16[2,2,193,128]{3,2,1,0:T(8,128)(2,1)S(1)}, u32[]{:S(2)}, u32[]{:S(2)}) collective-permute-start(bf16[2,2,193,128]{3,2,1,0:T(8,128)(2,1)S(1)} %pad_maximum_fusion.6), channel_id=1, source_target_pairs={{0,8},{1,9},{2,10},{3,11},{4,12},{5,13},{6,14},{7,15},{8,0},{9,1},... | collective-permute-start | bytes 592904 | tf_op jit(solution)/shard_map/ppermute | solution.py:316
  22.2 9.7 %collective-permute-start.3 = (bf16[2,2,2,193,128]{4,3,2,1,0:T(8,128)(2,1)S(1)}, bf16[2,2,2,193,128]{4,3,2,1,0:T(8,128)(2,1)S(1)}, u32[]{:S(2)}, u32[]{:S(2)}) collective-permute-start(bf16[2,2,2,193,128]{4,3,2,1,0:T(8,128)(2,1)S(1)} %pad_maximum_fusion.3), channel_id=1, source_target_pairs={{0,8},{1,9},{2,10},{3,11},{4,12},{5,13},{6,14},{7,15},{8,0},{9,1},... | collective-permute-start | bytes 1185800 | tf_op jit(solution)/shard_map/ppermute | solution.py:316
  26.1 8.0 %collective-permute-start.8 = (bf16[2,2,2,193,128]{4,3,2,1,0:T(8,128)(2,1)S(1)}, bf16[2,2,2,193,128]{4,3,2,1,0:T(8,128)(2,1)S(1)}, u32[]{:S(2)}, u32[]{:S(2)}) collective-permute-start(bf16[2,2,2,193,128]{4,3,2,1,0:T(8,128)(2,1)S(1)} %pad_maximum_fusion.4), channel_id=1, source_target_pairs={{0,16},{1,17},{2,18},{3,19},{4,20},{5,21},{6,22},{7,23},{8,24},{9,... | collective-permute-start | bytes 1185800 | tf_op jit(solution)/shard_map/ppermute | solution.py:316
  33.6 2.5 collective-permute-start.4
  177.5 3.8 %collective-permute-start.10 = (f32[2,2,2,2,192,128]{5,4,3,2,1,0:T(8,128)}, f32[2,2,2,2,192,128]{5,4,3,2,1,0:T(8,128)}, u32[]{:S(2)}, u32[]{:S(2)}) collective-permute-start(f32[2,2,2,2,192,128]{5,4,3,2,1,0:T(8,128)} %dynamic-slice_bitcast_fusion.1), channel_id=1, source_target_pairs={{0,1},{1,0},{2,3},{3,2},{4,5},{5,4},{6,7},{7,6},{8,9},{9,8},{10,11... | collective-permute-start | bytes 4718600 | tf_op jit(solution)/shard_map/ppermute | solution.py:344
  179.5 10.3 %collective-permute-start.15 = (f32[2,2,2,2,200,128]{5,4,3,2,1,0:T(8,128)}, f32[2,2,2,2,200,128]{5,4,3,2,1,0:T(8,128)}, u32[]{:S(2)}, u32[]{:S(2)}) collective-permute-start(f32[2,2,2,2,200,128]{5,4,3,2,1,0:T(8,128)} %dynamic-slice_bitcast_fusion), channel_id=1, source_target_pairs={{0,1},{1,0},{2,3},{3,2},{4,5},{5,4},{6,7},{7,6},{8,9},{9,8},{10,11... | collective-permute-start | bytes 4915208 | tf_op jit(solution)/shard_map/ppermute | solution.py:344
  184.3 23.9 %collective-permute-start.11 = (f32[2,2,2,192,128]{4,3,2,1,0:T(8,128)}, f32[2,2,2,192,128]{4,3,2,1,0:T(8,128)}, u32[]{:S(2)}, u32[]{:S(2)}) collective-permute-start(f32[2,2,2,192,128]{4,3,2,1,0:T(8,128)} %dynamic-slice_bitcast_fusion.3), channel_id=1, source_target_pairs={{0,8},{1,9},{2,10},{3,11},{4,12},{5,13},{6,14},{7,15},{8,0},{9,1},... | collective-permute-start | bytes 2359304 | tf_op jit(solution)/shard_map/ppermute | solution.py:344
  193.5 23.9 %collective-permute-start.16 = (f32[2,2,2,200,128]{4,3,2,1,0:T(8,128)}, f32[2,2,2,200,128]{4,3,2,1,0:T(8,128)}, u32[]{:S(2)}, u32[]{:S(2)}) collective-permute-start(f32[2,2,2,200,128]{4,3,2,1,0:T(8,128)} %dynamic-slice_bitcast_fusion.2), channel_id=1, source_target_pairs={{0,16},{1,17},{2,18},{3,19},{4,20},{5,21},{6,22},{7,23},{8,24},{9,... | collective-permute-start | bytes 2457608 | tf_op jit(solution)/shard_map/ppermute | solution.py:344
  210.2 15.4 %collective-permute-start.12 = (f32[2,2,192,128]{3,2,1,0:T(8,128)}, f32[2,2,192,128]{3,2,1,0:T(8,128)}, u32[]{:S(2)}, u32[]{:S(2)}) collective-permute-start(f32[2,2,192,128]{3,2,1,0:T(8,128)} %dynamic-slice_bitcast_fusion.5), channel_id=1, source_target_pairs={{0,16},{1,17},{2,18},{3,19},{4,20},{5,21},{6,22},{7,23},{8,24},{9,... | collective-permute-start | bytes 1179656 | tf_op jit(solution)/shard_map/ppermute | solution.py:344
  218.8 14.2 %collective-permute-start.17 = (f32[2,2,200,128]{3,2,1,0:T(8,128)S(1)}, f32[2,2,200,128]{3,2,1,0:T(8,128)S(1)}, u32[]{:S(2)}, u32[]{:S(2)}) collective-permute-start(f32[2,2,200,128]{3,2,1,0:T(8,128)S(1)} %dynamic-slice_bitcast_fusion.4), channel_id=1, source_target_pairs={{0,8},{1,9},{2,10},{3,11},{4,12},{5,13},{6,14},{7,15},{8,0},{9,1},... | collective-permute-start | bytes 1228808 | tf_op jit(solution)/shard_map/ppermute | solution.py:344
  226.7 12.1 %collective-permute-start.13 = (f32[2,192,128]{2,1,0:T(8,128)S(1)}, f32[2,192,128]{2,1,0:T(8,128)S(1)}, u32[]{:S(2)}, u32[]{:S(2)}) collective-permute-start(f32[2,192,128]{2,1,0:T(8,128)S(1)} %dynamic-slice_bitcast_fusion.7), channel_id=1, source_target_pairs={{0,2},{1,3},{2,0},{3,1},{4,6},{5,7},{6,4},{7,5},{8,10},{9,11},{10,... | collective-permute-start | bytes 589832 | tf_op jit(solution)/shard_map/ppermute | solution.py:344
  233.1 18.8 %collective-permute-start.18 = (f32[2,200,128]{2,1,0:T(8,128)S(1)}, f32[2,200,128]{2,1,0:T(8,128)S(1)}, u32[]{:S(2)}, u32[]{:S(2)}) collective-permute-start(f32[2,200,128]{2,1,0:T(8,128)S(1)} %dynamic-slice_bitcast_fusion.6), channel_id=1, source_target_pairs={{0,2},{1,3},{2,0},{3,1},{4,6},{5,7},{6,4},{7,5},{8,10},{9,11},{10,... | collective-permute-start | bytes 614408 | tf_op jit(solution)/shard_map/ppermute | solution.py:344
  238.8 20.3 %collective-permute-start.14 = (f32[192,128]{1,0:T(8,128)S(1)}, f32[192,128]{1,0:T(8,128)S(1)}, u32[]{:S(2)}, u32[]{:S(2)}) collective-permute-start(f32[192,128]{1,0:T(8,128)S(1)} %dynamic-slice_bitcast_fusion.9), channel_id=1, source_target_pairs={{0,4},{1,5},{2,6},{3,7},{4,0},{5,1},{6,2},{7,3},{8,12},{9,13},{10,... | collective-permute-start | bytes 294920 | tf_op jit(solution)/shard_map/ppermute | solution.py:344
  252.0 8.7 %collective-permute-start.19 = (f32[200,128]{1,0:T(8,128)S(1)}, f32[200,128]{1,0:T(8,128)S(1)}, u32[]{:S(2)}, u32[]{:S(2)}) collective-permute-start(f32[200,128]{1,0:T(8,128)S(1)} %dynamic-slice_bitcast_fusion.8), channel_id=1, source_target_pairs={{0,4},{1,5},{2,6},{3,7},{4,0},{5,1},{6,2},{7,3},{8,12},{9,13},{10,... | collective-permute-start | bytes 307208 | tf_op jit(solution)/shard_map/ppermute | solution.py:344
  260.7 8.8 %collective-permute-start.20 = (f32[392,128]{1,0:T(8,128)S(1)}, f32[392,128]{1,0:T(8,128)S(1)}, u32[]{:S(2)}, u32[]{:S(2)}) collective-permute-start(f32[392,128]{1,0:T(8,128)S(1)} %pad_maximum_fusion.7), channel_id=1, source_target_pairs={{0,1},{1,2},{2,3},{3,4},{4,5},{5,6},{6,7},{7,8},{8,9},{9,10},{10,1... | collective-permute-start | bytes 602120 | tf_op jit(solution)/shard_map/ppermute | solution.py:383
  269.8 4.6 %collective-permute-start.21 = (f32[8,128]{1,0:T(8,128)S(1)}, f32[8,128]{1,0:T(8,128)S(1)}, u32[]{:S(2)}, u32[]{:S(2)}) collective-permute-start(f32[8,128]{1,0:T(8,128)S(1)} %broadcast_in_dim.2), channel_id=1, source_target_pairs={{0,4},{1,5},{2,6},{3,7},{4,0},{5,1},{6,2},{7,3},{8,12},{9,13},{10,... | collective-permute-start | bytes 12296 | tf_op jit(solution)/shard_map/ppermute | solution.py:352
  274.4 3.6 %collective-permute-start.22 = (f32[8,128]{1,0:T(8,128)S(1)}, f32[8,128]{1,0:T(8,128)S(1)}, u32[]{:S(2)}, u32[]{:S(2)}) collective-permute-start(f32[8,128]{1,0:T(8,128)S(1)} %broadcast_add_fusion), channel_id=1, source_target_pairs={{0,2},{1,3},{2,0},{3,1},{4,6},{5,7},{6,4},{7,5},{8,10},{9,11},{10,... | collective-permute-start | bytes 12296 | tf_op jit(solution)/shard_map/ppermute | solution.py:352
  278.0 3.6 %collective-permute-start.23 = (f32[8,128]{1,0:T(8,128)S(1)}, f32[8,128]{1,0:T(8,128)S(1)}, u32[]{:S(2)}, u32[]{:S(2)}) collective-permute-start(f32[8,128]{1,0:T(8,128)S(1)} %fusion.8), channel_id=1, source_target_pairs={{0,16},{1,17},{2,18},{3,19},{4,20},{5,21},{6,22},{7,23},{8,24},{9,... | collective-permute-start | bytes 12296 | tf_op jit(solution)/shard_map/ppermute | solution.py:352
  281.6 3.6 %collective-permute-start.24 = (f32[8,128]{1,0:T(8,128)S(1)}, f32[8,128]{1,0:T(8,128)S(1)}, u32[]{:S(2)}, u32[]{:S(2)}) collective-permute-start(f32[8,128]{1,0:T(8,128)S(1)} %add.164), channel_id=1, source_target_pairs={{0,8},{1,9},{2,10},{3,11},{4,12},{5,13},{6,14},{7,15},{8,0},{9,1},... | collective-permute-start | bytes 12296 | tf_op jit(solution)/shard_map/ppermute | solution.py:352
  (17 other events, 272.6 us)

commit v8 on v7

--- a/solution.py
+++ b/solution.py
@@ -39,7 +39,7 @@
 
         @pl.when(clip == 0)
         def _weights():
-            load = pltpu.make_async_copy(wrows_hbm, wb_s, sems.at[1])
+            load = pltpu.make_async_copy(wrows_hbm.at[0:wb_s.shape[0], :], wb_s, sems.at[1])
             load.start()
             load.wait()
             wide = flat_s.at[0:wb_s.shape[0], :]
@@ -241,7 +241,7 @@
             pltpu.VMEM((width, hidden), F32),
             pltpu.VMEM((hidden, width), F32),
             pltpu.VMEM((flat_rows, LANE), F32),
-            pltpu.VMEM(wrows.shape, BF16),
+            pltpu.VMEM((2 * width * hidden // LANE, LANE), BF16),
             pltpu.VMEM((width, hidden), BF16),
             pltpu.VMEM((hidden, width), BF16),
             pltpu.SemaphoreType.DMA((2,)),
@@ -364,9 +364,14 @@
     total_frames = jnp.float32(rows * devices)
     rounded = master.astype(BF16).reshape(local // LANES, LANES)
     packed_rows = tree_all_gather(rounded, [o[::-1] for o in split_orders(order)], nbits)
-    wrows = packed_rows[: 2 * width * hidden // LANES]
-    packed = packed_rows.reshape(-1)
-    (w_one, w_two, conv_w, conv_b, ln_g, ln_b, b_two, gamma, b_one), used = unpack(packed, width, hidden)
+    weight_rows = 2 * width * hidden // LANES
+    small_rows = -(-(TAPS * width + 5 * width + hidden) // LANES)
+    small = packed_rows[weight_rows:weight_rows + small_rows].reshape(-1)
+    conv_w = small[: TAPS * width].reshape(TAPS, width)
+    at = TAPS * width
+    conv_b, ln_g, ln_b, b_two, gamma = [small[at + i * width: at + (i + 1) * width] for i in range(5)]
+    at = at + 5 * width
+    b_one = small[at: at + hidden]
     cw8 = jnp.zeros((8, width), F32).at[:TAPS].set(conv_w.astype(F32))
     vec8 = jnp.concatenate(
         [jnp.stack([conv_b, ln_g, ln_b, b_two, gamma]).astype(F32), jnp.zeros((3, width), F32)])
@@ -376,7 +381,7 @@
     aligned = padded_rows != shard_rows and (padded_rows - shard_rows) * (devices - 1) <= padded_rows
     block = padded_rows if aligned else shard_rows
     block_out, input_grad, grad_full, _, _, _ = fused_block(
-        frames, counts, cotangent, wrows, cw8, vec8, b1_8, devices * block)
+        frames, counts, cotangent, packed_rows, cw8, vec8, b1_8, devices * block)
     grad_block = tree_reduce_scatter(grad_full, split_orders(order), nbits)
     if aligned:
         me = lax.axis_index(AXES)

time: 288 us -> 276 us (0.958); the launches traced: 290 us -> 273 us
  Pallas kernels: 115 us -> 98 us
  local copies, waits for them, and re-layouts: 30.4 us -> 23.1 us
  starting transfers between devices: 57.3 us -> 64.2 us
    pallas_call x1, Pallas kernels: 115 us -> 98 us  [fused_block(): pl.pallas_call(kernel, grid_spec=grid_spec, out_shape=[jax.ShapeDtypeStru...]
    slice x7 -> x1, local copies, waits for them, and re-layouts: 7.27 us -> 0.7 us  [body(): conv_w = small[:TAPS * width].reshape(TAPS, width)]
    ppermute x10, starting transfers between devices: 43.6 us -> 49.8 us  [tree_reduce_scatter(): held[p] = keep + lax.ppermute(send, AXES, swap_perm(devices, bit))]
  transfers between devices with their start and end apart: 26 -> 26, of which waited for: 22 -> 22; matrix products, arithmetic and copies ran while one was open for 5% -> 6% of each run, Pallas kernels for 0% -> 0%
where the time goes in v8:
time: 276 us; the launch traced here: 273 us
  Pallas kernels  98 us (36%)
  waiting for transfers between devices  71 us (26%)
  starting transfers between devices  64.2 us (23%)
  local copies, waits for them, and re-layouts  23.1 us (8%)
  other arithmetic  14.1 us (5%)
  between operations  2.93 us (1%)
    pallas_call x1, Pallas kernels, fused_block(): pl.pallas_call(kernel, grid_spec=grid_spec, out_shape=[jax.ShapeDtypeStru...  98 us
    ppermute x10, starting transfers between devices, tree_reduce_scatter(): held[p] = keep + lax.ppermute(send, AXES, swap_perm(devices, bit))  49.8 us
    ppermute x10, waiting for transfers between devices, tree_reduce_scatter(): held[p] = keep + lax.ppermute(send, AXES, swap_perm(devices, bit))  27.2 us
    ppermute x10, waiting for transfers between devices, tree_all_gather(): other = lax.ppermute(held[p], AXES, swap_perm(devices, bit))  20.9 us
    ppermute x5, waiting for transfers between devices, tree_all_sum(): value = value + lax.ppermute(value, AXES, swap_perm(devices, bit))  14.3 us
    ppermute x10, starting transfers between devices, tree_all_gather(): other = lax.ppermute(held[p], AXES, swap_perm(devices, bit))  12.1 us
    ppermute x1, waiting for transfers between devices, body(): lax.ppermute(grad_block, AXES, [(i, (i + 1) % devices) for i in range(dev...  8.66 us
    add x10, other arithmetic, tree_reduce_scatter(): held[p] = keep + lax.ppermute(send, AXES, swap_perm(devices, bit))  7.33 us
  transfers between devices with their start and end apart: 26, of which 22 were waited for; matrix products, arithmetic and copies ran while one was open for 6% of the time, Pallas kernels for 0%

profile of v8, /device:TPU:0, one launch (start us, length us, event | category | flops | bytes accessed | tf_op | source)
XLA Modules:
  0.0 273.5 jit_solution(5994758099934174182)
XLA Ops:
  1.6 4.1 %collective-permute-start = (bf16[193,128]{1,0:T(8,128)(2,1)S(1)}, bf16[193,128]{1,0:T(8,128)(2,1)S(1)}, u32[]{:S(2)}, u32[]{:S(2)}) collective-permute-start(bf16[193,128]{1,0:T(8,128)(2,1)S(1)} %get-tuple-element.71), channel_id=1, source_target_pairs={{0,4},{1,5},{2,6},{3,7},{4,0},{5,1},{6,2},{7,3},{8,12},{9,13},{10,... | collective-permute-start | bytes 148232 | tf_op jit(solution)/shard_map/ppermute | solution.py:316
  5.8 2.6 collective-permute-done
  8.4 2.5 collective-permute-done.5
  13.1 3.1 %collective-permute-done.1 = bf16[2,193,128]{2,1,0:T(8,128)(2,1)S(1)} collective-permute-done((bf16[2,193,128]{2,1,0:T(8,128)(2,1)S(1)}, bf16[2,193,128]{2,1,0:T(8,128)(2,1)S(1)}, u32[]{:S(2)}, u32[]{:S(2)}) %collective-permute-start.1) | collective-permute-done | bytes 98848 | tf_op jit(solution)/shard_map/ppermute | solution.py:316
  19.5 2.6 collective-permute-done.2
  27.1 4.8 %collective-permute-done.3 = bf16[2,2,2,193,128]{4,3,2,1,0:T(8,128)(2,1)S(1)} collective-permute-done((bf16[2,2,2,193,128]{4,3,2,1,0:T(8,128)(2,1)S(1)}, bf16[2,2,2,193,128]{4,3,2,1,0:T(8,128)(2,1)S(1)}, u32[]{:S(2)}, u32[]{:S(2)}) %collective-permute-start.3) | collective-permute-done | bytes 395296 | tf_op jit(solution)/shard_map/ppermute | solution.py:316
  43.7 2.7 reshape.137.wrows_hbm
  50.5 98.0 %shard_map.134 = (bf16[8,1024,512]{2,1,0:T(8,128)(2,1)}, f32[8,1024,512]{2,1,0:T(8,128)}, f32[12544,128]{1,0:T(8,128)}, f32[8,512]{1,0:T(8,128)}, f32[8,512]{1,0:T(8,128)}, /*index=5*/f32[8,1536]{1,0:T(8,128)}) custom-call(s32[8]{0:T(128)} %counts_ref.1, bf16[8,1024,512]{2,1,0:T(8,128)(2,1)} %fr_ref.1, bf16[8,1024,512]{2,1,0:T(8,128)(2,1)} %cot_ref.1, ...), custom_call_target="tpu_custom_call" | custom-call | flops 77309411328 | bytes 46137344 | tf_op jit(solution)/shard_map/pallas_call | solution.py:253
  148.6 2.3 slice.126
  159.9 18.4 %collective-permute-start.11 = (f32[2,2,2,192,128]{4,3,2,1,0:T(8,128)}, f32[2,2,2,192,128]{4,3,2,1,0:T(8,128)}, u32[]{:S(2)}, u32[]{:S(2)}) collective-permute-start(f32[2,2,2,192,128]{4,3,2,1,0:T(8,128)} %dynamic-slice_bitcast_fusion.3), channel_id=1, source_target_pairs={{0,8},{1,9},{2,10},{3,11},{4,12},{5,13},{6,14},{7,15},{8,0},{9,1},... | collective-permute-start | bytes 2359304 | tf_op jit(solution)/shard_map/ppermute | solution.py:344
  182.1 4.2 %collective-permute-start.16 = (f32[2,2,2,200,128]{4,3,2,1,0:T(8,128)}, f32[2,2,2,200,128]{4,3,2,1,0:T(8,128)}, u32[]{:S(2)}, u32[]{:S(2)}) collective-permute-start(f32[2,2,2,200,128]{4,3,2,1,0:T(8,128)} %dynamic-slice_bitcast_fusion.2), channel_id=1, source_target_pairs={{0,16},{1,17},{2,18},{3,19},{4,20},{5,21},{6,22},{7,23},{8,24},{9,... | collective-permute-start | bytes 2457608 | tf_op jit(solution)/shard_map/ppermute | solution.py:344
  186.3 10.2 %collective-permute-done.11 = f32[2,2,2,192,128]{4,3,2,1,0:T(8,128)} collective-permute-done((f32[2,2,2,192,128]{4,3,2,1,0:T(8,128)}, f32[2,2,2,192,128]{4,3,2,1,0:T(8,128)}, u32[]{:S(2)}, u32[]{:S(2)}) %collective-permute-start.11) | collective-permute-done | bytes 786464 | tf_op jit(solution)/shard_map/ppermute | solution.py:344
  198.6 5.6 %collective-permute-start.12 = (f32[2,2,192,128]{3,2,1,0:T(8,128)}, f32[2,2,192,128]{3,2,1,0:T(8,128)}, u32[]{:S(2)}, u32[]{:S(2)}) collective-permute-start(f32[2,2,192,128]{3,2,1,0:T(8,128)} %dynamic-slice_bitcast_fusion.5), channel_id=1, source_target_pairs={{0,16},{1,17},{2,18},{3,19},{4,20},{5,21},{6,22},{7,23},{8,24},{9,... | collective-permute-start | bytes 1179656 | tf_op jit(solution)/shard_map/ppermute | solution.py:344
  208.8 4.9 %collective-permute-done.12 = f32[2,2,192,128]{3,2,1,0:T(8,128)} collective-permute-done((f32[2,2,192,128]{3,2,1,0:T(8,128)}, f32[2,2,192,128]{3,2,1,0:T(8,128)}, u32[]{:S(2)}, u32[]{:S(2)}) %collective-permute-start.12) | collective-permute-done | bytes 393248 | tf_op jit(solution)/shard_map/ppermute | solution.py:344
  214.8 11.6 %collective-permute-start.13 = (f32[2,192,128]{2,1,0:T(8,128)S(1)}, f32[2,192,128]{2,1,0:T(8,128)S(1)}, u32[]{:S(2)}, u32[]{:S(2)}) collective-permute-start(f32[2,192,128]{2,1,0:T(8,128)S(1)} %dynamic-slice_bitcast_fusion.7), channel_id=1, source_target_pairs={{0,2},{1,3},{2,0},{3,1},{4,6},{5,7},{6,4},{7,5},{8,10},{9,11},{10,... | collective-permute-start | bytes 589832 | tf_op jit(solution)/shard_map/ppermute | solution.py:344
  226.5 2.6 collective-permute-start.18
  229.1 3.0 %collective-permute-done.13 = f32[2,192,128]{2,1,0:T(8,128)S(1)} collective-permute-done((f32[2,192,128]{2,1,0:T(8,128)S(1)}, f32[2,192,128]{2,1,0:T(8,128)S(1)}, u32[]{:S(2)}, u32[]{:S(2)}) %collective-permute-start.13) | collective-permute-done | bytes 196640 | tf_op jit(solution)/shard_map/ppermute | solution.py:344
  232.1 2.9 %collective-permute-start.14 = (f32[192,128]{1,0:T(8,128)S(1)}, f32[192,128]{1,0:T(8,128)S(1)}, u32[]{:S(2)}, u32[]{:S(2)}) collective-permute-start(f32[192,128]{1,0:T(8,128)S(1)} %dynamic-slice_bitcast_fusion.9), channel_id=1, source_target_pairs={{0,4},{1,5},{2,6},{3,7},{4,0},{5,1},{6,2},{7,3},{8,12},{9,13},{10,... | collective-permute-start | bytes 294920 | tf_op jit(solution)/shard_map/ppermute | solution.py:344
  236.2 2.8 %collective-permute-start.19 = (f32[200,128]{1,0:T(8,128)S(1)}, f32[200,128]{1,0:T(8,128)S(1)}, u32[]{:S(2)}, u32[]{:S(2)}) collective-permute-start(f32[200,128]{1,0:T(8,128)S(1)} %dynamic-slice_bitcast_fusion.8), channel_id=1, source_target_pairs={{0,4},{1,5},{2,6},{3,7},{4,0},{5,1},{6,2},{7,3},{8,12},{9,13},{10,... | collective-permute-start | bytes 307208 | tf_op jit(solution)/shard_map/ppermute | solution.py:344
  239.0 4.8 %collective-permute-done.19 = f32[200,128]{1,0:T(8,128)S(1)} collective-permute-done((f32[200,128]{1,0:T(8,128)S(1)}, f32[200,128]{1,0:T(8,128)S(1)}, u32[]{:S(2)}, u32[]{:S(2)}) %collective-permute-start.19) | collective-permute-done | bytes 102432 | tf_op jit(solution)/shard_map/ppermute | solution.py:344
  243.9 8.7 %collective-permute-done.20 = f32[392,128]{1,0:T(8,128)S(1)} collective-permute-done((f32[392,128]{1,0:T(8,128)S(1)}, f32[392,128]{1,0:T(8,128)S(1)}, u32[]{:S(2)}, u32[]{:S(2)}) %collective-permute-start.20) | collective-permute-done | bytes 200736 | tf_op jit(solution)/shard_map/ppermute | solution.py:388
  252.9 4.5 %collective-permute-done.21 = f32[8,128]{1,0:T(8,128)S(1)} collective-permute-done((f32[8,128]{1,0:T(8,128)S(1)}, f32[8,128]{1,0:T(8,128)S(1)}, u32[]{:S(2)}, u32[]{:S(2)}) %collective-permute-start.21) | collective-permute-done | bytes 4128 | tf_op jit(solution)/shard_map/ppermute | solution.py:352
  257.4 3.6 %collective-permute-done.22 = f32[8,128]{1,0:T(8,128)S(1)} collective-permute-done((f32[8,128]{1,0:T(8,128)S(1)}, f32[8,128]{1,0:T(8,128)S(1)}, u32[]{:S(2)}, u32[]{:S(2)}) %collective-permute-start.22) | collective-permute-done | bytes 4128 | tf_op jit(solution)/shard_map/ppermute | solution.py:352
  265.4 2.9 %collective-permute-done.24 = f32[8,128]{1,0:T(8,128)S(1)} collective-permute-done((f32[8,128]{1,0:T(8,128)S(1)}, f32[8,128]{1,0:T(8,128)S(1)}, u32[]{:S(2)}, u32[]{:S(2)}) %collective-permute-start.24) | collective-permute-done | bytes 4128 | tf_op jit(solution)/shard_map/ppermute | solution.py:352
  (131 shorter events, 57.3 us)
Async XLA Ops:
  1.6 6.8 %collective-permute-start = (bf16[193,128]{1,0:T(8,128)(2,1)S(1)}, bf16[193,128]{1,0:T(8,128)(2,1)S(1)}, u32[]{:S(2)}, u32[]{:S(2)}) collective-permute-start(bf16[193,128]{1,0:T(8,128)(2,1)S(1)} %get-tuple-element.71), channel_id=1, source_target_pairs={{0,4},{1,5},{2,6},{3,7},{4,0},{5,1},{6,2},{7,3},{8,12},{9,13},{10,... | collective-permute-start | bytes 148232 | tf_op jit(solution)/shard_map/ppermute | solution.py:316
  5.7 5.2 %collective-permute-start.5 = (bf16[193,128]{1,0:T(8,128)(2,1)S(1)}, bf16[193,128]{1,0:T(8,128)(2,1)S(1)}, u32[]{:S(2)}, u32[]{:S(2)}) collective-permute-start(bf16[193,128]{1,0:T(8,128)(2,1)S(1)} %get-tuple-element.72), channel_id=1, source_target_pairs={{0,4},{1,5},{2,6},{3,7},{4,0},{5,1},{6,2},{7,3},{8,12},{9,13},{10,... | collective-permute-start | bytes 148232 | tf_op jit(solution)/shard_map/ppermute | solution.py:316
  11.0 5.3 %collective-permute-start.1 = (bf16[2,193,128]{2,1,0:T(8,128)(2,1)S(1)}, bf16[2,193,128]{2,1,0:T(8,128)(2,1)S(1)}, u32[]{:S(2)}, u32[]{:S(2)}) collective-permute-start(bf16[2,193,128]{2,1,0:T(8,128)(2,1)S(1)} %pad_maximum_fusion.8), channel_id=1, source_target_pairs={{0,2},{1,3},{2,0},{3,1},{4,6},{5,7},{6,4},{7,5},{8,10},{9,11},{10,... | collective-permute-start | bytes 296456 | tf_op jit(solution)/shard_map/ppermute | solution.py:316
  12.5 5.4 %collective-permute-start.6 = (bf16[2,193,128]{2,1,0:T(8,128)(2,1)S(1)}, bf16[2,193,128]{2,1,0:T(8,128)(2,1)S(1)}, u32[]{:S(2)}, u32[]{:S(2)}) collective-permute-start(bf16[2,193,128]{2,1,0:T(8,128)(2,1)S(1)} %pad_maximum_fusion.9), channel_id=1, source_target_pairs={{0,2},{1,3},{2,0},{3,1},{4,6},{5,7},{6,4},{7,5},{8,10},{9,11},{10,... | collective-permute-start | bytes 296456 | tf_op jit(solution)/shard_map/ppermute | solution.py:316
  16.3 5.8 %collective-permute-start.2 = (bf16[2,2,193,128]{3,2,1,0:T(8,128)(2,1)S(1)}, bf16[2,2,193,128]{3,2,1,0:T(8,128)(2,1)S(1)}, u32[]{:S(2)}, u32[]{:S(2)}) collective-permute-start(bf16[2,2,193,128]{3,2,1,0:T(8,128)(2,1)S(1)} %pad_maximum_fusion.5), channel_id=1, source_target_pairs={{0,16},{1,17},{2,18},{3,19},{4,20},{5,21},{6,22},{7,23},{8,24},{9,... | collective-permute-start | bytes 592904 | tf_op jit(solution)/shard_map/ppermute | solution.py:316
  18.0 8.0 %collective-permute-start.7 = (bf16[2,2,193,128]{3,2,1,0:T(8,128)(2,1)S(1)}, bf16[2,2,193,128]{3,2,1,0:T(8,128)(2,1)S(1)}, u32[]{:S(2)}, u32[]{:S(2)}) collective-permute-start(bf16[2,2,193,128]{3,2,1,0:T(8,128)(2,1)S(1)} %pad_maximum_fusion.6), channel_id=1, source_target_pairs={{0,8},{1,9},{2,10},{3,11},{4,12},{5,13},{6,14},{7,15},{8,0},{9,1},... | collective-permute-start | bytes 592904 | tf_op jit(solution)/shard_map/ppermute | solution.py:316
  22.2 9.7 %collective-permute-start.3 = (bf16[2,2,2,193,128]{4,3,2,1,0:T(8,128)(2,1)S(1)}, bf16[2,2,2,193,128]{4,3,2,1,0:T(8,128)(2,1)S(1)}, u32[]{:S(2)}, u32[]{:S(2)}) collective-permute-start(bf16[2,2,2,193,128]{4,3,2,1,0:T(8,128)(2,1)S(1)} %pad_maximum_fusion.3), channel_id=1, source_target_pairs={{0,8},{1,9},{2,10},{3,11},{4,12},{5,13},{6,14},{7,15},{8,0},{9,1},... | collective-permute-start | bytes 1185800 | tf_op jit(solution)/shard_map/ppermute | solution.py:316
  26.1 8.0 %collective-permute-start.8 = (bf16[2,2,2,193,128]{4,3,2,1,0:T(8,128)(2,1)S(1)}, bf16[2,2,2,193,128]{4,3,2,1,0:T(8,128)(2,1)S(1)}, u32[]{:S(2)}, u32[]{:S(2)}) collective-permute-start(bf16[2,2,2,193,128]{4,3,2,1,0:T(8,128)(2,1)S(1)} %pad_maximum_fusion.4), channel_id=1, source_target_pairs={{0,16},{1,17},{2,18},{3,19},{4,20},{5,21},{6,22},{7,23},{8,24},{9,... | collective-permute-start | bytes 1185800 | tf_op jit(solution)/shard_map/ppermute | solution.py:316
  33.6 2.5 collective-permute-start.4
  153.1 3.8 %collective-permute-start.10 = (f32[2,2,2,2,192,128]{5,4,3,2,1,0:T(8,128)}, f32[2,2,2,2,192,128]{5,4,3,2,1,0:T(8,128)}, u32[]{:S(2)}, u32[]{:S(2)}) collective-permute-start(f32[2,2,2,2,192,128]{5,4,3,2,1,0:T(8,128)} %dynamic-slice_bitcast_fusion.1), channel_id=1, source_target_pairs={{0,1},{1,0},{2,3},{3,2},{4,5},{5,4},{6,7},{7,6},{8,9},{9,8},{10,11... | collective-permute-start | bytes 4718600 | tf_op jit(solution)/shard_map/ppermute | solution.py:344
  155.1 23.2 %collective-permute-start.15 = (f32[2,2,2,2,200,128]{5,4,3,2,1,0:T(8,128)}, f32[2,2,2,2,200,128]{5,4,3,2,1,0:T(8,128)}, u32[]{:S(2)}, u32[]{:S(2)}) collective-permute-start(f32[2,2,2,2,200,128]{5,4,3,2,1,0:T(8,128)} %dynamic-slice_bitcast_fusion), channel_id=1, source_target_pairs={{0,1},{1,0},{2,3},{3,2},{4,5},{5,4},{6,7},{7,6},{8,9},{9,8},{10,11... | collective-permute-start | bytes 4915208 | tf_op jit(solution)/shard_map/ppermute | solution.py:344
  159.9 36.6 %collective-permute-start.11 = (f32[2,2,2,192,128]{4,3,2,1,0:T(8,128)}, f32[2,2,2,192,128]{4,3,2,1,0:T(8,128)}, u32[]{:S(2)}, u32[]{:S(2)}) collective-permute-start(f32[2,2,2,192,128]{4,3,2,1,0:T(8,128)} %dynamic-slice_bitcast_fusion.3), channel_id=1, source_target_pairs={{0,8},{1,9},{2,10},{3,11},{4,12},{5,13},{6,14},{7,15},{8,0},{9,1},... | collective-permute-start | bytes 2359304 | tf_op jit(solution)/shard_map/ppermute | solution.py:344
  182.1 23.6 %collective-permute-start.16 = (f32[2,2,2,200,128]{4,3,2,1,0:T(8,128)}, f32[2,2,2,200,128]{4,3,2,1,0:T(8,128)}, u32[]{:S(2)}, u32[]{:S(2)}) collective-permute-start(f32[2,2,2,200,128]{4,3,2,1,0:T(8,128)} %dynamic-slice_bitcast_fusion.2), channel_id=1, source_target_pairs={{0,16},{1,17},{2,18},{3,19},{4,20},{5,21},{6,22},{7,23},{8,24},{9,... | collective-permute-start | bytes 2457608 | tf_op jit(solution)/shard_map/ppermute | solution.py:344
  198.6 15.1 %collective-permute-start.12 = (f32[2,2,192,128]{3,2,1,0:T(8,128)}, f32[2,2,192,128]{3,2,1,0:T(8,128)}, u32[]{:S(2)}, u32[]{:S(2)}) collective-permute-start(f32[2,2,192,128]{3,2,1,0:T(8,128)} %dynamic-slice_bitcast_fusion.5), channel_id=1, source_target_pairs={{0,16},{1,17},{2,18},{3,19},{4,20},{5,21},{6,22},{7,23},{8,24},{9,... | collective-permute-start | bytes 1179656 | tf_op jit(solution)/shard_map/ppermute | solution.py:344
  207.1 19.2 %collective-permute-start.17 = (f32[2,2,200,128]{3,2,1,0:T(8,128)S(1)}, f32[2,2,200,128]{3,2,1,0:T(8,128)S(1)}, u32[]{:S(2)}, u32[]{:S(2)}) collective-permute-start(f32[2,2,200,128]{3,2,1,0:T(8,128)S(1)} %dynamic-slice_bitcast_fusion.4), channel_id=1, source_target_pairs={{0,8},{1,9},{2,10},{3,11},{4,12},{5,13},{6,14},{7,15},{8,0},{9,1},... | collective-permute-start | bytes 1228808 | tf_op jit(solution)/shard_map/ppermute | solution.py:344
  214.8 17.3 %collective-permute-start.13 = (f32[2,192,128]{2,1,0:T(8,128)S(1)}, f32[2,192,128]{2,1,0:T(8,128)S(1)}, u32[]{:S(2)}, u32[]{:S(2)}) collective-permute-start(f32[2,192,128]{2,1,0:T(8,128)S(1)} %dynamic-slice_bitcast_fusion.7), channel_id=1, source_target_pairs={{0,2},{1,3},{2,0},{3,1},{4,6},{5,7},{6,4},{7,5},{8,10},{9,11},{10,... | collective-permute-start | bytes 589832 | tf_op jit(solution)/shard_map/ppermute | solution.py:344
  226.5 9.7 %collective-permute-start.18 = (f32[2,200,128]{2,1,0:T(8,128)S(1)}, f32[2,200,128]{2,1,0:T(8,128)S(1)}, u32[]{:S(2)}, u32[]{:S(2)}) collective-permute-start(f32[2,200,128]{2,1,0:T(8,128)S(1)} %dynamic-slice_bitcast_fusion.6), channel_id=1, source_target_pairs={{0,2},{1,3},{2,0},{3,1},{4,6},{5,7},{6,4},{7,5},{8,10},{9,11},{10,... | collective-permute-start | bytes 614408 | tf_op jit(solution)/shard_map/ppermute | solution.py:344
  232.1 6.8 %collective-permute-start.14 = (f32[192,128]{1,0:T(8,128)S(1)}, f32[192,128]{1,0:T(8,128)S(1)}, u32[]{:S(2)}, u32[]{:S(2)}) collective-permute-start(f32[192,128]{1,0:T(8,128)S(1)} %dynamic-slice_bitcast_fusion.9), channel_id=1, source_target_pairs={{0,4},{1,5},{2,6},{3,7},{4,0},{5,1},{6,2},{7,3},{8,12},{9,13},{10,... | collective-permute-start | bytes 294920 | tf_op jit(solution)/shard_map/ppermute | solution.py:344
  236.2 7.6 %collective-permute-start.19 = (f32[200,128]{1,0:T(8,128)S(1)}, f32[200,128]{1,0:T(8,128)S(1)}, u32[]{:S(2)}, u32[]{:S(2)}) collective-permute-start(f32[200,128]{1,0:T(8,128)S(1)} %dynamic-slice_bitcast_fusion.8), channel_id=1, source_target_pairs={{0,4},{1,5},{2,6},{3,7},{4,0},{5,1},{6,2},{7,3},{8,12},{9,13},{10,... | collective-permute-start | bytes 307208 | tf_op jit(solution)/shard_map/ppermute | solution.py:344
  243.8 8.8 %collective-permute-start.20 = (f32[392,128]{1,0:T(8,128)S(1)}, f32[392,128]{1,0:T(8,128)S(1)}, u32[]{:S(2)}, u32[]{:S(2)}) collective-permute-start(f32[392,128]{1,0:T(8,128)S(1)} %pad_maximum_fusion.7), channel_id=1, source_target_pairs={{0,1},{1,2},{2,3},{3,4},{4,5},{5,6},{6,7},{7,8},{8,9},{9,10},{10,1... | collective-permute-start | bytes 602120 | tf_op jit(solution)/shard_map/ppermute | solution.py:388
  252.8 4.6 %collective-permute-start.21 = (f32[8,128]{1,0:T(8,128)S(1)}, f32[8,128]{1,0:T(8,128)S(1)}, u32[]{:S(2)}, u32[]{:S(2)}) collective-permute-start(f32[8,128]{1,0:T(8,128)S(1)} %broadcast_in_dim.2), channel_id=1, source_target_pairs={{0,4},{1,5},{2,6},{3,7},{4,0},{5,1},{6,2},{7,3},{8,12},{9,13},{10,... | collective-permute-start | bytes 12296 | tf_op jit(solution)/shard_map/ppermute | solution.py:352
  257.4 3.6 %collective-permute-start.22 = (f32[8,128]{1,0:T(8,128)S(1)}, f32[8,128]{1,0:T(8,128)S(1)}, u32[]{:S(2)}, u32[]{:S(2)}) collective-permute-start(f32[8,128]{1,0:T(8,128)S(1)} %broadcast_add_fusion), channel_id=1, source_target_pairs={{0,2},{1,3},{2,0},{3,1},{4,6},{5,7},{6,4},{7,5},{8,10},{9,11},{10,... | collective-permute-start | bytes 12296 | tf_op jit(solution)/shard_map/ppermute | solution.py:352
  261.0 3.6 %collective-permute-start.23 = (f32[8,128]{1,0:T(8,128)S(1)}, f32[8,128]{1,0:T(8,128)S(1)}, u32[]{:S(2)}, u32[]{:S(2)}) collective-permute-start(f32[8,128]{1,0:T(8,128)S(1)} %fusion.7), channel_id=1, source_target_pairs={{0,16},{1,17},{2,18},{3,19},{4,20},{5,21},{6,22},{7,23},{8,24},{9,... | collective-permute-start | bytes 12296 | tf_op jit(solution)/shard_map/ppermute | solution.py:352
  264.6 3.6 %collective-permute-start.24 = (f32[8,128]{1,0:T(8,128)S(1)}, f32[8,128]{1,0:T(8,128)S(1)}, u32[]{:S(2)}, u32[]{:S(2)}) collective-permute-start(f32[8,128]{1,0:T(8,128)S(1)} %add.164), channel_id=1, source_target_pairs={{0,8},{1,9},{2,10},{3,11},{4,12},{5,13},{6,14},{7,15},{8,0},{9,1},... | collective-permute-start | bytes 12296 | tf_op jit(solution)/shard_map/ppermute | solution.py:352
  (15 other events, 236.2 us)
